TPU v7x, 512 devices: a whole 4x8x8 slice. The times are simulated.
512 devices in a mesh: section: 8 (over y), dp: 64 (over x, z, core).
Axes of the slice: x: 4, y: 8, z: 8, core: 2. Of those that a mesh axis runs over, the one named last changes fastest.
Arguments:
- queries: bfloat16 [65536, 3584], P(('section', 'dp')), may hold values from -1 to 1
- passages: bfloat16 [128, 64, 3584], P('dp'), may hold values from -1 to 1
- candidates: int32 [512, 3], P('section'), may hold values from 0 to 63, as said below
- counts: int32 [512], P('section'), may hold values from 1 to 3, 1024 in all
- teacher: float32 [65536, 384], P(('section', 'dp')), may hold values from -20 to 450
- section_weights: bfloat16 [8, 3584, 3584], P('section', 'dp'), may hold values from -0.09375 to 0.09375
- section_inputs: bfloat16 [8, 64, 3584], P('section', None, 'dp'), may hold values from -1.5 to 1.5
- pre_acts: bfloat16 [8, 64, 3584], P('section', None, 'dp'), may hold values from -8 to 8
Outputs:
- query_grads: bfloat16 [65536, 3584], P(('section', 'dp'))
- passage_grads: bfloat16 [128, 64, 3584], P('dp')
- grad_inputs: float32 [8, 64, 3584], P('section', None, 'dp')
- weight_grads: bfloat16 [8, 3584, 3584], P('section', 'dp')
Inputs may be any that keep to these rules, and one draw needn't show every extreme that they name: `candidates`: each row names 3 different passage blocks. A query block uses the first counts[b] entries of its row of candidates.
All inputs are finite; a program needn't handle non-finite values.
Results may differ from a plain program's by a relative error of at most 0.0085.
Values may be sent and summed in bfloat16 or wider, within the bound.
No kernel may reach another device: no remote copies, remote signals or barrier semaphores. Data moves between devices by JAX's collectives and lax.ppermute only.
A program may use at most 64 MiB of HBM per device.

v0:
```python
import jax
import jax.numpy as jnp
from jax import lax
from jax.sharding import PartitionSpec as P

INVERSE_TEMP = 20.0


def passed_along(value, axis, steps):
    count = lax.axis_size(axis)
    initial, last = (max(0, -steps), min(count, count - steps))
    return lax.ppermute(value, axis, [(source, source + steps) for source in range(initial, last)])


def gathered_pieces(value, axis):
    count = lax.axis_size(axis)
    copies = jnp.broadcast_to(value[None], (count,) + value.shape)
    return lax.all_to_all(copies, axis, 0, 0, tiled=True)


def gathered_columns(value, axis):
    count = lax.axis_size(axis)
    copies = jnp.broadcast_to(value[None], (count,) + value.shape)
    pieces = lax.all_to_all(copies, axis, 0, 0, tiled=True)
    return jnp.transpose(pieces, (1, 0, 2)).reshape(value.shape[0], count * value.shape[1])


def soft_weights(logits, valid):
    masked = jnp.where(valid, logits, -1e30)
    highest = jnp.max(masked, axis=-1, keepdims=True)
    expons = jnp.where(valid, jnp.exp(masked - highest), 0.0)
    return expons / jnp.sum(expons, axis=-1, keepdims=True)


def body(queries, passages, candidates, counts, teacher, section_weights, section_inputs, pre_acts):
    dp_count = lax.axis_size("dp")
    dp_index = lax.axis_index("dp")
    stripe, block_total, width = passages.shape
    row_block_count = stripe * dp_count
    blocks_here = candidates.shape[0] // dp_count
    slot_count = candidates.shape[1]
    requests = blocks_here * slot_count
    all_slots = candidates.reshape(-1)
    chooser = (all_slots[:, None] == jnp.arange(block_total, dtype=jnp.int32)[None, :]).astype(
        passages.dtype
    )
    outgoing = jnp.einsum(
        "rpj,sp->rsj", passages, chooser, preferred_element_type=jnp.float32
    ).astype(passages.dtype)
    pulled_rows = lax.all_to_all(outgoing, "dp", split_axis=1, concat_axis=0, tiled=True)
    pulled_rows = pulled_rows.reshape(row_block_count, blocks_here, slot_count, width)
    own_counts = lax.dynamic_slice_in_dim(counts, dp_index * blocks_here, blocks_here)
    slot_valid = jnp.arange(slot_count, dtype=jnp.int32)[None, :] < own_counts[:, None]
    column_valid = jnp.repeat(slot_valid, row_block_count, axis=1)[:, None, :]
    query_row_items = queries.reshape(blocks_here, row_block_count, width)
    logits = (
        jnp.einsum(
            "ixp,wifp->ixfw", query_row_items, pulled_rows, preferred_element_type=jnp.float32
        )
        * INVERSE_TEMP
    )
    logits = logits.reshape(blocks_here, row_block_count, slot_count * row_block_count)
    target_logits = soft_weights(
        teacher.reshape(blocks_here, row_block_count, slot_count * row_block_count), column_valid
    )
    weight_matrices = (soft_weights(logits, column_valid) - target_logits).astype(jnp.bfloat16)
    weight_matrices = weight_matrices.reshape(
        blocks_here, row_block_count, slot_count, row_block_count
    )
    query_sums = (
        jnp.einsum(
            "geal,lgay->gey", weight_matrices, pulled_rows, preferred_element_type=jnp.float32
        )
        * INVERSE_TEMP
    )
    passage_sums = (
        jnp.einsum(
            "fnyw,fnj->wfyj", weight_matrices, query_row_items, preferred_element_type=jnp.float32
        )
        * INVERSE_TEMP
    )
    block_terms = passage_sums.reshape(row_block_count, requests, width).astype(jnp.bfloat16)
    micro_count = section_inputs.shape[1] // dp_count
    col_width = width // dp_count
    micro_cols = jnp.transpose(
        query_sums[0, :micro_count].reshape(micro_count, dp_count, col_width), (1, 0, 2)
    )
    section_count = lax.axis_size("section")
    chunk = width // section_count
    term_pieces = passage_sums.reshape(dp_count, stripe, requests, section_count, chunk)
    term_pieces = jnp.transpose(term_pieces, (3, 0, 1, 2, 4)).astype(jnp.bfloat16)
    term_pieces = term_pieces.reshape(section_count * dp_count, stripe, requests, chunk)
    own_slots = lax.dynamic_slice_in_dim(all_slots, dp_index * requests, requests)
    slot_tags = jnp.broadcast_to(
        own_slots.astype(jnp.bfloat16)[None, None, :, None],
        (section_count * dp_count, stripe, requests, 1),
    )
    term_pieces = jnp.concatenate([term_pieces, slot_tags], axis=3)
    incoming_terms = lax.all_to_all(
        term_pieces, ("section", "dp"), split_axis=0, concat_axis=0, tiled=True
    )
    incoming_terms, carry_start = lax.optimization_barrier((incoming_terms, micro_cols))
    every_slot = incoming_terms[:, 0, :, chunk].astype(jnp.int32)
    onehot = (every_slot[:, :, None] == jnp.arange(block_total, dtype=jnp.int32)).astype(
        jnp.bfloat16
    )
    dense = jnp.einsum(
        "qsfc,qfn->snc",
        incoming_terms[:, :, :, :chunk],
        onehot,
        preferred_element_type=jnp.float32,
    )
    dense = dense.reshape(stripe, block_total, chunk).astype(jnp.bfloat16)
    passage_out = gathered_columns(dense.reshape(stripe * block_total, chunk), "section")
    passage_out = passage_out.reshape(stripe, block_total, width)
    entry = lax.all_to_all(carry_start, "dp", split_axis=0, concat_axis=1, tiled=True)
    weight_rows = section_weights[0]
    split_rows = weight_rows.reshape(col_width, dp_count, col_width)
    input_cols = section_inputs[0]
    pre = pre_acts[0].astype(jnp.float32)
    sigma = jax.nn.sigmoid(pre)
    slope = sigma * (1.0 + pre * (1.0 - sigma))
    carry = entry.reshape(dp_count * micro_count, col_width)
    section_count = lax.axis_size("section")
    section_index = lax.axis_index("section")
    grad_cols = jnp.zeros_like(carry)
    grad_weight = jnp.zeros((col_width, width), jnp.float32)
    for section_turn in range(section_count):
        active_flag = section_count - 1 - section_turn
        inner = (carry * slope).astype(jnp.bfloat16)
        piece = gathered_pieces(inner, "dp")
        back_sum = jnp.einsum(
            "dmj,idj->mi", piece, split_rows, preferred_element_type=jnp.float32
        )
        weight_part = jnp.einsum(
            "mi,dmj->idj", input_cols, piece, preferred_element_type=jnp.float32
        ).reshape(col_width, width)
        back_sum, layer_weight = (back_sum, weight_part)
        updated = carry + back_sum
        is_active = section_index == active_flag
        grad_cols = jnp.where(is_active, updated, grad_cols)
        grad_weight = jnp.where(is_active, layer_weight, grad_weight)
        if section_turn + 1 < section_count:
            carry = passed_along(updated, "section", -1)
    return (
        query_sums.reshape(blocks_here * row_block_count, width).astype(jnp.bfloat16),
        passage_out,
        grad_cols[None],
        grad_weight[None].astype(jnp.bfloat16),
    )


def solution(mesh):
    placed = (
        P(("section", "dp"), None),
        P("dp", None, None),
        P("section", None),
        P("section"),
        P(("section", "dp"), None),
        P("section", "dp", None),
        P("section", None, "dp"),
        P("section", None, "dp"),
    )
    return jax.shard_map(
        body,
        mesh=mesh,
        in_specs=placed,
        out_specs=(
            P(("section", "dp"), None),
            P("dp", None, None),
            P("section", None, "dp"),
            P("section", "dp", None),
        ),
        check_vma=False,
    )
```

profile of v0, /device:TPU:31, one launch (start us, length us, event | category | flops | bytes accessed | tf_op | source)
XLA Modules:
  0.0 504.5 jit_solution(12400093895437170567)
XLA Ops:
  3.7 4.4 copy.145
  8.1 14.6 %all-to-all-start = ((bf16[2,192,3584]{2,0,1:T(2,128)(2,1)}), bf16[2,192,3584]{2,0,1:T(2,128)(2,1)}, u32[]{:S(2)}, u32[]{:S(2)}) async-start(bf16[2,192,3584]{2,0,1:T(2,128)(2,1)} %copy.145), calls=%async_computation | async-start | bytes 5505024 | tf_op jit(solution)/shard_map/all_to_all | solution.py:50
  24.6 63.0 %all-to-all-done = bf16[2,192,3584]{2,0,1:T(2,128)(2,1)} async-done(((bf16[2,192,3584]{2,0,1:T(2,128)(2,1)}), bf16[2,192,3584]{2,0,1:T(2,128)(2,1)}, u32[]{:S(2)}, u32[]{:S(2)}) %all-to-all-start) | async-done | bytes 2752544 | tf_op jit(solution)/shard_map/all_to_all | solution.py:50
  87.6 5.2 %copy.146 = bf16[64,2,3,3584]{3,1,0,2:T(2,128)(2,1)} copy(bf16[64,2,3,3584]{3,1,2,0:T(2,128)(2,1)} %bitcast.5) | data formatting | bytes 5505024 | tf_op jit(solution)/shard_map/all_to_all | solution.py:50
  92.8 6.8 %reshape.331 = bf16[128,3,3584]{2,0,1:T(8,128)(2,1)} reshape(bf16[64,2,3,3584]{3,1,0,2:T(2,128)(2,1)} %copy.146) | data formatting | bytes 5505024 | tf_op jit(solution)/shard_map/reshape.5
  105.0 6.8 %convert_element_type.98 = bf16[64,2,3,8,448]{4,3,1,0,2:T(8,128)(2,1)} reshape(bf16[128,1,3,3584]{3,0,2,1:T(8,128)(2,1)} %fusion.2) | data formatting | bytes 5505024 | tf_op jit(solution)/shard_map/convert_element_type | solution.py:91
  116.2 4.9 copy.150
  121.1 14.6 %all-to-all-start.1 = ((bf16[512,2,3,449]{3,1,2,0:T(2,128)(2,1)}), bf16[512,2,3,449]{3,1,2,0:T(2,128)(2,1)}, u32[]{:S(2)}, u32[]{:S(2)}) async-start(bf16[512,2,3,449]{3,1,2,0:T(2,128)(2,1)} %copy.150), calls=%async_computation.1 | async-start | bytes 6291456 | tf_op jit(solution)/shard_map/all_to_all | solution.py:99
  139.2 68.6 %all-to-all-done.1 = bf16[512,2,3,449]{3,1,2,0:T(2,128)(2,1)} async-done(((bf16[512,2,3,449]{3,1,2,0:T(2,128)(2,1)}), bf16[512,2,3,449]{3,1,2,0:T(2,128)(2,1)}, u32[]{:S(2)}, u32[]{:S(2)}) %all-to-all-start.1) | async-done | bytes 2758688 | tf_op jit(solution)/shard_map/all_to_all | solution.py:99
  207.8 14.6 %all_to_all.74 = f32[64,1,56]{2,1,0:T(1,128)S(1)} all-to-all(f32[64,1,56]{2,1,0:T(1,128)S(1)} %bitcast.243), channel_id=1, replica_groups=mesh['section'=8,'dp'=64] {'dp'}, dimensions={0} | all-to-all | bytes 28672 | tf_op jit(solution)/shard_map/all_to_all | solution.py:116
  224.0 7.2 %all-to-all-start.4 = ((bf16[64,2,1792]{2,1,0:T(2,128)(2,1)}), bf16[64,2,1792]{2,1,0:T(2,128)(2,1)S(1)}, u32[]{:S(2)}, u32[]{:S(2)}) async-start(bf16[64,2,1792]{2,1,0:T(2,128)(2,1)} %reshape.370), calls=%async_computation.4 | async-start | bytes 917504 | tf_op jit(solution)/shard_map/all_to_all | solution.py:18
  233.1 13.7 %all-to-all-done.4 = bf16[64,2,1792]{2,1,0:T(2,128)(2,1)S(1)} async-done(((bf16[64,2,1792]{2,1,0:T(2,128)(2,1)}), bf16[64,2,1792]{2,1,0:T(2,128)(2,1)S(1)}, u32[]{:S(2)}, u32[]{:S(2)}) %all-to-all-start.4) | async-done | bytes 458784 | tf_op jit(solution)/shard_map/all_to_all | solution.py:18
  254.8 23.2 %all_to_all.75 = bf16[64,2,1792]{2,1,0:T(2,128)(2,1)S(1)} all-to-all(bf16[64,2,1792]{2,1,0:T(2,128)(2,1)S(1)} %reshape.372), channel_id=1, replica_groups=mesh['section'=8,'dp'=64] {'dp'}, dimensions={0} | all-to-all | bytes 917504 | tf_op jit(solution)/shard_map/all_to_all | solution.py:18
  286.0 23.2 %all_to_all.76 = bf16[64,2,1792]{2,1,0:T(2,128)(2,1)S(1)} all-to-all(bf16[64,2,1792]{2,1,0:T(2,128)(2,1)S(1)} %reshape.374), channel_id=1, replica_groups=mesh['section'=8,'dp'=64] {'dp'}, dimensions={0} | all-to-all | bytes 917504 | tf_op jit(solution)/shard_map/all_to_all | solution.py:18
  317.1 23.5 %all_to_all.77 = bf16[64,2,1792]{2,1,0:T(2,128)(2,1)S(1)} all-to-all(bf16[64,2,1792]{2,1,0:T(2,128)(2,1)S(1)} %reshape.376), channel_id=1, replica_groups=mesh['section'=8,'dp'=64] {'dp'}, dimensions={0} | all-to-all | bytes 917504 | tf_op jit(solution)/shard_map/all_to_all | solution.py:18
  348.7 23.2 %all_to_all.78 = bf16[64,2,1792]{2,1,0:T(2,128)(2,1)S(1)} all-to-all(bf16[64,2,1792]{2,1,0:T(2,128)(2,1)S(1)} %reshape.378), channel_id=1, replica_groups=mesh['section'=8,'dp'=64] {'dp'}, dimensions={0} | all-to-all | bytes 917504 | tf_op jit(solution)/shard_map/all_to_all | solution.py:18
  380.6 7.6 %all-to-all-start.9 = ((bf16[64,2,1792]{2,1,0:T(2,128)(2,1)}), bf16[64,2,1792]{2,1,0:T(2,128)(2,1)S(1)}, u32[]{:S(2)}, u32[]{:S(2)}) async-start(bf16[64,2,1792]{2,1,0:T(2,128)(2,1)} %reshape.380), calls=%async_computation.9 | async-start | bytes 917504 | tf_op jit(solution)/shard_map/all_to_all | solution.py:18
  388.2 8.7 %copy.151 = bf16[512,2,3,449]{0,3,2,1:T(8,128)(2,1)} copy(bf16[512,2,3,449]{3,1,2,0:T(2,128)(2,1)} %all-to-all-done.1) | data formatting | bytes 5517312 | tf_op jit(solution)/shard_map/optimization_barrier | solution.py:102
  405.0 4.5 all-to-all-start.2
  413.2 14.4 %collective-permute-done.5 = f32[64,56]{0,1:T(8,128)S(1)} collective-permute-done((f32[64,56]{0,1:T(8,128)S(1)}, f32[64,56]{0,1:T(8,128)S(1)}, u32[]{:S(2)}, u32[]{:S(2)}) %collective-permute-start.5) | collective-permute-done | bytes 14368 | tf_op jit(solution)/shard_map/ppermute | solution.py:12
  430.4 12.1 %all-to-all-start.10 = ((bf16[64,2,1792]{2,1,0:T(2,128)(2,1)}), bf16[64,2,1792]{2,1,0:T(2,128)(2,1)S(1)}, u32[]{:S(2)}, u32[]{:S(2)}) async-start(bf16[64,2,1792]{2,1,0:T(2,128)(2,1)} %reshape.382), calls=%async_computation.10 | async-start | bytes 917504 | tf_op jit(solution)/shard_map/all_to_all | solution.py:18
  448.8 9.3 %all-to-all-done.10 = bf16[64,2,1792]{2,1,0:T(2,128)(2,1)S(1)} async-done(((bf16[64,2,1792]{2,1,0:T(2,128)(2,1)}), bf16[64,2,1792]{2,1,0:T(2,128)(2,1)S(1)}, u32[]{:S(2)}, u32[]{:S(2)}) %all-to-all-start.10) | async-done | bytes 458784 | tf_op jit(solution)/shard_map/all_to_all | solution.py:18
  468.0 8.0 %all-to-all-start.11 = ((bf16[64,2,1792]{2,1,0:T(2,128)(2,1)}), bf16[64,2,1792]{2,1,0:T(2,128)(2,1)S(1)}, u32[]{:S(2)}, u32[]{:S(2)}) async-start(bf16[64,2,1792]{2,1,0:T(2,128)(2,1)} %reshape.384), calls=%async_computation.11 | async-start | bytes 917504 | tf_op jit(solution)/shard_map/all_to_all | solution.py:18
  483.7 7.9 %all-to-all-done.11 = bf16[64,2,1792]{2,1,0:T(2,128)(2,1)S(1)} async-done(((bf16[64,2,1792]{2,1,0:T(2,128)(2,1)}), bf16[64,2,1792]{2,1,0:T(2,128)(2,1)S(1)}, u32[]{:S(2)}, u32[]{:S(2)}) %all-to-all-start.11) | async-done | bytes 458784 | tf_op jit(solution)/shard_map/all_to_all | solution.py:18
  (136 shorter events, 113.0 us)
Async XLA Ops:
  0.6 99.0 %copy-start = (bf16[128,3584]{1,0:T(8,128)(2,1)S(1)}, bf16[128,3584]{1,0:T(8,128)(2,1)}, u32[]{:S(2)}) copy-start(bf16[128,3584]{1,0:T(8,128)(2,1)} %param.8) | copy-start | bytes 2752516
  8.1 14.7 %copy-start.17 = (f32[128,384]{1,0:T(8,128)S(1)}, f32[128,384]{1,0:T(8,128)}, u32[]{:S(2)}) copy-start(f32[128,384]{1,0:T(8,128)} %param.12) | copy-start | bytes 589828
  8.1 14.8 %copy-start.20 = (s32[64]{0:T(128)S(1)}, s32[64]{0:T(128)}, u32[]{:S(2)}) copy-start(s32[64]{0:T(128)} %param.11) | copy-start | bytes 772
  8.1 79.5 %all-to-all-start = ((bf16[2,192,3584]{2,0,1:T(2,128)(2,1)}), bf16[2,192,3584]{2,0,1:T(2,128)(2,1)}, u32[]{:S(2)}, u32[]{:S(2)}) async-start(bf16[2,192,3584]{2,0,1:T(2,128)(2,1)} %copy.145), calls=%async_computation | async-start | bytes 5505024 | tf_op jit(solution)/shard_map/all_to_all | solution.py:50
  121.1 86.7 %all-to-all-start.1 = ((bf16[512,2,3,449]{3,1,2,0:T(2,128)(2,1)}), bf16[512,2,3,449]{3,1,2,0:T(2,128)(2,1)}, u32[]{:S(2)}, u32[]{:S(2)}) async-start(bf16[512,2,3,449]{3,1,2,0:T(2,128)(2,1)} %copy.150), calls=%async_computation.1 | async-start | bytes 6291456 | tf_op jit(solution)/shard_map/all_to_all | solution.py:99
  135.7 86.8 %copy-start.13 = (bf16[1,64,56]{1,2,0:T(8,128)(2,1)S(1)}, bf16[1,64,56]{1,2,0:T(8,128)(2,1)}, u32[]{:S(2)}) copy-start(bf16[1,64,56]{1,2,0:T(8,128)(2,1)} %param.15) | copy-start | bytes 21508
  139.1 92.1 %copy-start.16 = (bf16[1,56,3584]{2,1,0:T(8,128)(2,1)S(1)}, bf16[1,56,3584]{2,1,0:T(8,128)(2,1)}, u32[]{:S(2)}) copy-start(bf16[1,56,3584]{2,1,0:T(8,128)(2,1)} %param.13) | copy-start | bytes 1204228
  224.0 22.8 %all-to-all-start.4 = ((bf16[64,2,1792]{2,1,0:T(2,128)(2,1)}), bf16[64,2,1792]{2,1,0:T(2,128)(2,1)S(1)}, u32[]{:S(2)}, u32[]{:S(2)}) async-start(bf16[64,2,1792]{2,1,0:T(2,128)(2,1)} %reshape.370), calls=%async_computation.4 | async-start | bytes 917504 | tf_op jit(solution)/shard_map/all_to_all | solution.py:18
  248.3 5.8 %collective-permute-start = (f32[64,56]{0,1:T(8,128)S(1)}, f32[64,56]{0,1:T(8,128)S(1)}, u32[]{:S(2)}, u32[]{:S(2)}) collective-permute-start(f32[64,56]{0,1:T(8,128)S(1)} %fusion.13), channel_id=1, source_target_pairs={{64,0},{128,64},{192,128},{256,192},{320,256},{384,320},{448,384},... | collective-permute-start | bytes 43016 | tf_op jit(solution)/shard_map/ppermute | solution.py:12
  279.4 5.8 %collective-permute-start.1 = (f32[64,56]{0,1:T(8,128)S(1)}, f32[64,56]{0,1:T(8,128)S(1)}, u32[]{:S(2)}, u32[]{:S(2)}) collective-permute-start(f32[64,56]{0,1:T(8,128)S(1)} %fusion.14), channel_id=1, source_target_pairs={{64,0},{128,64},{192,128},{256,192},{320,256},{384,320},{448,384},... | collective-permute-start | bytes 43016 | tf_op jit(solution)/shard_map/ppermute | solution.py:12
  310.6 5.8 %collective-permute-start.2 = (f32[64,56]{0,1:T(8,128)S(1)}, f32[64,56]{0,1:T(8,128)S(1)}, u32[]{:S(2)}, u32[]{:S(2)}) collective-permute-start(f32[64,56]{0,1:T(8,128)S(1)} %fusion.15), channel_id=1, source_target_pairs={{64,0},{128,64},{192,128},{256,192},{320,256},{384,320},{448,384},... | collective-permute-start | bytes 43016 | tf_op jit(solution)/shard_map/ppermute | solution.py:12
  342.1 5.8 %collective-permute-start.3 = (f32[64,56]{0,1:T(8,128)S(1)}, f32[64,56]{0,1:T(8,128)S(1)}, u32[]{:S(2)}, u32[]{:S(2)}) collective-permute-start(f32[64,56]{0,1:T(8,128)S(1)} %fusion.16), channel_id=1, source_target_pairs={{64,0},{128,64},{192,128},{256,192},{320,256},{384,320},{448,384},... | collective-permute-start | bytes 43016 | tf_op jit(solution)/shard_map/ppermute | solution.py:12
  373.3 5.8 %collective-permute-start.4 = (f32[64,56]{0,1:T(8,128)S(1)}, f32[64,56]{0,1:T(8,128)S(1)}, u32[]{:S(2)}, u32[]{:S(2)}) collective-permute-start(f32[64,56]{0,1:T(8,128)S(1)} %fusion.17), channel_id=1, source_target_pairs={{64,0},{128,64},{192,128},{256,192},{320,256},{384,320},{448,384},... | collective-permute-start | bytes 43016 | tf_op jit(solution)/shard_map/ppermute | solution.py:12
  380.6 23.4 %all-to-all-start.9 = ((bf16[64,2,1792]{2,1,0:T(2,128)(2,1)}), bf16[64,2,1792]{2,1,0:T(2,128)(2,1)S(1)}, u32[]{:S(2)}, u32[]{:S(2)}) async-start(bf16[64,2,1792]{2,1,0:T(2,128)(2,1)} %reshape.380), calls=%async_computation.9 | async-start | bytes 917504 | tf_op jit(solution)/shard_map/all_to_all | solution.py:18
  405.0 25.3 %all-to-all-start.2 = ((bf16[8,128,448]{1,2,0:T(8,128)(2,1)}), bf16[8,128,448]{1,2,0:T(8,128)(2,1)S(1)}, u32[]{:S(2)}, u32[]{:S(2)}) async-start(bf16[8,128,448]{1,2,0:T(8,128)(2,1)} %broadcast_in_dim.135), calls=%async_computation.2 | async-start | bytes 1835008 | tf_op jit(solution)/shard_map/all_to_all | solution.py:24
  410.1 17.5 %copy-start.9 = (bf16[64,56,64]{2,1,0:T(8,128)(2,1)}, bf16[64,56,64]{2,1,0:T(8,128)(2,1)S(1)}, u32[]{:S(2)}) copy-start(bf16[64,56,64]{2,1,0:T(8,128)(2,1)S(1)} %reshape.381) | copy-start | bytes 1376260
  411.0 16.6 %collective-permute-start.5 = (f32[64,56]{0,1:T(8,128)S(1)}, f32[64,56]{0,1:T(8,128)S(1)}, u32[]{:S(2)}, u32[]{:S(2)}) collective-permute-start(f32[64,56]{0,1:T(8,128)S(1)} %fusion.18), channel_id=1, source_target_pairs={{64,0},{128,64},{192,128},{256,192},{320,256},{384,320},{448,384},... | collective-permute-start | bytes 43016 | tf_op jit(solution)/shard_map/ppermute | solution.py:12
  427.6 14.8 %copy-start.18 = (f32[64,56]{0,1:T(8,128)}, f32[64,56]{0,1:T(8,128)S(1)}, u32[]{:S(2)}) copy-start(f32[64,56]{0,1:T(8,128)S(1)} %collective-permute-done.5) | copy-start | bytes 43012
  429.2 16.5 %copy-start.15 = (bf16[1,64,56]{1,2,0:T(8,128)(2,1)S(1)}, bf16[1,64,56]{1,2,0:T(8,128)(2,1)}, u32[]{:S(2)}) copy-start(bf16[1,64,56]{1,2,0:T(8,128)(2,1)} %param.14) | copy-start | bytes 21508
  430.4 27.7 %all-to-all-start.10 = ((bf16[64,2,1792]{2,1,0:T(2,128)(2,1)}), bf16[64,2,1792]{2,1,0:T(2,128)(2,1)S(1)}, u32[]{:S(2)}, u32[]{:S(2)}) async-start(bf16[64,2,1792]{2,1,0:T(2,128)(2,1)} %reshape.382), calls=%async_computation.10 | async-start | bytes 917504 | tf_op jit(solution)/shard_map/all_to_all | solution.py:18
  445.6 16.9 %copy-start.4 = (bf16[64,56,64]{2,1,0:T(8,128)(2,1)S(1)}, bf16[64,56,64]{2,1,0:T(8,128)(2,1)}, u32[]{:S(2)}) copy-start(bf16[64,56,64]{2,1,0:T(8,128)(2,1)} %copy-done.3) | copy-start | bytes 1376260
  460.5 15.6 %copy-start.6 = (bf16[64,56,64]{2,1,0:T(8,128)(2,1)S(1)}, bf16[64,56,64]{2,1,0:T(8,128)(2,1)}, u32[]{:S(2)}) copy-start(bf16[64,56,64]{2,1,0:T(8,128)(2,1)} %copy-done.5) | copy-start | bytes 1376260
  460.5 6.0 %collective-permute-start.6 = (f32[64,56]{0,1:T(8,128)S(1)}, f32[64,56]{0,1:T(8,128)S(1)}, u32[]{:S(2)}, u32[]{:S(2)}) collective-permute-start(f32[64,56]{0,1:T(8,128)S(1)} %fusion.19), channel_id=1, source_target_pairs={{64,0},{128,64},{192,128},{256,192},{320,256},{384,320},{448,384},... | collective-permute-start | bytes 43016 | tf_op jit(solution)/shard_map/ppermute | solution.py:12
  468.0 23.7 %all-to-all-start.11 = ((bf16[64,2,1792]{2,1,0:T(2,128)(2,1)}), bf16[64,2,1792]{2,1,0:T(2,128)(2,1)S(1)}, u32[]{:S(2)}, u32[]{:S(2)}) async-start(bf16[64,2,1792]{2,1,0:T(2,128)(2,1)} %reshape.384), calls=%async_computation.11 | async-start | bytes 917504 | tf_op jit(solution)/shard_map/all_to_all | solution.py:18
  (11 other events, 79.2 us)
where the time goes:
time: 514 us; the launch traced here: 504 us
  waiting for transfers between devices  202 us (39%)
  blocking collectives  108 us (21%)
  starting transfers between devices  83.4 us (16%)
  local copies, waits for them, and re-layouts  68.4 us (13%)
  matrix products  38.4 us (7%)
    all_to_all x4, blocking collectives, gathered_pieces(): return lax.all_to_all(copies, axis, 0, 0, tiled=True)  93 us
    all_to_all x1, waiting for transfers between devices, body(): lax.all_to_all(term_pieces, ('section', 'dp'), split_axis=0, concat_axis=...  68.6 us
    all_to_all x1, waiting for transfers between devices, body(): lax.all_to_all(outgoing, 'dp', split_axis=1, concat_axis=0, tiled=True)  63 us
    ppermute x7, waiting for transfers between devices, passed_along(): lax.ppermute(value, axis, [(source, source + steps) for source in range(i...  35 us
    all_to_all x4, starting transfers between devices, gathered_pieces(): return lax.all_to_all(copies, axis, 0, 0, tiled=True)  34.9 us
    all_to_all x4, waiting for transfers between devices, gathered_pieces(): return lax.all_to_all(copies, axis, 0, 0, tiled=True)  34.5 us
    dot_general x8, matrix products, body(): jnp.einsum('mi,dmj->idj', input_cols, piece, preferred_element_type=jnp.f...  17.4 us
    unnamed x69, local copies, waits for them, and re-layouts  14.9 us
  transfers between devices with their start and end apart: 14, of which 14 were waited for; matrix products, arithmetic and copies ran while one was open for 8% of the time, Pallas kernels for 0%

commit v1 on v0

--- a/solution.py
+++ b/solution.py
@@ -114,39 +114,50 @@
     passage_out = gathered_columns(dense.reshape(stripe * block_total, chunk), "section")
     passage_out = passage_out.reshape(stripe, block_total, width)
     entry = lax.all_to_all(carry_start, "dp", split_axis=0, concat_axis=1, tiled=True)
-    weight_rows = section_weights[0]
-    split_rows = weight_rows.reshape(col_width, dp_count, col_width)
-    input_cols = section_inputs[0]
-    pre = pre_acts[0].astype(jnp.float32)
-    sigma = jax.nn.sigmoid(pre)
-    slope = sigma * (1.0 + pre * (1.0 - sigma))
-    carry = entry.reshape(dp_count * micro_count, col_width)
     section_count = lax.axis_size("section")
     section_index = lax.axis_index("section")
-    grad_cols = jnp.zeros_like(carry)
-    grad_weight = jnp.zeros((col_width, width), jnp.float32)
-    for section_turn in range(section_count):
-        active_flag = section_count - 1 - section_turn
+    last = section_count - 1
+    own_rows = section_weights[0]
+    own_cols = jnp.stack([pre_acts[0], section_inputs[0]])
+    rows_of = {last: own_rows}
+    cols_of = {last: own_cols}
+    for source in range(last):
+        rows_of[source] = lax.ppermute(own_rows, "section", [(source, last)])
+        cols_of[source] = lax.ppermute(own_cols, "section", [(source, last)])
+    carry = entry.reshape(dp_count * micro_count, col_width)
+    grads_of = {}
+    weights_of = {}
+    for source in range(last, -1, -1):
+        pre = cols_of[source][0].astype(jnp.float32)
+        sigma = jax.nn.sigmoid(pre)
+        slope = sigma * (1.0 + pre * (1.0 - sigma))
         inner = (carry * slope).astype(jnp.bfloat16)
         piece = gathered_pieces(inner, "dp")
+        split_rows = rows_of[source].reshape(col_width, dp_count, col_width)
         back_sum = jnp.einsum(
             "dmj,idj->mi", piece, split_rows, preferred_element_type=jnp.float32
         )
-        weight_part = jnp.einsum(
-            "mi,dmj->idj", input_cols, piece, preferred_element_type=jnp.float32
-        ).reshape(col_width, width)
-        back_sum, layer_weight = (back_sum, weight_part)
-        updated = carry + back_sum
-        is_active = section_index == active_flag
-        grad_cols = jnp.where(is_active, updated, grad_cols)
-        grad_weight = jnp.where(is_active, layer_weight, grad_weight)
-        if section_turn + 1 < section_count:
-            carry = passed_along(updated, "section", -1)
+        weights_of[source] = (
+            jnp.einsum(
+                "mi,dmj->idj", cols_of[source][1], piece, preferred_element_type=jnp.float32
+            )
+            .reshape(col_width, width)
+            .astype(jnp.bfloat16)
+        )
+        carry = carry + back_sum
+        grads_of[source] = carry
+    grad_cols = grads_of[last]
+    grad_weight = weights_of[last]
+    for source in range(last):
+        sent_grads = lax.ppermute(grads_of[source], "section", [(last, source)])
+        sent_weights = lax.ppermute(weights_of[source], "section", [(last, source)])
+        grad_cols = jnp.where(section_index == source, sent_grads, grad_cols)
+        grad_weight = jnp.where(section_index == source, sent_weights, grad_weight)
     return (
         query_sums.reshape(blocks_here * row_block_count, width).astype(jnp.bfloat16),
         passage_out,
         grad_cols[None],
-        grad_weight[None].astype(jnp.bfloat16),
+        grad_weight[None],
     )
 
 

time: 514 us -> 573 us (1.11)
  the two profiles are of different devices: /device:TPU:31 before, /device:TPU:6 now
where the time goes in v1:
time: 573 us; the launch traced here: 563 us
  waiting for transfers between devices  257 us (45%)
  starting transfers between devices  165 us (29%)
  local copies, waits for them, and re-layouts  89.3 us (16%)
  matrix products  43.8 us (8%)
    all_to_all x8, waiting for transfers between devices, gathered_pieces(): return lax.all_to_all(copies, axis, 0, 0, tiled=True)  71.8 us
    all_to_all x1, waiting for transfers between devices, body(): lax.all_to_all(term_pieces, ('section', 'dp'), split_axis=0, concat_axis=...  69 us
    all_to_all x1, waiting for transfers between devices, body(): lax.all_to_all(outgoing, 'dp', split_axis=1, concat_axis=0, tiled=True)  60.9 us
    all_to_all x8, starting transfers between devices, gathered_pieces(): return lax.all_to_all(copies, axis, 0, 0, tiled=True)  57.8 us
    ppermute x7, starting transfers between devices, body(): rows_of[source] = lax.ppermute(own_rows, 'section', [(source, last)])  39.8 us
    ppermute x7, waiting for transfers between devices, body(): sent_weights = lax.ppermute(weights_of[source], 'section', [(last, source)])  28.2 us
    reshape x7, local copies, waits for them, and re-layouts, body(): split_rows = rows_of[source].reshape(col_width, dp_count, col_width)  19.6 us
    dot_general x8, matrix products, body(): jnp.einsum('dmj,idj->mi', piece, split_rows, preferred_element_type=jnp.f...  18.2 us
  transfers between devices with their start and end apart: 40, of which 13 were waited for; matrix products, arithmetic and copies ran while one was open for 12% of the time, Pallas kernels for 0%

profile of v1, /device:TPU:6, one launch (start us, length us, event | category | flops | bytes accessed | tf_op | source)
XLA Modules:
  0.0 562.5 jit_solution(17578276170574108647)
XLA Ops:
  8.1 14.3 %all-to-all-start = ((bf16[2,192,3584]{2,0,1:T(2,128)(2,1)}), bf16[2,192,3584]{2,0,1:T(2,128)(2,1)}, u32[]{:S(2)}, u32[]{:S(2)}) async-start(bf16[2,192,3584]{2,0,1:T(2,128)(2,1)} %copy.149), calls=%async_computation | async-start | bytes 5505024 | tf_op jit(solution)/shard_map/all_to_all | solution.py:50
  24.3 60.9 %all-to-all-done = bf16[2,192,3584]{2,0,1:T(2,128)(2,1)} async-done(((bf16[2,192,3584]{2,0,1:T(2,128)(2,1)}), bf16[2,192,3584]{2,0,1:T(2,128)(2,1)}, u32[]{:S(2)}, u32[]{:S(2)}) %all-to-all-start) | async-done | bytes 2752544 | tf_op jit(solution)/shard_map/all_to_all | solution.py:50
  118.7 17.0 %all-to-all-start.1 = ((bf16[512,2,3,449]{3,1,2,0:T(2,128)(2,1)}), bf16[512,2,3,449]{3,1,2,0:T(2,128)(2,1)}, u32[]{:S(2)}, u32[]{:S(2)}) async-start(bf16[512,2,3,449]{3,1,2,0:T(2,128)(2,1)} %copy.154), calls=%async_computation.1 | async-start | bytes 6291456 | tf_op jit(solution)/shard_map/all_to_all | solution.py:99
  139.8 69.0 %all-to-all-done.1 = bf16[512,2,3,449]{3,1,2,0:T(2,128)(2,1)} async-done(((bf16[512,2,3,449]{3,1,2,0:T(2,128)(2,1)}), bf16[512,2,3,449]{3,1,2,0:T(2,128)(2,1)}, u32[]{:S(2)}, u32[]{:S(2)}) %all-to-all-start.1) | async-done | bytes 2758688 | tf_op jit(solution)/shard_map/all_to_all | solution.py:99
  208.8 8.9 %all-to-all-start.3 = ((f32[64,1,56]{2,1,0:T(1,128)}), f32[64,1,56]{2,1,0:T(1,128)S(1)}, u32[]{:S(2)}, u32[]{:S(2)}) async-start(f32[64,1,56]{2,1,0:T(1,128)} %bitcast.26), calls=%async_computation.3 | async-start | bytes 65536 | tf_op jit(solution)/shard_map/all_to_all | solution.py:116
  217.8 7.4 %all-to-all-done.3 = f32[64,1,56]{2,1,0:T(1,128)S(1)} async-done(((f32[64,1,56]{2,1,0:T(1,128)}), f32[64,1,56]{2,1,0:T(1,128)S(1)}, u32[]{:S(2)}, u32[]{:S(2)}) %all-to-all-start.3) | async-done | bytes 14368 | tf_op jit(solution)/shard_map/all_to_all | solution.py:116
  236.4 12.3 %all-to-all-done.4 = bf16[64,2,1792]{2,1,0:T(2,128)(2,1)S(1)} async-done(((bf16[64,2,1792]{2,1,0:T(2,128)(2,1)}), bf16[64,2,1792]{2,1,0:T(2,128)(2,1)S(1)}, u32[]{:S(2)}, u32[]{:S(2)}) %all-to-all-start.4) | async-done | bytes 458784 | tf_op jit(solution)/shard_map/all_to_all | solution.py:18
  251.7 6.8 %all-to-all-start.5 = ((bf16[64,2,1792]{2,1,0:T(2,128)(2,1)}), bf16[64,2,1792]{2,1,0:T(2,128)(2,1)S(1)}, u32[]{:S(2)}, u32[]{:S(2)}) async-start(bf16[64,2,1792]{2,1,0:T(2,128)(2,1)} %reshape.310), calls=%async_computation.5 | async-start | bytes 917504 | tf_op jit(solution)/shard_map/all_to_all | solution.py:18
  262.7 11.2 %all-to-all-done.5 = bf16[64,2,1792]{2,1,0:T(2,128)(2,1)S(1)} async-done(((bf16[64,2,1792]{2,1,0:T(2,128)(2,1)}), bf16[64,2,1792]{2,1,0:T(2,128)(2,1)S(1)}, u32[]{:S(2)}, u32[]{:S(2)}) %all-to-all-start.5) | async-done | bytes 458784 | tf_op jit(solution)/shard_map/all_to_all | solution.py:18
  278.1 6.8 %all-to-all-start.6 = ((bf16[64,2,1792]{2,1,0:T(2,128)(2,1)}), bf16[64,2,1792]{2,1,0:T(2,128)(2,1)S(1)}, u32[]{:S(2)}, u32[]{:S(2)}) async-start(bf16[64,2,1792]{2,1,0:T(2,128)(2,1)} %reshape.312), calls=%async_computation.6 | async-start | bytes 917504 | tf_op jit(solution)/shard_map/all_to_all | solution.py:18
  289.2 11.1 %all-to-all-done.6 = bf16[64,2,1792]{2,1,0:T(2,128)(2,1)S(1)} async-done(((bf16[64,2,1792]{2,1,0:T(2,128)(2,1)}), bf16[64,2,1792]{2,1,0:T(2,128)(2,1)S(1)}, u32[]{:S(2)}, u32[]{:S(2)}) %all-to-all-start.6) | async-done | bytes 458784 | tf_op jit(solution)/shard_map/all_to_all | solution.py:18
  304.8 6.8 %all-to-all-start.7 = ((bf16[64,2,1792]{2,1,0:T(2,128)(2,1)}), bf16[64,2,1792]{2,1,0:T(2,128)(2,1)S(1)}, u32[]{:S(2)}, u32[]{:S(2)}) async-start(bf16[64,2,1792]{2,1,0:T(2,128)(2,1)} %reshape.314), calls=%async_computation.7 | async-start | bytes 917504 | tf_op jit(solution)/shard_map/all_to_all | solution.py:18
  315.8 11.2 %all-to-all-done.7 = bf16[64,2,1792]{2,1,0:T(2,128)(2,1)S(1)} async-done(((bf16[64,2,1792]{2,1,0:T(2,128)(2,1)}), bf16[64,2,1792]{2,1,0:T(2,128)(2,1)S(1)}, u32[]{:S(2)}, u32[]{:S(2)}) %all-to-all-start.7) | async-done | bytes 458784 | tf_op jit(solution)/shard_map/all_to_all | solution.py:18
  331.5 6.8 %all-to-all-start.8 = ((bf16[64,2,1792]{2,1,0:T(2,128)(2,1)}), bf16[64,2,1792]{2,1,0:T(2,128)(2,1)S(1)}, u32[]{:S(2)}, u32[]{:S(2)}) async-start(bf16[64,2,1792]{2,1,0:T(2,128)(2,1)} %reshape.316), calls=%async_computation.8 | async-start | bytes 917504 | tf_op jit(solution)/shard_map/all_to_all | solution.py:18
  342.7 11.0 %all-to-all-done.8 = bf16[64,2,1792]{2,1,0:T(2,128)(2,1)S(1)} async-done(((bf16[64,2,1792]{2,1,0:T(2,128)(2,1)}), bf16[64,2,1792]{2,1,0:T(2,128)(2,1)S(1)}, u32[]{:S(2)}, u32[]{:S(2)}) %all-to-all-start.8) | async-done | bytes 458784 | tf_op jit(solution)/shard_map/all_to_all | solution.py:18
  358.2 6.8 %all-to-all-start.9 = ((bf16[64,2,1792]{2,1,0:T(2,128)(2,1)}), bf16[64,2,1792]{2,1,0:T(2,128)(2,1)S(1)}, u32[]{:S(2)}, u32[]{:S(2)}) async-start(bf16[64,2,1792]{2,1,0:T(2,128)(2,1)} %reshape.318), calls=%async_computation.9 | async-start | bytes 917504 | tf_op jit(solution)/shard_map/all_to_all | solution.py:18
  369.2 11.2 %all-to-all-done.9 = bf16[64,2,1792]{2,1,0:T(2,128)(2,1)S(1)} async-done(((bf16[64,2,1792]{2,1,0:T(2,128)(2,1)}), bf16[64,2,1792]{2,1,0:T(2,128)(2,1)S(1)}, u32[]{:S(2)}, u32[]{:S(2)}) %all-to-all-start.9) | async-done | bytes 458784 | tf_op jit(solution)/shard_map/all_to_all | solution.py:18
  385.5 6.8 %all-to-all-start.10 = ((bf16[64,2,1792]{2,1,0:T(2,128)(2,1)}), bf16[64,2,1792]{2,1,0:T(2,128)(2,1)S(1)}, u32[]{:S(2)}, u32[]{:S(2)}) async-start(bf16[64,2,1792]{2,1,0:T(2,128)(2,1)} %reshape.320), calls=%async_computation.10 | async-start | bytes 917504 | tf_op jit(solution)/shard_map/all_to_all | solution.py:18
  393.0 35.7 %collective-permute-start.19 = (bf16[56,3584]{1,0:T(8,128)(2,1)}, bf16[56,3584]{1,0:T(8,128)(2,1)S(1)}, u32[]{:S(2)}, u32[]{:S(2)}) collective-permute-start(bf16[56,3584]{1,0:T(8,128)(2,1)} %bitcast.286), channel_id=1, source_target_pairs={{0,448},{1,449},{2,450},{3,451},{4,452},{5,453},{6,454},{7,455},{8... | collective-permute-start | bytes 1204232 | tf_op jit(solution)/shard_map/ppermute | solution.py:125
  433.1 13.0 %collective-permute-done.19 = bf16[56,3584]{1,0:T(8,128)(2,1)S(1)} collective-permute-done((bf16[56,3584]{1,0:T(8,128)(2,1)}, bf16[56,3584]{1,0:T(8,128)(2,1)S(1)}, u32[]{:S(2)}, u32[]{:S(2)}) %collective-permute-start.19) | collective-permute-done | bytes 401440 | tf_op jit(solution)/shard_map/ppermute | solution.py:125
  448.9 8.6 %copy.155 = bf16[512,2,3,449]{0,3,2,1:T(8,128)(2,1)} copy(bf16[512,2,3,449]{3,1,2,0:T(2,128)(2,1)} %all-to-all-done.1) | data formatting | bytes 5517312 | tf_op jit(solution)/shard_map/optimization_barrier | solution.py:102
  462.6 10.5 %all-to-all-start.11 = ((bf16[64,2,1792]{2,1,0:T(2,128)(2,1)}), bf16[64,2,1792]{2,1,0:T(2,128)(2,1)S(1)}, u32[]{:S(2)}, u32[]{:S(2)}) async-start(bf16[64,2,1792]{2,1,0:T(2,128)(2,1)} %reshape.322), calls=%async_computation.11 | async-start | bytes 917504 | tf_op jit(solution)/shard_map/all_to_all | solution.py:18
  513.5 7.0 %collective-permute-done.20 = f32[64,56]{0,1:T(8,128)S(1)} collective-permute-done((f32[64,56]{0,1:T(8,128)S(1)}, f32[64,56]{0,1:T(8,128)S(1)}, u32[]{:S(2)}, u32[]{:S(2)}) %collective-permute-start.20) | collective-permute-done | bytes 14368 | tf_op jit(solution)/shard_map/ppermute | solution.py:152
  531.9 28.2 %collective-permute-done.27 = bf16[56,3584]{1,0:T(8,128)(2,1)} collective-permute-done((bf16[56,3584]{1,0:T(8,128)(2,1)}, bf16[56,3584]{1,0:T(8,128)(2,1)}, u32[]{:S(2)}, u32[]{:S(2)}) %collective-permute-start.27) | collective-permute-done | bytes 401440 | tf_op jit(solution)/shard_map/ppermute | solution.py:153
  (211 shorter events, 170.9 us)
Async XLA Ops:
  8.1 77.0 %all-to-all-start = ((bf16[2,192,3584]{2,0,1:T(2,128)(2,1)}), bf16[2,192,3584]{2,0,1:T(2,128)(2,1)}, u32[]{:S(2)}, u32[]{:S(2)}) async-start(bf16[2,192,3584]{2,0,1:T(2,128)(2,1)} %copy.149), calls=%async_computation | async-start | bytes 5505024 | tf_op jit(solution)/shard_map/all_to_all | solution.py:50
  118.7 90.1 %all-to-all-start.1 = ((bf16[512,2,3,449]{3,1,2,0:T(2,128)(2,1)}), bf16[512,2,3,449]{3,1,2,0:T(2,128)(2,1)}, u32[]{:S(2)}, u32[]{:S(2)}) async-start(bf16[512,2,3,449]{3,1,2,0:T(2,128)(2,1)} %copy.154), calls=%async_computation.1 | async-start | bytes 6291456 | tf_op jit(solution)/shard_map/all_to_all | solution.py:99
  226.8 22.0 %all-to-all-start.4 = ((bf16[64,2,1792]{2,1,0:T(2,128)(2,1)}), bf16[64,2,1792]{2,1,0:T(2,128)(2,1)S(1)}, u32[]{:S(2)}, u32[]{:S(2)}) async-start(bf16[64,2,1792]{2,1,0:T(2,128)(2,1)} %reshape.308), calls=%async_computation.4 | async-start | bytes 917504 | tf_op jit(solution)/shard_map/all_to_all | solution.py:18
  251.7 22.2 %all-to-all-start.5 = ((bf16[64,2,1792]{2,1,0:T(2,128)(2,1)}), bf16[64,2,1792]{2,1,0:T(2,128)(2,1)S(1)}, u32[]{:S(2)}, u32[]{:S(2)}) async-start(bf16[64,2,1792]{2,1,0:T(2,128)(2,1)} %reshape.310), calls=%async_computation.5 | async-start | bytes 917504 | tf_op jit(solution)/shard_map/all_to_all | solution.py:18
  278.1 22.2 %all-to-all-start.6 = ((bf16[64,2,1792]{2,1,0:T(2,128)(2,1)}), bf16[64,2,1792]{2,1,0:T(2,128)(2,1)S(1)}, u32[]{:S(2)}, u32[]{:S(2)}) async-start(bf16[64,2,1792]{2,1,0:T(2,128)(2,1)} %reshape.312), calls=%async_computation.6 | async-start | bytes 917504 | tf_op jit(solution)/shard_map/all_to_all | solution.py:18
  304.8 22.2 %all-to-all-start.7 = ((bf16[64,2,1792]{2,1,0:T(2,128)(2,1)}), bf16[64,2,1792]{2,1,0:T(2,128)(2,1)S(1)}, u32[]{:S(2)}, u32[]{:S(2)}) async-start(bf16[64,2,1792]{2,1,0:T(2,128)(2,1)} %reshape.314), calls=%async_computation.7 | async-start | bytes 917504 | tf_op jit(solution)/shard_map/all_to_all | solution.py:18
  331.5 22.2 %all-to-all-start.8 = ((bf16[64,2,1792]{2,1,0:T(2,128)(2,1)}), bf16[64,2,1792]{2,1,0:T(2,128)(2,1)S(1)}, u32[]{:S(2)}, u32[]{:S(2)}) async-start(bf16[64,2,1792]{2,1,0:T(2,128)(2,1)} %reshape.316), calls=%async_computation.8 | async-start | bytes 917504 | tf_op jit(solution)/shard_map/all_to_all | solution.py:18
  358.2 22.2 %all-to-all-start.9 = ((bf16[64,2,1792]{2,1,0:T(2,128)(2,1)}), bf16[64,2,1792]{2,1,0:T(2,128)(2,1)S(1)}, u32[]{:S(2)}, u32[]{:S(2)}) async-start(bf16[64,2,1792]{2,1,0:T(2,128)(2,1)} %reshape.318), calls=%async_computation.9 | async-start | bytes 917504 | tf_op jit(solution)/shard_map/all_to_all | solution.py:18
  385.5 72.1 %all-to-all-start.10 = ((bf16[64,2,1792]{2,1,0:T(2,128)(2,1)}), bf16[64,2,1792]{2,1,0:T(2,128)(2,1)S(1)}, u32[]{:S(2)}, u32[]{:S(2)}) async-start(bf16[64,2,1792]{2,1,0:T(2,128)(2,1)} %reshape.320), calls=%async_computation.10 | async-start | bytes 917504 | tf_op jit(solution)/shard_map/all_to_all | solution.py:18
  392.3 38.0 %collective-permute-start.16 = (bf16[56,3584]{1,0:T(8,128)(2,1)}, bf16[56,3584]{1,0:T(8,128)(2,1)S(1)}, u32[]{:S(2)}, u32[]{:S(2)}) collective-permute-start(bf16[56,3584]{1,0:T(8,128)(2,1)} %bitcast.285), channel_id=1, source_target_pairs={{64,448},{65,449},{66,450},{67,451},{68,452},{69,453},{70,454},{71... | collective-permute-start | bytes 1204232 | tf_op jit(solution)/shard_map/ppermute | solution.py:125
  393.0 53.1 %collective-permute-start.19 = (bf16[56,3584]{1,0:T(8,128)(2,1)}, bf16[56,3584]{1,0:T(8,128)(2,1)S(1)}, u32[]{:S(2)}, u32[]{:S(2)}) collective-permute-start(bf16[56,3584]{1,0:T(8,128)(2,1)} %bitcast.286), channel_id=1, source_target_pairs={{0,448},{1,449},{2,450},{3,451},{4,452},{5,453},{6,454},{7,455},{8... | collective-permute-start | bytes 1204232 | tf_op jit(solution)/shard_map/ppermute | solution.py:125
  428.7 29.4 %collective-permute-start.18 = (bf16[2,64,56]{1,2,0:T(8,128)(2,1)S(1)}, bf16[2,64,56]{1,2,0:T(8,128)(2,1)S(1)}, u32[]{:S(2)}, u32[]{:S(2)}) collective-permute-start(bf16[2,64,56]{1,2,0:T(8,128)(2,1)S(1)} %constant_dynamic-update-slice_fusion), channel_id=1, source_target_pairs={{0,448},{1,449},{2,450},{3,451},{4,452},{5,453},{6,454},{7,455},{8... | collective-permute-start | bytes 43016 | tf_op jit(solution)/shard_map/ppermute | solution.py:126
  462.6 25.9 %all-to-all-start.11 = ((bf16[64,2,1792]{2,1,0:T(2,128)(2,1)}), bf16[64,2,1792]{2,1,0:T(2,128)(2,1)S(1)}, u32[]{:S(2)}, u32[]{:S(2)}) async-start(bf16[64,2,1792]{2,1,0:T(2,128)(2,1)} %reshape.322), calls=%async_computation.11 | async-start | bytes 917504 | tf_op jit(solution)/shard_map/all_to_all | solution.py:18
  476.6 26.7 %collective-permute-start.2 = (f32[64,56]{0,1:T(8,128)}, f32[64,56]{0,1:T(8,128)S(1)}, u32[]{:S(2)}, u32[]{:S(2)}) collective-permute-start(f32[64,56]{0,1:T(8,128)} %copy-done.26), channel_id=1, source_target_pairs={{448,384},{449,385},{450,386},{451,387},{452,388},{453,389},{454,3... | collective-permute-start | bytes 43016 | tf_op jit(solution)/shard_map/ppermute | solution.py:152
  478.5 25.5 %collective-permute-start.21 = (bf16[56,3584]{1,0:T(8,128)(2,1)}, bf16[56,3584]{1,0:T(8,128)(2,1)}, u32[]{:S(2)}, u32[]{:S(2)}) collective-permute-start(bf16[56,3584]{1,0:T(8,128)(2,1)} %convolution_convert_fusion.7), channel_id=1, source_target_pairs={{448,384},{449,385},{450,386},{451,387},{452,388},{453,389},{454,3... | collective-permute-start | bytes 1204232 | tf_op jit(solution)/shard_map/ppermute | solution.py:153
  479.9 24.8 %collective-permute-start.5 = (f32[64,56]{0,1:T(8,128)}, f32[64,56]{0,1:T(8,128)S(1)}, u32[]{:S(2)}, u32[]{:S(2)}) collective-permute-start(f32[64,56]{0,1:T(8,128)} %copy-done.27), channel_id=1, source_target_pairs={{448,320},{449,321},{450,322},{451,323},{452,324},{453,325},{454,3... | collective-permute-start | bytes 43016 | tf_op jit(solution)/shard_map/ppermute | solution.py:152
  482.5 22.9 %collective-permute-start.22 = (bf16[56,3584]{1,0:T(8,128)(2,1)}, bf16[56,3584]{1,0:T(8,128)(2,1)}, u32[]{:S(2)}, u32[]{:S(2)}) collective-permute-start(bf16[56,3584]{1,0:T(8,128)(2,1)} %convolution_convert_fusion.6), channel_id=1, source_target_pairs={{448,320},{449,321},{450,322},{451,323},{452,324},{453,325},{454,3... | collective-permute-start | bytes 1204232 | tf_op jit(solution)/shard_map/ppermute | solution.py:153
  484.1 23.8 %collective-permute-start.8 = (f32[64,56]{0,1:T(8,128)}, f32[64,56]{0,1:T(8,128)S(1)}, u32[]{:S(2)}, u32[]{:S(2)}) collective-permute-start(f32[64,56]{0,1:T(8,128)} %copy-done.28), channel_id=1, source_target_pairs={{448,256},{449,257},{450,258},{451,259},{452,260},{453,261},{454,2... | collective-permute-start | bytes 43016 | tf_op jit(solution)/shard_map/ppermute | solution.py:152
  489.5 38.6 %all-to-all-start.2 = ((bf16[8,128,448]{1,2,0:T(8,128)(2,1)}), bf16[8,128,448]{1,2,0:T(8,128)(2,1)S(1)}, u32[]{:S(2)}, u32[]{:S(2)}) async-start(bf16[8,128,448]{1,2,0:T(8,128)(2,1)} %broadcast_in_dim.131), calls=%async_computation.2 | async-start | bytes 1835008 | tf_op jit(solution)/shard_map/all_to_all | solution.py:24
  507.9 24.0 %collective-permute-start.23 = (bf16[56,3584]{1,0:T(8,128)(2,1)}, bf16[56,3584]{1,0:T(8,128)(2,1)}, u32[]{:S(2)}, u32[]{:S(2)}) collective-permute-start(bf16[56,3584]{1,0:T(8,128)(2,1)} %convolution_convert_fusion.5), channel_id=1, source_target_pairs={{448,256},{449,257},{450,258},{451,259},{452,260},{453,261},{454,2... | collective-permute-start | bytes 1204232 | tf_op jit(solution)/shard_map/ppermute | solution.py:153
  509.3 22.6 %collective-permute-start.24 = (bf16[56,3584]{1,0:T(8,128)(2,1)}, bf16[56,3584]{1,0:T(8,128)(2,1)}, u32[]{:S(2)}, u32[]{:S(2)}) collective-permute-start(bf16[56,3584]{1,0:T(8,128)(2,1)} %convolution_convert_fusion.4), channel_id=1, source_target_pairs={{448,192},{449,193},{450,194},{451,195},{452,196},{453,197},{454,1... | collective-permute-start | bytes 1204232 | tf_op jit(solution)/shard_map/ppermute | solution.py:153
  510.7 21.2 %collective-permute-start.25 = (bf16[56,3584]{1,0:T(8,128)(2,1)}, bf16[56,3584]{1,0:T(8,128)(2,1)}, u32[]{:S(2)}, u32[]{:S(2)}) collective-permute-start(bf16[56,3584]{1,0:T(8,128)(2,1)} %convolution_convert_fusion.3), channel_id=1, source_target_pairs={{448,128},{449,129},{450,130},{451,131},{452,132},{453,133},{454,1... | collective-permute-start | bytes 1204232 | tf_op jit(solution)/shard_map/ppermute | solution.py:153
  512.1 19.8 %collective-permute-start.26 = (bf16[56,3584]{1,0:T(8,128)(2,1)}, bf16[56,3584]{1,0:T(8,128)(2,1)}, u32[]{:S(2)}, u32[]{:S(2)}) collective-permute-start(bf16[56,3584]{1,0:T(8,128)(2,1)} %convolution_convert_fusion.2), channel_id=1, source_target_pairs={{448,64},{449,65},{450,66},{451,67},{452,68},{453,69},{454,70},{45... | collective-permute-start | bytes 1204232 | tf_op jit(solution)/shard_map/ppermute | solution.py:153
  520.6 39.5 %collective-permute-start.27 = (bf16[56,3584]{1,0:T(8,128)(2,1)}, bf16[56,3584]{1,0:T(8,128)(2,1)}, u32[]{:S(2)}, u32[]{:S(2)}) collective-permute-start(bf16[56,3584]{1,0:T(8,128)(2,1)} %convolution_convert_fusion.1), channel_id=1, source_target_pairs={{448,0},{449,1},{450,2},{451,3},{452,4},{453,5},{454,6},{455,7},{4... | collective-permute-start | bytes 1204232 | tf_op jit(solution)/shard_map/ppermute | solution.py:153
  (48 other events, 910.8 us)

commit v2 on v1

--- a/solution.py
+++ b/solution.py
@@ -99,7 +99,21 @@
     incoming_terms = lax.all_to_all(
         term_pieces, ("section", "dp"), split_axis=0, concat_axis=0, tiled=True
     )
-    incoming_terms, carry_start = lax.optimization_barrier((incoming_terms, micro_cols))
+    last_section = section_count - 1
+    packed = jnp.concatenate(
+        [
+            section_weights[0].reshape(col_width, dp_count, col_width),
+            pre_acts[0][None],
+        ]
+    )
+    moved = tuple(
+        lax.ppermute(packed, "section", [(source, last_section)]) for source in range(last_section)
+    )
+    incoming_terms, carry_start, moved = lax.optimization_barrier(
+        (incoming_terms, micro_cols, moved)
+    )
+    packed_of = dict(enumerate(moved))
+    packed_of[last_section] = packed
     every_slot = incoming_terms[:, 0, :, chunk].astype(jnp.int32)
     onehot = (every_slot[:, :, None] == jnp.arange(block_total, dtype=jnp.int32)).astype(
         jnp.bfloat16
@@ -114,45 +128,34 @@
     passage_out = gathered_columns(dense.reshape(stripe * block_total, chunk), "section")
     passage_out = passage_out.reshape(stripe, block_total, width)
     entry = lax.all_to_all(carry_start, "dp", split_axis=0, concat_axis=1, tiled=True)
-    section_count = lax.axis_size("section")
     section_index = lax.axis_index("section")
     last = section_count - 1
-    own_rows = section_weights[0]
-    own_cols = jnp.stack([pre_acts[0], section_inputs[0]])
-    rows_of = {last: own_rows}
-    cols_of = {last: own_cols}
-    for source in range(last):
-        rows_of[source] = lax.ppermute(own_rows, "section", [(source, last)])
-        cols_of[source] = lax.ppermute(own_cols, "section", [(source, last)])
     carry = entry.reshape(dp_count * micro_count, col_width)
-    grads_of = {}
-    weights_of = {}
+    sent_of = {}
     for source in range(last, -1, -1):
-        pre = cols_of[source][0].astype(jnp.float32)
+        rows = packed_of[source][:col_width]
+        pre = packed_of[source][col_width].astype(jnp.float32)
         sigma = jax.nn.sigmoid(pre)
         slope = sigma * (1.0 + pre * (1.0 - sigma))
         inner = (carry * slope).astype(jnp.bfloat16)
         piece = gathered_pieces(inner, "dp")
-        split_rows = rows_of[source].reshape(col_width, dp_count, col_width)
-        back_sum = jnp.einsum(
-            "dmj,idj->mi", piece, split_rows, preferred_element_type=jnp.float32
-        )
-        weights_of[source] = (
-            jnp.einsum(
-                "mi,dmj->idj", cols_of[source][1], piece, preferred_element_type=jnp.float32
-            )
-            .reshape(col_width, width)
-            .astype(jnp.bfloat16)
-        )
+        back_sum = jnp.einsum("dmj,idj->mi", piece, rows, preferred_element_type=jnp.float32)
         carry = carry + back_sum
-        grads_of[source] = carry
-    grad_cols = grads_of[last]
-    grad_weight = weights_of[last]
+        if source == last:
+            grad_cols, home_inner = carry, inner
+        else:
+            both = jnp.stack([carry, inner.astype(jnp.float32)])
+            sent_of[source] = lax.ppermute(both, "section", [(last, source)])
     for source in range(last):
-        sent_grads = lax.ppermute(grads_of[source], "section", [(last, source)])
-        sent_weights = lax.ppermute(weights_of[source], "section", [(last, source)])
-        grad_cols = jnp.where(section_index == source, sent_grads, grad_cols)
-        grad_weight = jnp.where(section_index == source, sent_weights, grad_weight)
+        here = section_index == source
+        grad_cols = jnp.where(here, sent_of[source][0], grad_cols)
+        home_inner = jnp.where(here, sent_of[source][1].astype(jnp.bfloat16), home_inner)
+    home_piece = gathered_pieces(home_inner, "dp")
+    grad_weight = (
+        jnp.einsum("mi,dmj->idj", section_inputs[0], home_piece, preferred_element_type=jnp.float32)
+        .reshape(col_width, width)
+        .astype(jnp.bfloat16)
+    )
     return (
         query_sums.reshape(blocks_here * row_block_count, width).astype(jnp.bfloat16),
         passage_out,

time: 573 us -> 612 us (1.068)
  blocking collectives: 0 us -> 41.1 us
  waiting for transfers between devices: 257 us -> 282 us
  starting transfers between devices: 165 us -> 146 us
  matrix products: 43.8 us -> 26.7 us
    ppermute x28 -> x14, waiting for transfers between devices: 48.4 us -> 136 us  [the longest x7 119 us: body(): lax.ppermute(packed, 'section', [(source, last_section)])]
    all_to_all x1, waiting for transfers between devices: 69 us -> 0.01 us  [body(): lax.all_to_all(term_pieces, ('section', 'dp'), split_axis=0, concat_axis=...]
    all_to_all x0 -> x2, blocking collectives: none -> 41.1 us  [the longest x1 21.1 us: gathered_pieces(): return lax.all_to_all(copies, axis, 0, 0, tiled=True)]
    ppermute x28 -> x14, starting transfers between devices: 61.6 us -> 21.8 us  [the longest x7 13.5 us: body(): lax.ppermute(packed, 'section', [(source, last_section)])]
    all_to_all x1, starting transfers between devices: 5 us -> 37.7 us  [gathered_columns(): pieces = lax.all_to_all(copies, axis, 0, 0, tiled=True)]
    slice x0 -> x14, local copies, waits for them, and re-layouts: none -> 22.6 us  [body(): rows = packed_of[source][:col_width]]
    reshape x7 -> x0, local copies, waits for them, and re-layouts: 19.6 us -> none  [body(): split_rows = rows_of[source].reshape(col_width, dp_count, col_width)]
    dot_general x16 -> x9, matrix products: 30.6 us -> 13.4 us  [the longest x8 12.4 us: body(): jnp.einsum('dmj,idj->mi', piece, rows, preferred_element_type=jnp.float32)]
  transfers between devices with their start and end apart: 40 -> 25, of which waited for: 13 -> 11; matrix products, arithmetic and copies ran while one was open for 12% -> 9% of each run, Pallas kernels for 0% -> 0%
where the time goes in v2:
time: 612 us; the launch traced here: 600 us
  waiting for transfers between devices  282 us (46%)
  starting transfers between devices  146 us (24%)
  local copies, waits for them, and re-layouts  94.4 us (15%)
  blocking collectives  41.1 us (7%)
  matrix products  26.7 us (4%)
  other arithmetic  7.1 us (1%)
    ppermute x7, waiting for transfers between devices, body(): lax.ppermute(packed, 'section', [(source, last_section)])  119 us
    all_to_all x8, waiting for transfers between devices, gathered_pieces(): return lax.all_to_all(copies, axis, 0, 0, tiled=True)  85.6 us
    all_to_all x1, waiting for transfers between devices, body(): lax.all_to_all(outgoing, 'dp', split_axis=1, concat_axis=0, tiled=True)  60.9 us
    all_to_all x8, starting transfers between devices, gathered_pieces(): return lax.all_to_all(copies, axis, 0, 0, tiled=True)  55.6 us
    all_to_all x1, starting transfers between devices, gathered_columns(): pieces = lax.all_to_all(copies, axis, 0, 0, tiled=True)  37.7 us
    slice x14, local copies, waits for them, and re-layouts, body(): rows = packed_of[source][:col_width]  22.6 us
    all_to_all x1, blocking collectives, gathered_pieces(): return lax.all_to_all(copies, axis, 0, 0, tiled=True)  21.1 us
    all_to_all x1, blocking collectives, body(): lax.all_to_all(carry_start, 'dp', split_axis=0, concat_axis=1, tiled=True)  20 us
  transfers between devices with their start and end apart: 25, of which 11 were waited for; matrix products, arithmetic and copies ran while one was open for 9% of the time, Pallas kernels for 0%

profile of v2, /device:TPU:6, one launch (start us, length us, event | category | flops | bytes accessed | tf_op | source)
XLA Modules:
  0.0 599.9 jit_solution(9847557009770879357)
XLA Ops:
  8.1 14.3 %all-to-all-start = ((bf16[2,192,3584]{2,0,1:T(2,128)(2,1)}), bf16[2,192,3584]{2,0,1:T(2,128)(2,1)}, u32[]{:S(2)}, u32[]{:S(2)}) async-start(bf16[2,192,3584]{2,0,1:T(2,128)(2,1)} %copy.128), calls=%async_computation | async-start | bytes 5505024 | tf_op jit(solution)/shard_map/all_to_all | solution.py:50
  24.3 60.9 %all-to-all-done = bf16[2,192,3584]{2,0,1:T(2,128)(2,1)} async-done(((bf16[2,192,3584]{2,0,1:T(2,128)(2,1)}), bf16[2,192,3584]{2,0,1:T(2,128)(2,1)}, u32[]{:S(2)}, u32[]{:S(2)}) %all-to-all-start) | async-done | bytes 2752544 | tf_op jit(solution)/shard_map/all_to_all | solution.py:50
  118.6 17.0 %all-to-all-start.1 = ((bf16[512,2,3,449]{3,1,2,0:T(2,128)(2,1)}), bf16[512,2,3,449]{3,1,2,0:T(2,128)(2,1)}, u32[]{:S(2)}, u32[]{:S(2)}) async-start(bf16[512,2,3,449]{3,1,2,0:T(2,128)(2,1)} %copy.133), calls=%async_computation.1 | async-start | bytes 6291456 | tf_op jit(solution)/shard_map/all_to_all | solution.py:99
  148.7 119.4 %collective-permute-done = bf16[57,64,56]{1,2,0:T(8,128)(2,1)S(1)} collective-permute-done((bf16[57,64,56]{1,2,0:T(8,128)(2,1)S(1)}, bf16[57,64,56]{1,2,0:T(8,128)(2,1)S(1)}, u32[]{:S(2)}, u32[]{:S(2)}) %collective-permute-start) | collective-permute-done | bytes 408608 | tf_op jit(solution)/shard_map/ppermute | solution.py:110
  275.6 20.0 %all_to_all.79 = f32[64,1,56]{2,1,0:T(1,128)S(1)} all-to-all(f32[64,1,56]{2,1,0:T(1,128)S(1)} %bitcast.302), channel_id=1, replica_groups=mesh['section'=8,'dp'=64] {'dp'}, dimensions={0} | all-to-all | bytes 28672 | tf_op jit(solution)/shard_map/all_to_all | solution.py:130
  297.1 21.1 %all_to_all.80 = bf16[64,2,1792]{2,1,0:T(2,128)(2,1)S(1)} all-to-all(bf16[64,2,1792]{2,1,0:T(2,128)(2,1)S(1)} %reshape.284), channel_id=1, replica_groups=mesh['section'=8,'dp'=64] {'dp'}, dimensions={0} | all-to-all | bytes 917504 | tf_op jit(solution)/shard_map/all_to_all | solution.py:18
  322.4 6.8 %all-to-all-start.5 = ((bf16[64,2,1792]{2,1,0:T(2,128)(2,1)}), bf16[64,2,1792]{2,1,0:T(2,128)(2,1)S(1)}, u32[]{:S(2)}, u32[]{:S(2)}) async-start(bf16[64,2,1792]{2,1,0:T(2,128)(2,1)} %reshape.286), calls=%async_computation.5 | async-start | bytes 917504 | tf_op jit(solution)/shard_map/all_to_all | solution.py:18
  332.6 12.0 %all-to-all-done.5 = bf16[64,2,1792]{2,1,0:T(2,128)(2,1)S(1)} async-done(((bf16[64,2,1792]{2,1,0:T(2,128)(2,1)}), bf16[64,2,1792]{2,1,0:T(2,128)(2,1)S(1)}, u32[]{:S(2)}, u32[]{:S(2)}) %all-to-all-start.5) | async-done | bytes 458784 | tf_op jit(solution)/shard_map/all_to_all | solution.py:18
  348.4 6.8 %all-to-all-start.6 = ((bf16[64,2,1792]{2,1,0:T(2,128)(2,1)}), bf16[64,2,1792]{2,1,0:T(2,128)(2,1)S(1)}, u32[]{:S(2)}, u32[]{:S(2)}) async-start(bf16[64,2,1792]{2,1,0:T(2,128)(2,1)} %reshape.288), calls=%async_computation.6 | async-start | bytes 917504 | tf_op jit(solution)/shard_map/all_to_all | solution.py:18
  358.6 12.0 %all-to-all-done.6 = bf16[64,2,1792]{2,1,0:T(2,128)(2,1)S(1)} async-done(((bf16[64,2,1792]{2,1,0:T(2,128)(2,1)}), bf16[64,2,1792]{2,1,0:T(2,128)(2,1)S(1)}, u32[]{:S(2)}, u32[]{:S(2)}) %all-to-all-start.6) | async-done | bytes 458784 | tf_op jit(solution)/shard_map/all_to_all | solution.py:18
  374.4 6.8 %all-to-all-start.7 = ((bf16[64,2,1792]{2,1,0:T(2,128)(2,1)}), bf16[64,2,1792]{2,1,0:T(2,128)(2,1)S(1)}, u32[]{:S(2)}, u32[]{:S(2)}) async-start(bf16[64,2,1792]{2,1,0:T(2,128)(2,1)} %reshape.290), calls=%async_computation.7 | async-start | bytes 917504 | tf_op jit(solution)/shard_map/all_to_all | solution.py:18
  384.6 12.0 %all-to-all-done.7 = bf16[64,2,1792]{2,1,0:T(2,128)(2,1)S(1)} async-done(((bf16[64,2,1792]{2,1,0:T(2,128)(2,1)}), bf16[64,2,1792]{2,1,0:T(2,128)(2,1)S(1)}, u32[]{:S(2)}, u32[]{:S(2)}) %all-to-all-start.7) | async-done | bytes 458784 | tf_op jit(solution)/shard_map/all_to_all | solution.py:18
  400.3 6.8 %all-to-all-start.8 = ((bf16[64,2,1792]{2,1,0:T(2,128)(2,1)}), bf16[64,2,1792]{2,1,0:T(2,128)(2,1)S(1)}, u32[]{:S(2)}, u32[]{:S(2)}) async-start(bf16[64,2,1792]{2,1,0:T(2,128)(2,1)} %reshape.292), calls=%async_computation.8 | async-start | bytes 917504 | tf_op jit(solution)/shard_map/all_to_all | solution.py:18
  410.5 12.0 %all-to-all-done.8 = bf16[64,2,1792]{2,1,0:T(2,128)(2,1)S(1)} async-done(((bf16[64,2,1792]{2,1,0:T(2,128)(2,1)}), bf16[64,2,1792]{2,1,0:T(2,128)(2,1)S(1)}, u32[]{:S(2)}, u32[]{:S(2)}) %all-to-all-start.8) | async-done | bytes 458784 | tf_op jit(solution)/shard_map/all_to_all | solution.py:18
  426.3 6.8 %all-to-all-start.9 = ((bf16[64,2,1792]{2,1,0:T(2,128)(2,1)}), bf16[64,2,1792]{2,1,0:T(2,128)(2,1)S(1)}, u32[]{:S(2)}, u32[]{:S(2)}) async-start(bf16[64,2,1792]{2,1,0:T(2,128)(2,1)} %reshape.294), calls=%async_computation.9 | async-start | bytes 917504 | tf_op jit(solution)/shard_map/all_to_all | solution.py:18
  436.5 12.0 %all-to-all-done.9 = bf16[64,2,1792]{2,1,0:T(2,128)(2,1)S(1)} async-done(((bf16[64,2,1792]{2,1,0:T(2,128)(2,1)}), bf16[64,2,1792]{2,1,0:T(2,128)(2,1)S(1)}, u32[]{:S(2)}, u32[]{:S(2)}) %all-to-all-start.9) | async-done | bytes 458784 | tf_op jit(solution)/shard_map/all_to_all | solution.py:18
  452.3 7.1 %all-to-all-start.10 = ((bf16[64,2,1792]{2,1,0:T(2,128)(2,1)}), bf16[64,2,1792]{2,1,0:T(2,128)(2,1)S(1)}, u32[]{:S(2)}, u32[]{:S(2)}) async-start(bf16[64,2,1792]{2,1,0:T(2,128)(2,1)} %reshape.296), calls=%async_computation.10 | async-start | bytes 917504 | tf_op jit(solution)/shard_map/all_to_all | solution.py:18
  462.8 11.9 %all-to-all-done.10 = bf16[64,2,1792]{2,1,0:T(2,128)(2,1)S(1)} async-done(((bf16[64,2,1792]{2,1,0:T(2,128)(2,1)}), bf16[64,2,1792]{2,1,0:T(2,128)(2,1)S(1)}, u32[]{:S(2)}, u32[]{:S(2)}) %all-to-all-start.10) | async-done | bytes 458784 | tf_op jit(solution)/shard_map/all_to_all | solution.py:18
  477.7 6.8 %all-to-all-start.11 = ((bf16[64,2,1792]{2,1,0:T(2,128)(2,1)}), bf16[64,2,1792]{2,1,0:T(2,128)(2,1)S(1)}, u32[]{:S(2)}, u32[]{:S(2)}) async-start(bf16[64,2,1792]{2,1,0:T(2,128)(2,1)} %reshape.298), calls=%async_computation.11 | async-start | bytes 917504 | tf_op jit(solution)/shard_map/all_to_all | solution.py:18
  484.5 8.7 %copy.135 = bf16[512,2,3,449]{0,3,2,1:T(8,128)(2,1)} copy(bf16[512,2,3,449]{3,1,2,0:T(2,128)(2,1)} %all-to-all-done.1) | data formatting | bytes 5517312 | tf_op jit(solution)/shard_map/optimization_barrier | solution.py:112
  501.0 37.7 %all-to-all-start.2 = ((bf16[8,128,448]{1,2,0:T(8,128)(2,1)}), bf16[8,128,448]{1,2,0:T(8,128)(2,1)S(1)}, u32[]{:S(2)}, u32[]{:S(2)}) async-start(bf16[8,128,448]{1,2,0:T(8,128)(2,1)} %broadcast_in_dim.137), calls=%async_computation.2 | async-start | bytes 1835008 | tf_op jit(solution)/shard_map/all_to_all | solution.py:24
  552.4 16.5 %collective-permute-done.13 = f32[2,64,56]{1,2,0:T(8,128)S(1)} collective-permute-done((f32[2,64,56]{1,2,0:T(8,128)S(1)}, f32[2,64,56]{1,2,0:T(8,128)S(1)}, u32[]{:S(2)}, u32[]{:S(2)}) %collective-permute-start.13) | collective-permute-done | bytes 28704 | tf_op jit(solution)/shard_map/ppermute | solution.py:148
  571.2 7.7 %all-to-all-start.12 = ((bf16[64,2,1792]{2,1,0:T(2,128)(2,1)}), bf16[64,2,1792]{2,1,0:T(2,128)(2,1)S(1)}, u32[]{:S(2)}, u32[]{:S(2)}) async-start(bf16[64,2,1792]{2,1,0:T(2,128)(2,1)} %reshape.300), calls=%async_computation.12 | async-start | bytes 917504 | tf_op jit(solution)/shard_map/all_to_all | solution.py:18
  583.7 10.6 %all-to-all-done.12 = bf16[64,2,1792]{2,1,0:T(2,128)(2,1)S(1)} async-done(((bf16[64,2,1792]{2,1,0:T(2,128)(2,1)}), bf16[64,2,1792]{2,1,0:T(2,128)(2,1)S(1)}, u32[]{:S(2)}, u32[]{:S(2)}) %all-to-all-start.12) | async-done | bytes 458784 | tf_op jit(solution)/shard_map/all_to_all | solution.py:18
  (181 shorter events, 144.6 us)
Async XLA Ops:
  8.1 77.0 %all-to-all-start = ((bf16[2,192,3584]{2,0,1:T(2,128)(2,1)}), bf16[2,192,3584]{2,0,1:T(2,128)(2,1)}, u32[]{:S(2)}, u32[]{:S(2)}) async-start(bf16[2,192,3584]{2,0,1:T(2,128)(2,1)} %copy.128), calls=%async_computation | async-start | bytes 5505024 | tf_op jit(solution)/shard_map/all_to_all | solution.py:50
  118.6 157.0 %all-to-all-start.1 = ((bf16[512,2,3,449]{3,1,2,0:T(2,128)(2,1)}), bf16[512,2,3,449]{3,1,2,0:T(2,128)(2,1)}, u32[]{:S(2)}, u32[]{:S(2)}) async-start(bf16[512,2,3,449]{3,1,2,0:T(2,128)(2,1)} %copy.133), calls=%async_computation.1 | async-start | bytes 6291456 | tf_op jit(solution)/shard_map/all_to_all | solution.py:99
  138.3 129.8 %collective-permute-start = (bf16[57,64,56]{1,2,0:T(8,128)(2,1)S(1)}, bf16[57,64,56]{1,2,0:T(8,128)(2,1)S(1)}, u32[]{:S(2)}, u32[]{:S(2)}) collective-permute-start(bf16[57,64,56]{1,2,0:T(8,128)(2,1)S(1)} %pad_maximum_fusion.1), channel_id=1, source_target_pairs={{0,448},{1,449},{2,450},{3,451},{4,452},{5,453},{6,454},{7,455},{8... | collective-permute-start | bytes 1225736 | tf_op jit(solution)/shard_map/ppermute | solution.py:110
  143.3 126.4 %collective-permute-start.1 = (bf16[57,64,56]{1,2,0:T(8,128)(2,1)S(1)}, bf16[57,64,56]{1,2,0:T(8,128)(2,1)S(1)}, u32[]{:S(2)}, u32[]{:S(2)}) collective-permute-start(bf16[57,64,56]{1,2,0:T(8,128)(2,1)S(1)} %pad_maximum_fusion.1), channel_id=1, source_target_pairs={{64,448},{65,449},{66,450},{67,451},{68,452},{69,453},{70,454},{71... | collective-permute-start | bytes 1225736 | tf_op jit(solution)/shard_map/ppermute | solution.py:110
  144.0 131.6 %collective-permute-start.2 = (bf16[57,64,56]{1,2,0:T(8,128)(2,1)S(1)}, bf16[57,64,56]{1,2,0:T(8,128)(2,1)}, u32[]{:S(2)}, u32[]{:S(2)}) collective-permute-start(bf16[57,64,56]{1,2,0:T(8,128)(2,1)S(1)} %pad_maximum_fusion.1), channel_id=1, source_target_pairs={{128,448},{129,449},{130,450},{131,451},{132,452},{133,453},{134,4... | collective-permute-start | bytes 1225736 | tf_op jit(solution)/shard_map/ppermute | solution.py:110
  145.6 130.0 %collective-permute-start.3 = (bf16[57,64,56]{1,2,0:T(8,128)(2,1)S(1)}, bf16[57,64,56]{1,2,0:T(8,128)(2,1)}, u32[]{:S(2)}, u32[]{:S(2)}) collective-permute-start(bf16[57,64,56]{1,2,0:T(8,128)(2,1)S(1)} %pad_maximum_fusion.1), channel_id=1, source_target_pairs={{192,448},{193,449},{194,450},{195,451},{196,452},{197,453},{198,4... | collective-permute-start | bytes 1225736 | tf_op jit(solution)/shard_map/ppermute | solution.py:110
  147.1 128.5 %collective-permute-start.4 = (bf16[57,64,56]{1,2,0:T(8,128)(2,1)S(1)}, bf16[57,64,56]{1,2,0:T(8,128)(2,1)}, u32[]{:S(2)}, u32[]{:S(2)}) collective-permute-start(bf16[57,64,56]{1,2,0:T(8,128)(2,1)S(1)} %pad_maximum_fusion.1), channel_id=1, source_target_pairs={{256,448},{257,449},{258,450},{259,451},{260,452},{261,453},{262,4... | collective-permute-start | bytes 1225736 | tf_op jit(solution)/shard_map/ppermute | solution.py:110
  268.1 7.5 %collective-permute-start.5 = (bf16[57,64,56]{1,2,0:T(8,128)(2,1)S(1)}, bf16[57,64,56]{1,2,0:T(8,128)(2,1)}, u32[]{:S(2)}, u32[]{:S(2)}) collective-permute-start(bf16[57,64,56]{1,2,0:T(8,128)(2,1)S(1)} %pad_maximum_fusion.1), channel_id=1, source_target_pairs={{320,448},{321,449},{322,450},{323,451},{324,452},{325,453},{326,4... | collective-permute-start | bytes 1225736 | tf_op jit(solution)/shard_map/ppermute | solution.py:110
  270.5 5.1 collective-permute-start.6
  322.4 22.2 %all-to-all-start.5 = ((bf16[64,2,1792]{2,1,0:T(2,128)(2,1)}), bf16[64,2,1792]{2,1,0:T(2,128)(2,1)S(1)}, u32[]{:S(2)}, u32[]{:S(2)}) async-start(bf16[64,2,1792]{2,1,0:T(2,128)(2,1)} %reshape.286), calls=%async_computation.5 | async-start | bytes 917504 | tf_op jit(solution)/shard_map/all_to_all | solution.py:18
  348.4 22.2 %all-to-all-start.6 = ((bf16[64,2,1792]{2,1,0:T(2,128)(2,1)}), bf16[64,2,1792]{2,1,0:T(2,128)(2,1)S(1)}, u32[]{:S(2)}, u32[]{:S(2)}) async-start(bf16[64,2,1792]{2,1,0:T(2,128)(2,1)} %reshape.288), calls=%async_computation.6 | async-start | bytes 917504 | tf_op jit(solution)/shard_map/all_to_all | solution.py:18
  374.4 22.2 %all-to-all-start.7 = ((bf16[64,2,1792]{2,1,0:T(2,128)(2,1)}), bf16[64,2,1792]{2,1,0:T(2,128)(2,1)S(1)}, u32[]{:S(2)}, u32[]{:S(2)}) async-start(bf16[64,2,1792]{2,1,0:T(2,128)(2,1)} %reshape.290), calls=%async_computation.7 | async-start | bytes 917504 | tf_op jit(solution)/shard_map/all_to_all | solution.py:18
  400.3 22.2 %all-to-all-start.8 = ((bf16[64,2,1792]{2,1,0:T(2,128)(2,1)}), bf16[64,2,1792]{2,1,0:T(2,128)(2,1)S(1)}, u32[]{:S(2)}, u32[]{:S(2)}) async-start(bf16[64,2,1792]{2,1,0:T(2,128)(2,1)} %reshape.292), calls=%async_computation.8 | async-start | bytes 917504 | tf_op jit(solution)/shard_map/all_to_all | solution.py:18
  426.3 22.2 %all-to-all-start.9 = ((bf16[64,2,1792]{2,1,0:T(2,128)(2,1)}), bf16[64,2,1792]{2,1,0:T(2,128)(2,1)S(1)}, u32[]{:S(2)}, u32[]{:S(2)}) async-start(bf16[64,2,1792]{2,1,0:T(2,128)(2,1)} %reshape.294), calls=%async_computation.9 | async-start | bytes 917504 | tf_op jit(solution)/shard_map/all_to_all | solution.py:18
  452.3 22.4 %all-to-all-start.10 = ((bf16[64,2,1792]{2,1,0:T(2,128)(2,1)}), bf16[64,2,1792]{2,1,0:T(2,128)(2,1)S(1)}, u32[]{:S(2)}, u32[]{:S(2)}) async-start(bf16[64,2,1792]{2,1,0:T(2,128)(2,1)} %reshape.296), calls=%async_computation.10 | async-start | bytes 917504 | tf_op jit(solution)/shard_map/all_to_all | solution.py:18
  477.7 22.2 %all-to-all-start.11 = ((bf16[64,2,1792]{2,1,0:T(2,128)(2,1)}), bf16[64,2,1792]{2,1,0:T(2,128)(2,1)S(1)}, u32[]{:S(2)}, u32[]{:S(2)}) async-start(bf16[64,2,1792]{2,1,0:T(2,128)(2,1)} %reshape.298), calls=%async_computation.11 | async-start | bytes 917504 | tf_op jit(solution)/shard_map/all_to_all | solution.py:18
  501.0 70.2 %all-to-all-start.2 = ((bf16[8,128,448]{1,2,0:T(8,128)(2,1)}), bf16[8,128,448]{1,2,0:T(8,128)(2,1)S(1)}, u32[]{:S(2)}, u32[]{:S(2)}) async-start(bf16[8,128,448]{1,2,0:T(8,128)(2,1)} %broadcast_in_dim.137), calls=%async_computation.2 | async-start | bytes 1835008 | tf_op jit(solution)/shard_map/all_to_all | solution.py:24
  541.6 8.7 %collective-permute-start.7 = (f32[2,64,56]{1,2,0:T(8,128)}, f32[2,64,56]{1,2,0:T(8,128)}, u32[]{:S(2)}, u32[]{:S(2)}) collective-permute-start(f32[2,64,56]{1,2,0:T(8,128)} %pad_maximum_fusion.2), channel_id=1, source_target_pairs={{448,384},{449,385},{450,386},{451,387},{452,388},{453,389},{454,3... | collective-permute-start | bytes 86024 | tf_op jit(solution)/shard_map/ppermute | solution.py:148
  543.5 7.5 %collective-permute-start.8 = (f32[2,64,56]{1,2,0:T(8,128)}, f32[2,64,56]{1,2,0:T(8,128)}, u32[]{:S(2)}, u32[]{:S(2)}) collective-permute-start(f32[2,64,56]{1,2,0:T(8,128)} %pad_maximum_fusion.3), channel_id=1, source_target_pairs={{448,320},{449,321},{450,322},{451,323},{452,324},{453,325},{454,3... | collective-permute-start | bytes 86024 | tf_op jit(solution)/shard_map/ppermute | solution.py:148
  544.8 7.5 %collective-permute-start.9 = (f32[2,64,56]{1,2,0:T(8,128)S(1)}, f32[2,64,56]{1,2,0:T(8,128)}, u32[]{:S(2)}, u32[]{:S(2)}) collective-permute-start(f32[2,64,56]{1,2,0:T(8,128)S(1)} %pad_maximum_fusion.4), channel_id=1, source_target_pairs={{448,256},{449,257},{450,258},{451,259},{452,260},{453,261},{454,2... | collective-permute-start | bytes 86024 | tf_op jit(solution)/shard_map/ppermute | solution.py:148
  546.1 6.3 %collective-permute-start.10 = (f32[2,64,56]{1,2,0:T(8,128)S(1)}, f32[2,64,56]{1,2,0:T(8,128)}, u32[]{:S(2)}, u32[]{:S(2)}) collective-permute-start(f32[2,64,56]{1,2,0:T(8,128)S(1)} %pad_maximum_fusion.5), channel_id=1, source_target_pairs={{448,192},{449,193},{450,194},{451,195},{452,196},{453,197},{454,1... | collective-permute-start | bytes 86024 | tf_op jit(solution)/shard_map/ppermute | solution.py:148
  547.4 5.0 collective-permute-start.11
  551.0 17.9 %collective-permute-start.13 = (f32[2,64,56]{1,2,0:T(8,128)S(1)}, f32[2,64,56]{1,2,0:T(8,128)S(1)}, u32[]{:S(2)}, u32[]{:S(2)}) collective-permute-start(f32[2,64,56]{1,2,0:T(8,128)S(1)} %pad_maximum_fusion.8), channel_id=1, source_target_pairs={{448,0},{449,1},{450,2},{451,3},{452,4},{453,5},{454,6},{455,7},{4... | collective-permute-start | bytes 86024 | tf_op jit(solution)/shard_map/ppermute | solution.py:148
  571.2 23.0 %all-to-all-start.12 = ((bf16[64,2,1792]{2,1,0:T(2,128)(2,1)}), bf16[64,2,1792]{2,1,0:T(2,128)(2,1)S(1)}, u32[]{:S(2)}, u32[]{:S(2)}) async-start(bf16[64,2,1792]{2,1,0:T(2,128)(2,1)} %reshape.300), calls=%async_computation.12 | async-start | bytes 917504 | tf_op jit(solution)/shard_map/all_to_all | solution.py:18
  (28 other events, 964.2 us)

commit v3 on v2

--- a/solution.py
+++ b/solution.py
@@ -47,7 +47,22 @@
     outgoing = jnp.einsum(
         "rpj,sp->rsj", passages, chooser, preferred_element_type=jnp.float32
     ).astype(passages.dtype)
+    col_width = width // dp_count
+    section_count = lax.axis_size("section")
+    last_section = section_count - 1
+    packed = jnp.concatenate(
+        [
+            section_weights[0].reshape(col_width, dp_count, col_width),
+            pre_acts[0][None],
+        ]
+    )
+    moved = tuple(
+        lax.ppermute(packed, "section", [(source, last_section)]) for source in range(last_section)
+    )
     pulled_rows = lax.all_to_all(outgoing, "dp", split_axis=1, concat_axis=0, tiled=True)
+    pulled_rows, moved = lax.optimization_barrier((pulled_rows, moved))
+    packed_of = dict(enumerate(moved))
+    packed_of[last_section] = packed
     pulled_rows = pulled_rows.reshape(row_block_count, blocks_here, slot_count, width)
     own_counts = lax.dynamic_slice_in_dim(counts, dp_index * blocks_here, blocks_here)
     slot_valid = jnp.arange(slot_count, dtype=jnp.int32)[None, :] < own_counts[:, None]
@@ -81,7 +96,6 @@
     )
     block_terms = passage_sums.reshape(row_block_count, requests, width).astype(jnp.bfloat16)
     micro_count = section_inputs.shape[1] // dp_count
-    col_width = width // dp_count
     micro_cols = jnp.transpose(
         query_sums[0, :micro_count].reshape(micro_count, dp_count, col_width), (1, 0, 2)
     )
@@ -96,38 +110,7 @@
         (section_count * dp_count, stripe, requests, 1),
     )
     term_pieces = jnp.concatenate([term_pieces, slot_tags], axis=3)
-    incoming_terms = lax.all_to_all(
-        term_pieces, ("section", "dp"), split_axis=0, concat_axis=0, tiled=True
-    )
-    last_section = section_count - 1
-    packed = jnp.concatenate(
-        [
-            section_weights[0].reshape(col_width, dp_count, col_width),
-            pre_acts[0][None],
-        ]
-    )
-    moved = tuple(
-        lax.ppermute(packed, "section", [(source, last_section)]) for source in range(last_section)
-    )
-    incoming_terms, carry_start, moved = lax.optimization_barrier(
-        (incoming_terms, micro_cols, moved)
-    )
-    packed_of = dict(enumerate(moved))
-    packed_of[last_section] = packed
-    every_slot = incoming_terms[:, 0, :, chunk].astype(jnp.int32)
-    onehot = (every_slot[:, :, None] == jnp.arange(block_total, dtype=jnp.int32)).astype(
-        jnp.bfloat16
-    )
-    dense = jnp.einsum(
-        "qsfc,qfn->snc",
-        incoming_terms[:, :, :, :chunk],
-        onehot,
-        preferred_element_type=jnp.float32,
-    )
-    dense = dense.reshape(stripe, block_total, chunk).astype(jnp.bfloat16)
-    passage_out = gathered_columns(dense.reshape(stripe * block_total, chunk), "section")
-    passage_out = passage_out.reshape(stripe, block_total, width)
-    entry = lax.all_to_all(carry_start, "dp", split_axis=0, concat_axis=1, tiled=True)
+    entry = lax.all_to_all(micro_cols, "dp", split_axis=0, concat_axis=1, tiled=True)
     section_index = lax.axis_index("section")
     last = section_count - 1
     carry = entry.reshape(dp_count * micro_count, col_width)
@@ -150,6 +133,23 @@
         here = section_index == source
         grad_cols = jnp.where(here, sent_of[source][0], grad_cols)
         home_inner = jnp.where(here, sent_of[source][1].astype(jnp.bfloat16), home_inner)
+    term_pieces, carry = lax.optimization_barrier((term_pieces, carry))
+    incoming_terms = lax.all_to_all(
+        term_pieces, ("section", "dp"), split_axis=0, concat_axis=0, tiled=True
+    )
+    every_slot = incoming_terms[:, 0, :, chunk].astype(jnp.int32)
+    onehot = (every_slot[:, :, None] == jnp.arange(block_total, dtype=jnp.int32)).astype(
+        jnp.bfloat16
+    )
+    dense = jnp.einsum(
+        "qsfc,qfn->snc",
+        incoming_terms[:, :, :, :chunk],
+        onehot,
+        preferred_element_type=jnp.float32,
+    )
+    dense = dense.reshape(stripe, block_total, chunk).astype(jnp.bfloat16)
+    passage_out = gathered_columns(dense.reshape(stripe * block_total, chunk), "section")
+    passage_out = passage_out.reshape(stripe, block_total, width)
     home_piece = gathered_pieces(home_inner, "dp")
     grad_weight = (
         jnp.einsum("mi,dmj->idj", section_inputs[0], home_piece, preferred_element_type=jnp.float32)

time: 612 us -> 548 us (0.90)
  waiting for transfers between devices: 282 us -> 230 us
  starting transfers between devices: 146 us -> 139 us
    all_to_all x1, waiting for transfers between devices: 60.9 us -> 0.01 us  [body(): lax.all_to_all(outgoing, 'dp', split_axis=1, concat_axis=0, tiled=True)]
    ppermute x7, waiting for transfers between devices: 119 us -> 62.2 us  [body(): lax.ppermute(packed, 'section', [(source, last_section)])]
    ppermute x7, waiting for transfers between devices: 16.5 us -> 65.7 us  [body(): sent_of[source] = lax.ppermute(both, 'section', [(last, source)])]
    all_to_all x1, starting transfers between devices: 37.7 us -> 4.52 us  [gathered_columns(): pieces = lax.all_to_all(copies, axis, 0, 0, tiled=True)]
    all_to_all x1, starting transfers between devices: 17 us -> 40.5 us  [body(): lax.all_to_all(term_pieces, ('section', 'dp'), split_axis=0, concat_axis=...]
    all_to_all x1, waiting for transfers between devices: 0.01 us -> 18.7 us  [gathered_columns(): pieces = lax.all_to_all(copies, axis, 0, 0, tiled=True)]
    all_to_all x1 -> x2, local copies, waits for them, and re-layouts: 5.2 us -> 12 us  [body(): lax.all_to_all(outgoing, 'dp', split_axis=1, concat_axis=0, tiled=True)]
    another operation x1 -> x0, local copies, waits for them, and re-layouts: 6.76 us -> none
  transfers between devices with their start and end apart: 25 -> 25, of which waited for: 11 -> 10; matrix products, arithmetic and copies ran while one was open for 9% -> 12% of each run, Pallas kernels for 0% -> 0%
where the time goes in v3:
time: 548 us; the launch traced here: 539 us
  waiting for transfers between devices  230 us (42%)
  starting transfers between devices  139 us (25%)
  local copies, waits for them, and re-layouts  93.2 us (17%)
  blocking collectives  38.8 us (7%)
  matrix products  27.6 us (5%)
  other arithmetic  7.83 us (1%)
    all_to_all x8, waiting for transfers between devices, gathered_pieces(): return lax.all_to_all(copies, axis, 0, 0, tiled=True)  83.7 us
    ppermute x7, waiting for transfers between devices, body(): sent_of[source] = lax.ppermute(both, 'section', [(last, source)])  65.7 us
    ppermute x7, waiting for transfers between devices, body(): lax.ppermute(packed, 'section', [(source, last_section)])  62.2 us
    all_to_all x8, starting transfers between devices, gathered_pieces(): return lax.all_to_all(copies, axis, 0, 0, tiled=True)  61.5 us
    all_to_all x1, starting transfers between devices, body(): lax.all_to_all(term_pieces, ('section', 'dp'), split_axis=0, concat_axis=...  40.5 us
    unnamed x107, local copies, waits for them, and re-layouts  25 us
    all_to_all x1, blocking collectives, gathered_pieces(): return lax.all_to_all(copies, axis, 0, 0, tiled=True)  21.1 us
    slice x17, local copies, waits for them, and re-layouts, body(): rows = packed_of[source][:col_width]  20.1 us
  transfers between devices with their start and end apart: 25, of which 10 were waited for; matrix products, arithmetic and copies ran while one was open for 12% of the time, Pallas kernels for 0%

profile of v3, /device:TPU:6, one launch (start us, length us, event | category | flops | bytes accessed | tf_op | source)
XLA Modules:
  0.0 539.3 jit_solution(1058683701435200731)
XLA Ops:
  8.1 14.3 %all-to-all-start = ((bf16[2,192,3584]{2,0,1:T(2,128)(2,1)}), bf16[2,192,3584]{2,0,1:T(2,128)(2,1)}, u32[]{:S(2)}, u32[]{:S(2)}) async-start(bf16[2,192,3584]{2,0,1:T(2,128)(2,1)} %copy.145), calls=%async_computation | async-start | bytes 5505024 | tf_op jit(solution)/shard_map/all_to_all | solution.py:62
  39.8 62.2 %collective-permute-done = bf16[57,64,56]{1,2,0:T(8,128)(2,1)S(1)} collective-permute-done((bf16[57,64,56]{1,2,0:T(8,128)(2,1)}, bf16[57,64,56]{1,2,0:T(8,128)(2,1)S(1)}, u32[]{:S(2)}, u32[]{:S(2)}) %collective-permute-start) | collective-permute-done | bytes 408608 | tf_op jit(solution)/shard_map/ppermute | solution.py:60
  111.3 6.8 %all_to_all.56 = bf16[128,3,3584]{2,0,1:T(8,128)(2,1)} reshape(bf16[64,2,3,3584]{3,1,0,2:T(2,128)(2,1)} %copy.146) | data formatting | bytes 5505024 | tf_op jit(solution)/shard_map/all_to_all | solution.py:62
  123.5 17.7 %all_to_all.82 = f32[64,1,56]{2,1,0:T(1,128)S(1)} all-to-all(f32[64,1,56]{2,1,0:T(1,128)S(1)} %bitcast.300), channel_id=1, replica_groups=mesh['section'=8,'dp'=64] {'dp'}, dimensions={0} | all-to-all | bytes 28672 | tf_op jit(solution)/shard_map/all_to_all | solution.py:113
  143.2 21.1 %all_to_all.83 = bf16[64,2,1792]{2,1,0:T(2,128)(2,1)S(1)} all-to-all(bf16[64,2,1792]{2,1,0:T(2,128)(2,1)S(1)} %reshape.280), channel_id=1, replica_groups=mesh['section'=8,'dp'=64] {'dp'}, dimensions={0} | all-to-all | bytes 917504 | tf_op jit(solution)/shard_map/all_to_all | solution.py:18
  168.8 7.3 %all-to-all-start.3 = ((bf16[64,2,1792]{2,1,0:T(2,128)(2,1)}), bf16[64,2,1792]{2,1,0:T(2,128)(2,1)S(1)}, u32[]{:S(2)}, u32[]{:S(2)}) async-start(bf16[64,2,1792]{2,1,0:T(2,128)(2,1)} %reshape.282), calls=%async_computation.3 | async-start | bytes 917504 | tf_op jit(solution)/shard_map/all_to_all | solution.py:18
  178.3 13.1 %all-to-all-done.3 = bf16[64,2,1792]{2,1,0:T(2,128)(2,1)S(1)} async-done(((bf16[64,2,1792]{2,1,0:T(2,128)(2,1)}), bf16[64,2,1792]{2,1,0:T(2,128)(2,1)S(1)}, u32[]{:S(2)}, u32[]{:S(2)}) %all-to-all-start.3) | async-done | bytes 458784 | tf_op jit(solution)/shard_map/all_to_all | solution.py:18
  195.3 7.0 %all-to-all-start.4 = ((bf16[64,2,1792]{2,1,0:T(2,128)(2,1)}), bf16[64,2,1792]{2,1,0:T(2,128)(2,1)}, u32[]{:S(2)}, u32[]{:S(2)}) async-start(bf16[64,2,1792]{2,1,0:T(2,128)(2,1)} %reshape.284), calls=%async_computation.4 | async-start | bytes 917504 | tf_op jit(solution)/shard_map/all_to_all | solution.py:18
  204.4 13.1 %all-to-all-done.4 = bf16[64,2,1792]{2,1,0:T(2,128)(2,1)} async-done(((bf16[64,2,1792]{2,1,0:T(2,128)(2,1)}), bf16[64,2,1792]{2,1,0:T(2,128)(2,1)}, u32[]{:S(2)}, u32[]{:S(2)}) %all-to-all-start.4) | async-done | bytes 458784 | tf_op jit(solution)/shard_map/all_to_all | solution.py:18
  222.9 6.8 %all-to-all-start.5 = ((bf16[64,2,1792]{2,1,0:T(2,128)(2,1)}), bf16[64,2,1792]{2,1,0:T(2,128)(2,1)S(1)}, u32[]{:S(2)}, u32[]{:S(2)}) async-start(bf16[64,2,1792]{2,1,0:T(2,128)(2,1)} %reshape.286), calls=%async_computation.5 | async-start | bytes 917504 | tf_op jit(solution)/shard_map/all_to_all | solution.py:18
  233.2 12.0 %all-to-all-done.5 = bf16[64,2,1792]{2,1,0:T(2,128)(2,1)S(1)} async-done(((bf16[64,2,1792]{2,1,0:T(2,128)(2,1)}), bf16[64,2,1792]{2,1,0:T(2,128)(2,1)S(1)}, u32[]{:S(2)}, u32[]{:S(2)}) %all-to-all-start.5) | async-done | bytes 458784 | tf_op jit(solution)/shard_map/all_to_all | solution.py:18
  248.9 7.1 %all-to-all-start.6 = ((bf16[64,2,1792]{2,1,0:T(2,128)(2,1)}), bf16[64,2,1792]{2,1,0:T(2,128)(2,1)S(1)}, u32[]{:S(2)}, u32[]{:S(2)}) async-start(bf16[64,2,1792]{2,1,0:T(2,128)(2,1)} %reshape.288), calls=%async_computation.6 | async-start | bytes 917504 | tf_op jit(solution)/shard_map/all_to_all | solution.py:18
  259.4 11.9 %all-to-all-done.6 = bf16[64,2,1792]{2,1,0:T(2,128)(2,1)S(1)} async-done(((bf16[64,2,1792]{2,1,0:T(2,128)(2,1)}), bf16[64,2,1792]{2,1,0:T(2,128)(2,1)S(1)}, u32[]{:S(2)}, u32[]{:S(2)}) %all-to-all-start.6) | async-done | bytes 458784 | tf_op jit(solution)/shard_map/all_to_all | solution.py:18
  275.1 6.8 %all-to-all-start.7 = ((bf16[64,2,1792]{2,1,0:T(2,128)(2,1)}), bf16[64,2,1792]{2,1,0:T(2,128)(2,1)S(1)}, u32[]{:S(2)}, u32[]{:S(2)}) async-start(bf16[64,2,1792]{2,1,0:T(2,128)(2,1)} %reshape.290), calls=%async_computation.7 | async-start | bytes 917504 | tf_op jit(solution)/shard_map/all_to_all | solution.py:18
  285.3 12.0 %all-to-all-done.7 = bf16[64,2,1792]{2,1,0:T(2,128)(2,1)S(1)} async-done(((bf16[64,2,1792]{2,1,0:T(2,128)(2,1)}), bf16[64,2,1792]{2,1,0:T(2,128)(2,1)S(1)}, u32[]{:S(2)}, u32[]{:S(2)}) %all-to-all-start.7) | async-done | bytes 458784 | tf_op jit(solution)/shard_map/all_to_all | solution.py:18
  301.1 6.8 %all-to-all-start.8 = ((bf16[64,2,1792]{2,1,0:T(2,128)(2,1)}), bf16[64,2,1792]{2,1,0:T(2,128)(2,1)S(1)}, u32[]{:S(2)}, u32[]{:S(2)}) async-start(bf16[64,2,1792]{2,1,0:T(2,128)(2,1)} %reshape.292), calls=%async_computation.8 | async-start | bytes 917504 | tf_op jit(solution)/shard_map/all_to_all | solution.py:18
  311.3 12.0 %all-to-all-done.8 = bf16[64,2,1792]{2,1,0:T(2,128)(2,1)S(1)} async-done(((bf16[64,2,1792]{2,1,0:T(2,128)(2,1)}), bf16[64,2,1792]{2,1,0:T(2,128)(2,1)S(1)}, u32[]{:S(2)}, u32[]{:S(2)}) %all-to-all-start.8) | async-done | bytes 458784 | tf_op jit(solution)/shard_map/all_to_all | solution.py:18
  327.2 7.4 %all-to-all-start.9 = ((bf16[64,2,1792]{2,1,0:T(2,128)(2,1)}), bf16[64,2,1792]{2,1,0:T(2,128)(2,1)}, u32[]{:S(2)}, u32[]{:S(2)}) async-start(bf16[64,2,1792]{2,1,0:T(2,128)(2,1)} %reshape.294), calls=%async_computation.9 | async-start | bytes 917504 | tf_op jit(solution)/shard_map/all_to_all | solution.py:18
  355.1 6.8 %copy.162 = bf16[512,2,3,449]{3,1,2,0:T(2,128)(2,1)} copy(bf16[512,2,3,449]{3,0,2,1:T(8,128)(2,1)} %pad_maximum_fusion) | data formatting | bytes 5517312 | tf_op jit(solution)/shard_map/optimization_barrier | solution.py:136
  361.9 40.5 %all-to-all-start.10 = ((bf16[512,2,3,449]{3,1,2,0:T(2,128)(2,1)}), bf16[512,2,3,449]{3,1,2,0:T(2,128)(2,1)}, u32[]{:S(2)}, u32[]{:S(2)}) async-start(bf16[512,2,3,449]{3,1,2,0:T(2,128)(2,1)} %copy.162), calls=%async_computation.10 | async-start | bytes 6291456 | tf_op jit(solution)/shard_map/all_to_all | solution.py:137
  408.1 65.7 %collective-permute-done.13 = f32[2,64,56]{1,2,0:T(8,128)S(1)} collective-permute-done((f32[2,64,56]{1,2,0:T(8,128)S(1)}, f32[2,64,56]{1,2,0:T(8,128)S(1)}, u32[]{:S(2)}, u32[]{:S(2)}) %collective-permute-start.13) | collective-permute-done | bytes 28704 | tf_op jit(solution)/shard_map/ppermute | solution.py:131
  475.9 12.3 %all-to-all-start.12 = ((bf16[64,2,1792]{2,1,0:T(2,128)(2,1)}), bf16[64,2,1792]{2,1,0:T(2,128)(2,1)S(1)}, u32[]{:S(2)}, u32[]{:S(2)}) async-start(bf16[64,2,1792]{2,1,0:T(2,128)(2,1)} %reshape.296), calls=%async_computation.12 | async-start | bytes 917504 | tf_op jit(solution)/shard_map/all_to_all | solution.py:18
  494.0 9.6 %all-to-all-done.12 = bf16[64,2,1792]{2,1,0:T(2,128)(2,1)S(1)} async-done(((bf16[64,2,1792]{2,1,0:T(2,128)(2,1)}), bf16[64,2,1792]{2,1,0:T(2,128)(2,1)S(1)}, u32[]{:S(2)}, u32[]{:S(2)}) %all-to-all-start.12) | async-done | bytes 458784 | tf_op jit(solution)/shard_map/all_to_all | solution.py:18
  517.1 18.7 %all-to-all-done.11 = bf16[8,128,448]{1,2,0:T(8,128)(2,1)S(1)} async-done(((bf16[8,128,448]{1,2,0:T(8,128)(2,1)}), bf16[8,128,448]{1,2,0:T(8,128)(2,1)S(1)}, u32[]{:S(2)}, u32[]{:S(2)}) %all-to-all-start.11) | async-done | bytes 917536 | tf_op jit(solution)/shard_map/all_to_all | solution.py:24
  (207 shorter events, 138.3 us)
Async XLA Ops:
  8.1 97.9 %all-to-all-start = ((bf16[2,192,3584]{2,0,1:T(2,128)(2,1)}), bf16[2,192,3584]{2,0,1:T(2,128)(2,1)}, u32[]{:S(2)}, u32[]{:S(2)}) async-start(bf16[2,192,3584]{2,0,1:T(2,128)(2,1)} %copy.145), calls=%async_computation | async-start | bytes 5505024 | tf_op jit(solution)/shard_map/all_to_all | solution.py:62
  26.0 76.0 %collective-permute-start = (bf16[57,64,56]{1,2,0:T(8,128)(2,1)}, bf16[57,64,56]{1,2,0:T(8,128)(2,1)S(1)}, u32[]{:S(2)}, u32[]{:S(2)}) collective-permute-start(bf16[57,64,56]{1,2,0:T(8,128)(2,1)} %pad_maximum_fusion.1), channel_id=1, source_target_pairs={{0,448},{1,449},{2,450},{3,451},{4,452},{5,453},{6,454},{7,455},{8... | collective-permute-start | bytes 1225736 | tf_op jit(solution)/shard_map/ppermute | solution.py:60
  31.4 71.5 %collective-permute-start.1 = (bf16[57,64,56]{1,2,0:T(8,128)(2,1)}, bf16[57,64,56]{1,2,0:T(8,128)(2,1)}, u32[]{:S(2)}, u32[]{:S(2)}) collective-permute-start(bf16[57,64,56]{1,2,0:T(8,128)(2,1)} %pad_maximum_fusion.1), channel_id=1, source_target_pairs={{64,448},{65,449},{66,450},{67,451},{68,452},{69,453},{70,454},{71... | collective-permute-start | bytes 1225736 | tf_op jit(solution)/shard_map/ppermute | solution.py:60
  33.0 85.0 %collective-permute-start.2 = (bf16[57,64,56]{1,2,0:T(8,128)(2,1)}, bf16[57,64,56]{1,2,0:T(8,128)(2,1)}, u32[]{:S(2)}, u32[]{:S(2)}) collective-permute-start(bf16[57,64,56]{1,2,0:T(8,128)(2,1)} %pad_maximum_fusion.1), channel_id=1, source_target_pairs={{128,448},{129,449},{130,450},{131,451},{132,452},{133,453},{134,4... | collective-permute-start | bytes 1225736 | tf_op jit(solution)/shard_map/ppermute | solution.py:60
  34.6 83.4 %collective-permute-start.3 = (bf16[57,64,56]{1,2,0:T(8,128)(2,1)}, bf16[57,64,56]{1,2,0:T(8,128)(2,1)}, u32[]{:S(2)}, u32[]{:S(2)}) collective-permute-start(bf16[57,64,56]{1,2,0:T(8,128)(2,1)} %pad_maximum_fusion.1), channel_id=1, source_target_pairs={{192,448},{193,449},{194,450},{195,451},{196,452},{197,453},{198,4... | collective-permute-start | bytes 1225736 | tf_op jit(solution)/shard_map/ppermute | solution.py:60
  36.2 81.8 %collective-permute-start.4 = (bf16[57,64,56]{1,2,0:T(8,128)(2,1)}, bf16[57,64,56]{1,2,0:T(8,128)(2,1)}, u32[]{:S(2)}, u32[]{:S(2)}) collective-permute-start(bf16[57,64,56]{1,2,0:T(8,128)(2,1)} %pad_maximum_fusion.1), channel_id=1, source_target_pairs={{256,448},{257,449},{258,450},{259,451},{260,452},{261,453},{262,4... | collective-permute-start | bytes 1225736 | tf_op jit(solution)/shard_map/ppermute | solution.py:60
  102.0 16.1 %collective-permute-start.5 = (bf16[57,64,56]{1,2,0:T(8,128)(2,1)}, bf16[57,64,56]{1,2,0:T(8,128)(2,1)S(1)}, u32[]{:S(2)}, u32[]{:S(2)}) collective-permute-start(bf16[57,64,56]{1,2,0:T(8,128)(2,1)} %pad_maximum_fusion.1), channel_id=1, source_target_pairs={{320,448},{321,449},{322,450},{323,451},{324,452},{325,453},{326,4... | collective-permute-start | bytes 1225736 | tf_op jit(solution)/shard_map/ppermute | solution.py:60
  102.9 15.2 %collective-permute-start.6 = (bf16[57,64,56]{1,2,0:T(8,128)(2,1)}, bf16[57,64,56]{1,2,0:T(8,128)(2,1)S(1)}, u32[]{:S(2)}, u32[]{:S(2)}) collective-permute-start(bf16[57,64,56]{1,2,0:T(8,128)(2,1)} %pad_maximum_fusion.1), channel_id=1, source_target_pairs={{384,448},{385,449},{386,450},{387,451},{388,452},{389,453},{390,4... | collective-permute-start | bytes 1225736 | tf_op jit(solution)/shard_map/ppermute | solution.py:60
  168.8 22.6 %all-to-all-start.3 = ((bf16[64,2,1792]{2,1,0:T(2,128)(2,1)}), bf16[64,2,1792]{2,1,0:T(2,128)(2,1)S(1)}, u32[]{:S(2)}, u32[]{:S(2)}) async-start(bf16[64,2,1792]{2,1,0:T(2,128)(2,1)} %reshape.282), calls=%async_computation.3 | async-start | bytes 917504 | tf_op jit(solution)/shard_map/all_to_all | solution.py:18
  195.3 22.3 %all-to-all-start.4 = ((bf16[64,2,1792]{2,1,0:T(2,128)(2,1)}), bf16[64,2,1792]{2,1,0:T(2,128)(2,1)}, u32[]{:S(2)}, u32[]{:S(2)}) async-start(bf16[64,2,1792]{2,1,0:T(2,128)(2,1)} %reshape.284), calls=%async_computation.4 | async-start | bytes 917504 | tf_op jit(solution)/shard_map/all_to_all | solution.py:18
  222.9 22.2 %all-to-all-start.5 = ((bf16[64,2,1792]{2,1,0:T(2,128)(2,1)}), bf16[64,2,1792]{2,1,0:T(2,128)(2,1)S(1)}, u32[]{:S(2)}, u32[]{:S(2)}) async-start(bf16[64,2,1792]{2,1,0:T(2,128)(2,1)} %reshape.286), calls=%async_computation.5 | async-start | bytes 917504 | tf_op jit(solution)/shard_map/all_to_all | solution.py:18
  248.9 22.4 %all-to-all-start.6 = ((bf16[64,2,1792]{2,1,0:T(2,128)(2,1)}), bf16[64,2,1792]{2,1,0:T(2,128)(2,1)S(1)}, u32[]{:S(2)}, u32[]{:S(2)}) async-start(bf16[64,2,1792]{2,1,0:T(2,128)(2,1)} %reshape.288), calls=%async_computation.6 | async-start | bytes 917504 | tf_op jit(solution)/shard_map/all_to_all | solution.py:18
  275.1 22.2 %all-to-all-start.7 = ((bf16[64,2,1792]{2,1,0:T(2,128)(2,1)}), bf16[64,2,1792]{2,1,0:T(2,128)(2,1)S(1)}, u32[]{:S(2)}, u32[]{:S(2)}) async-start(bf16[64,2,1792]{2,1,0:T(2,128)(2,1)} %reshape.290), calls=%async_computation.7 | async-start | bytes 917504 | tf_op jit(solution)/shard_map/all_to_all | solution.py:18
  301.1 22.2 %all-to-all-start.8 = ((bf16[64,2,1792]{2,1,0:T(2,128)(2,1)}), bf16[64,2,1792]{2,1,0:T(2,128)(2,1)S(1)}, u32[]{:S(2)}, u32[]{:S(2)}) async-start(bf16[64,2,1792]{2,1,0:T(2,128)(2,1)} %reshape.292), calls=%async_computation.8 | async-start | bytes 917504 | tf_op jit(solution)/shard_map/all_to_all | solution.py:18
  327.2 25.3 %all-to-all-start.9 = ((bf16[64,2,1792]{2,1,0:T(2,128)(2,1)}), bf16[64,2,1792]{2,1,0:T(2,128)(2,1)}, u32[]{:S(2)}, u32[]{:S(2)}) async-start(bf16[64,2,1792]{2,1,0:T(2,128)(2,1)} %reshape.294), calls=%async_computation.9 | async-start | bytes 917504 | tf_op jit(solution)/shard_map/all_to_all | solution.py:18
  361.9 114.0 %all-to-all-start.10 = ((bf16[512,2,3,449]{3,1,2,0:T(2,128)(2,1)}), bf16[512,2,3,449]{3,1,2,0:T(2,128)(2,1)}, u32[]{:S(2)}, u32[]{:S(2)}) async-start(bf16[512,2,3,449]{3,1,2,0:T(2,128)(2,1)} %copy.162), calls=%async_computation.10 | async-start | bytes 6291456 | tf_op jit(solution)/shard_map/all_to_all | solution.py:137
  402.4 3.6 collective-permute-start.7
  403.2 3.5 collective-permute-start.8
  403.9 4.2 collective-permute-start.9
  404.6 3.5 collective-permute-start.10
  405.3 2.8 collective-permute-start.11
  406.7 67.1 %collective-permute-start.13 = (f32[2,64,56]{1,2,0:T(8,128)S(1)}, f32[2,64,56]{1,2,0:T(8,128)S(1)}, u32[]{:S(2)}, u32[]{:S(2)}) collective-permute-start(f32[2,64,56]{1,2,0:T(8,128)S(1)} %pad_maximum_fusion.8), channel_id=1, source_target_pairs={{448,0},{449,1},{450,2},{451,3},{452,4},{453,5},{454,6},{455,7},{4... | collective-permute-start | bytes 86024 | tf_op jit(solution)/shard_map/ppermute | solution.py:131
  475.9 27.7 %all-to-all-start.12 = ((bf16[64,2,1792]{2,1,0:T(2,128)(2,1)}), bf16[64,2,1792]{2,1,0:T(2,128)(2,1)S(1)}, u32[]{:S(2)}, u32[]{:S(2)}) async-start(bf16[64,2,1792]{2,1,0:T(2,128)(2,1)} %reshape.296), calls=%async_computation.12 | async-start | bytes 917504 | tf_op jit(solution)/shard_map/all_to_all | solution.py:18
  504.7 31.1 %all-to-all-start.11 = ((bf16[8,128,448]{1,2,0:T(8,128)(2,1)}), bf16[8,128,448]{1,2,0:T(8,128)(2,1)S(1)}, u32[]{:S(2)}, u32[]{:S(2)}) async-start(bf16[8,128,448]{1,2,0:T(8,128)(2,1)} %broadcast_in_dim.146), calls=%async_computation.11 | async-start | bytes 1835008 | tf_op jit(solution)/shard_map/all_to_all | solution.py:24
  (42 other events, 1089.2 us)

commit v4 on v3

--- a/solution.py
+++ b/solution.py
@@ -88,21 +88,21 @@
         )
         * INVERSE_TEMP
     )
-    passage_sums = (
-        jnp.einsum(
-            "fnyw,fnj->wfyj", weight_matrices, query_row_items, preferred_element_type=jnp.float32
-        )
-        * INVERSE_TEMP
-    )
-    block_terms = passage_sums.reshape(row_block_count, requests, width).astype(jnp.bfloat16)
     micro_count = section_inputs.shape[1] // dp_count
     micro_cols = jnp.transpose(
         query_sums[0, :micro_count].reshape(micro_count, dp_count, col_width), (1, 0, 2)
     )
     section_count = lax.axis_size("section")
     chunk = width // section_count
-    term_pieces = passage_sums.reshape(dp_count, stripe, requests, section_count, chunk)
-    term_pieces = jnp.transpose(term_pieces, (3, 0, 1, 2, 4)).astype(jnp.bfloat16)
+    term_pieces = (
+        jnp.einsum(
+            "fnydr,fnsc->sdryc",
+            weight_matrices.reshape(blocks_here, row_block_count, slot_count, dp_count, stripe),
+            query_row_items.reshape(blocks_here, row_block_count, section_count, chunk),
+            preferred_element_type=jnp.float32,
+        )
+        * INVERSE_TEMP
+    ).astype(jnp.bfloat16)
     term_pieces = term_pieces.reshape(section_count * dp_count, stripe, requests, chunk)
     own_slots = lax.dynamic_slice_in_dim(all_slots, dp_index * requests, requests)
     slot_tags = jnp.broadcast_to(
@@ -129,11 +129,13 @@
         else:
             both = jnp.stack([carry, inner.astype(jnp.float32)])
             sent_of[source] = lax.ppermute(both, "section", [(last, source)])
+    term_pieces, sent = lax.optimization_barrier(
+        (term_pieces, tuple(sent_of[source] for source in range(last)))
+    )
     for source in range(last):
         here = section_index == source
-        grad_cols = jnp.where(here, sent_of[source][0], grad_cols)
-        home_inner = jnp.where(here, sent_of[source][1].astype(jnp.bfloat16), home_inner)
-    term_pieces, carry = lax.optimization_barrier((term_pieces, carry))
+        grad_cols = jnp.where(here, sent[source][0], grad_cols)
+        home_inner = jnp.where(here, sent[source][1].astype(jnp.bfloat16), home_inner)
     incoming_terms = lax.all_to_all(
         term_pieces, ("section", "dp"), split_axis=0, concat_axis=0, tiled=True
     )

time: 548 us -> 542 us (0.989)
  waiting for transfers between devices: 230 us -> 254 us
  starting transfers between devices: 139 us -> 117 us
  matrix products: 27.6 us -> 20.9 us
  local copies, waits for them, and re-layouts: 93.2 us -> 87.1 us
  other arithmetic: 7.83 us -> 13.9 us
    all_to_all x1, waiting for transfers between devices: 0.01 us -> 70 us  [body(): lax.all_to_all(term_pieces, ('section', 'dp'), split_axis=0, concat_axis=...]
    ppermute x7, waiting for transfers between devices: 65.7 us -> 27.2 us  [body(): sent_of[source] = lax.ppermute(both, 'section', [(last, source)])]
    all_to_all x1, starting transfers between devices: 40.5 us -> 16.8 us  [body(): lax.all_to_all(term_pieces, ('section', 'dp'), split_axis=0, concat_axis=...]
    convert_element_type x2 -> x0, local copies, waits for them, and re-layouts: 10.3 us -> none  [body(): jnp.transpose(term_pieces, (3, 0, 1, 2, 4)).astype(jnp.bfloat16)]
    optimization_barrier x1 -> x0, local copies, waits for them, and re-layouts: 6.76 us -> none  [body(): term_pieces, carry = lax.optimization_barrier((term_pieces, carry))]
    slice x17 -> x14, local copies, waits for them, and re-layouts: 20.1 us -> 24.3 us  [body(): rows = packed_of[source][:col_width]]
    unnamed x107 -> x64, local copies, waits for them, and re-layouts: 25 us -> 28.3 us
  transfers between devices with their start and end apart: 25 -> 25, of which waited for: 10 -> 12; matrix products, arithmetic and copies ran while one was open for 12% -> 14% of each run, Pallas kernels for 0% -> 0%
where the time goes in v4:
time: 542 us; the launch traced here: 534 us
  waiting for transfers between devices  254 us (47%)
  starting transfers between devices  117 us (22%)
  local copies, waits for them, and re-layouts  87.1 us (16%)
  blocking collectives  39 us (7%)
  matrix products  20.9 us (4%)
  other arithmetic  13.9 us (3%)
    all_to_all x8, waiting for transfers between devices, gathered_pieces(): return lax.all_to_all(copies, axis, 0, 0, tiled=True)  79.5 us
    all_to_all x1, waiting for transfers between devices, body(): lax.all_to_all(term_pieces, ('section', 'dp'), split_axis=0, concat_axis=...  70 us
    ppermute x7, waiting for transfers between devices, body(): lax.ppermute(packed, 'section', [(source, last_section)])  60.5 us
    all_to_all x8, starting transfers between devices, gathered_pieces(): return lax.all_to_all(copies, axis, 0, 0, tiled=True)  58.1 us
    unnamed x64, local copies, waits for them, and re-layouts  28.3 us
    ppermute x7, waiting for transfers between devices, body(): sent_of[source] = lax.ppermute(both, 'section', [(last, source)])  27.2 us
    slice x14, local copies, waits for them, and re-layouts, body(): rows = packed_of[source][:col_width]  24.3 us
    all_to_all x1, blocking collectives, gathered_pieces(): return lax.all_to_all(copies, axis, 0, 0, tiled=True)  21.1 us
  transfers between devices with their start and end apart: 25, of which 12 were waited for; matrix products, arithmetic and copies ran while one was open for 14% of the time, Pallas kernels for 0%

profile of v4, /device:TPU:6, one launch (start us, length us, event | category | flops | bytes accessed | tf_op | source)
XLA Modules:
  0.0 533.7 jit_solution(18197971273316096458)
XLA Ops:
  7.1 14.1 %all-to-all-start = ((bf16[2,192,3584]{2,0,1:T(2,128)(2,1)}), bf16[2,192,3584]{2,0,1:T(2,128)(2,1)S(1)}, u32[]{:S(2)}, u32[]{:S(2)}) async-start(bf16[2,192,3584]{2,0,1:T(2,128)(2,1)} %copy.151), calls=%async_computation | async-start | bytes 5505024 | tf_op jit(solution)/shard_map/all_to_all | solution.py:62
  27.4 6.3 %collective-permute-start = (bf16[57,64,56]{1,2,0:T(8,128)(2,1)}, bf16[57,64,56]{1,2,0:T(8,128)(2,1)}, u32[]{:S(2)}, u32[]{:S(2)}) collective-permute-start(bf16[57,64,56]{1,2,0:T(8,128)(2,1)} %pad_maximum_fusion.1), channel_id=1, source_target_pairs={{0,448},{1,449},{2,450},{3,451},{4,452},{5,453},{6,454},{7,455},{8... | collective-permute-start | bytes 1225736 | tf_op jit(solution)/shard_map/ppermute | solution.py:60
  42.9 60.5 %collective-permute-done = bf16[57,64,56]{1,2,0:T(8,128)(2,1)} collective-permute-done((bf16[57,64,56]{1,2,0:T(8,128)(2,1)}, bf16[57,64,56]{1,2,0:T(8,128)(2,1)}, u32[]{:S(2)}, u32[]{:S(2)}) %collective-permute-start) | collective-permute-done | bytes 408608 | tf_op jit(solution)/shard_map/ppermute | solution.py:60
  120.3 17.8 %all_to_all.82 = f32[64,1,56]{2,1,0:T(1,128)S(1)} all-to-all(f32[64,1,56]{2,1,0:T(1,128)S(1)} %bitcast.288), channel_id=1, replica_groups=mesh['section'=8,'dp'=64] {'dp'}, dimensions={0} | all-to-all | bytes 28672 | tf_op jit(solution)/shard_map/all_to_all | solution.py:113
  138.9 21.1 %all_to_all.83 = bf16[64,2,1792]{2,1,0:T(2,128)(2,1)S(1)} all-to-all(bf16[64,2,1792]{2,1,0:T(2,128)(2,1)S(1)} %reshape.283), channel_id=1, replica_groups=mesh['section'=8,'dp'=64] {'dp'}, dimensions={0} | all-to-all | bytes 917504 | tf_op jit(solution)/shard_map/all_to_all | solution.py:18
  164.3 7.3 %all-to-all-start.3 = ((bf16[64,2,1792]{2,1,0:T(2,128)(2,1)}), bf16[64,2,1792]{2,1,0:T(2,128)(2,1)S(1)}, u32[]{:S(2)}, u32[]{:S(2)}) async-start(bf16[64,2,1792]{2,1,0:T(2,128)(2,1)} %reshape.285), calls=%async_computation.3 | async-start | bytes 917504 | tf_op jit(solution)/shard_map/all_to_all | solution.py:18
  175.0 11.9 %all-to-all-done.3 = bf16[64,2,1792]{2,1,0:T(2,128)(2,1)S(1)} async-done(((bf16[64,2,1792]{2,1,0:T(2,128)(2,1)}), bf16[64,2,1792]{2,1,0:T(2,128)(2,1)S(1)}, u32[]{:S(2)}, u32[]{:S(2)}) %all-to-all-start.3) | async-done | bytes 458784 | tf_op jit(solution)/shard_map/all_to_all | solution.py:18
  190.0 6.8 %all-to-all-start.4 = ((bf16[64,2,1792]{2,1,0:T(2,128)(2,1)}), bf16[64,2,1792]{2,1,0:T(2,128)(2,1)S(1)}, u32[]{:S(2)}, u32[]{:S(2)}) async-start(bf16[64,2,1792]{2,1,0:T(2,128)(2,1)} %reshape.287), calls=%async_computation.4 | async-start | bytes 917504 | tf_op jit(solution)/shard_map/all_to_all | solution.py:18
  200.3 12.0 %all-to-all-done.4 = bf16[64,2,1792]{2,1,0:T(2,128)(2,1)S(1)} async-done(((bf16[64,2,1792]{2,1,0:T(2,128)(2,1)}), bf16[64,2,1792]{2,1,0:T(2,128)(2,1)S(1)}, u32[]{:S(2)}, u32[]{:S(2)}) %all-to-all-start.4) | async-done | bytes 458784 | tf_op jit(solution)/shard_map/all_to_all | solution.py:18
  215.4 6.8 %all-to-all-start.5 = ((bf16[64,2,1792]{2,1,0:T(2,128)(2,1)}), bf16[64,2,1792]{2,1,0:T(2,128)(2,1)S(1)}, u32[]{:S(2)}, u32[]{:S(2)}) async-start(bf16[64,2,1792]{2,1,0:T(2,128)(2,1)} %reshape.289), calls=%async_computation.5 | async-start | bytes 917504 | tf_op jit(solution)/shard_map/all_to_all | solution.py:18
  225.6 12.0 %all-to-all-done.5 = bf16[64,2,1792]{2,1,0:T(2,128)(2,1)S(1)} async-done(((bf16[64,2,1792]{2,1,0:T(2,128)(2,1)}), bf16[64,2,1792]{2,1,0:T(2,128)(2,1)S(1)}, u32[]{:S(2)}, u32[]{:S(2)}) %all-to-all-start.5) | async-done | bytes 458784 | tf_op jit(solution)/shard_map/all_to_all | solution.py:18
  240.8 7.1 %all-to-all-start.6 = ((bf16[64,2,1792]{2,1,0:T(2,128)(2,1)}), bf16[64,2,1792]{2,1,0:T(2,128)(2,1)S(1)}, u32[]{:S(2)}, u32[]{:S(2)}) async-start(bf16[64,2,1792]{2,1,0:T(2,128)(2,1)} %reshape.291), calls=%async_computation.6 | async-start | bytes 917504 | tf_op jit(solution)/shard_map/all_to_all | solution.py:18
  251.3 11.9 %all-to-all-done.6 = bf16[64,2,1792]{2,1,0:T(2,128)(2,1)S(1)} async-done(((bf16[64,2,1792]{2,1,0:T(2,128)(2,1)}), bf16[64,2,1792]{2,1,0:T(2,128)(2,1)S(1)}, u32[]{:S(2)}, u32[]{:S(2)}) %all-to-all-start.6) | async-done | bytes 458784 | tf_op jit(solution)/shard_map/all_to_all | solution.py:18
  266.9 6.8 %all-to-all-start.7 = ((bf16[64,2,1792]{2,1,0:T(2,128)(2,1)}), bf16[64,2,1792]{2,1,0:T(2,128)(2,1)S(1)}, u32[]{:S(2)}, u32[]{:S(2)}) async-start(bf16[64,2,1792]{2,1,0:T(2,128)(2,1)} %reshape.293), calls=%async_computation.7 | async-start | bytes 917504 | tf_op jit(solution)/shard_map/all_to_all | solution.py:18
  277.1 12.0 %all-to-all-done.7 = bf16[64,2,1792]{2,1,0:T(2,128)(2,1)S(1)} async-done(((bf16[64,2,1792]{2,1,0:T(2,128)(2,1)}), bf16[64,2,1792]{2,1,0:T(2,128)(2,1)S(1)}, u32[]{:S(2)}, u32[]{:S(2)}) %all-to-all-start.7) | async-done | bytes 458784 | tf_op jit(solution)/shard_map/all_to_all | solution.py:18
  292.9 6.8 %all-to-all-start.8 = ((bf16[64,2,1792]{2,1,0:T(2,128)(2,1)}), bf16[64,2,1792]{2,1,0:T(2,128)(2,1)S(1)}, u32[]{:S(2)}, u32[]{:S(2)}) async-start(bf16[64,2,1792]{2,1,0:T(2,128)(2,1)} %reshape.295), calls=%async_computation.8 | async-start | bytes 917504 | tf_op jit(solution)/shard_map/all_to_all | solution.py:18
  309.0 6.1 %all-to-all-done.8 = bf16[64,2,1792]{2,1,0:T(2,128)(2,1)S(1)} async-done(((bf16[64,2,1792]{2,1,0:T(2,128)(2,1)}), bf16[64,2,1792]{2,1,0:T(2,128)(2,1)S(1)}, u32[]{:S(2)}, u32[]{:S(2)}) %all-to-all-start.8) | async-done | bytes 458784 | tf_op jit(solution)/shard_map/all_to_all | solution.py:18
  318.8 7.4 %all-to-all-start.9 = ((bf16[64,2,1792]{2,1,0:T(2,128)(2,1)}), bf16[64,2,1792]{2,1,0:T(2,128)(2,1)}, u32[]{:S(2)}, u32[]{:S(2)}) async-start(bf16[64,2,1792]{2,1,0:T(2,128)(2,1)} %reshape.297), calls=%async_computation.9 | async-start | bytes 917504 | tf_op jit(solution)/shard_map/all_to_all | solution.py:18
  355.1 27.2 %collective-permute-done.7 = f32[2,64,56]{1,2,0:T(8,128)} collective-permute-done((f32[2,64,56]{1,2,0:T(8,128)S(1)}, f32[2,64,56]{1,2,0:T(8,128)}, u32[]{:S(2)}, u32[]{:S(2)}) %collective-permute-start.7) | collective-permute-done | bytes 28704 | tf_op jit(solution)/shard_map/ppermute | solution.py:131
  382.2 16.8 %all-to-all-start.10 = ((bf16[512,2,3,449]{3,1,2,0:T(2,128)(2,1)}), bf16[512,2,3,449]{3,1,2,0:T(2,128)(2,1)S(1)}, u32[]{:S(2)}, u32[]{:S(2)}) async-start(bf16[512,2,3,449]{3,1,2,0:T(2,128)(2,1)} %pad_maximum_fusion), calls=%async_computation.10 | async-start | bytes 6291456 | tf_op jit(solution)/shard_map/all_to_all | solution.py:139
  403.8 70.0 %all-to-all-done.10 = bf16[512,2,3,449]{3,1,2,0:T(2,128)(2,1)S(1)} async-done(((bf16[512,2,3,449]{3,1,2,0:T(2,128)(2,1)}), bf16[512,2,3,449]{3,1,2,0:T(2,128)(2,1)S(1)}, u32[]{:S(2)}, u32[]{:S(2)}) %all-to-all-start.10) | async-done | bytes 2758688 | tf_op jit(solution)/shard_map/all_to_all | solution.py:139
  473.9 9.1 %all-to-all-start.12 = ((bf16[64,2,1792]{2,1,0:T(2,128)(2,1)}), bf16[64,2,1792]{2,1,0:T(2,128)(2,1)}, u32[]{:S(2)}, u32[]{:S(2)}) async-start(bf16[64,2,1792]{2,1,0:T(2,128)(2,1)} %reshape.299), calls=%async_computation.12 | async-start | bytes 917504 | tf_op jit(solution)/shard_map/all_to_all | solution.py:18
  487.8 10.5 %all-to-all-done.12 = bf16[64,2,1792]{2,1,0:T(2,128)(2,1)} async-done(((bf16[64,2,1792]{2,1,0:T(2,128)(2,1)}), bf16[64,2,1792]{2,1,0:T(2,128)(2,1)}, u32[]{:S(2)}, u32[]{:S(2)}) %all-to-all-start.12) | async-done | bytes 458784 | tf_op jit(solution)/shard_map/all_to_all | solution.py:18
  513.4 16.6 %all-to-all-done.11 = bf16[8,128,448]{1,2,0:T(8,128)(2,1)S(1)} async-done(((bf16[8,128,448]{1,2,0:T(8,128)(2,1)}), bf16[8,128,448]{1,2,0:T(8,128)(2,1)S(1)}, u32[]{:S(2)}, u32[]{:S(2)}) %all-to-all-start.11) | async-done | bytes 917536 | tf_op jit(solution)/shard_map/all_to_all | solution.py:24
  (159 shorter events, 146.9 us)
Async XLA Ops:
  7.1 100.0 %all-to-all-start = ((bf16[2,192,3584]{2,0,1:T(2,128)(2,1)}), bf16[2,192,3584]{2,0,1:T(2,128)(2,1)S(1)}, u32[]{:S(2)}, u32[]{:S(2)}) async-start(bf16[2,192,3584]{2,0,1:T(2,128)(2,1)} %copy.151), calls=%async_computation | async-start | bytes 5505024 | tf_op jit(solution)/shard_map/all_to_all | solution.py:62
  27.4 76.0 %collective-permute-start = (bf16[57,64,56]{1,2,0:T(8,128)(2,1)}, bf16[57,64,56]{1,2,0:T(8,128)(2,1)}, u32[]{:S(2)}, u32[]{:S(2)}) collective-permute-start(bf16[57,64,56]{1,2,0:T(8,128)(2,1)} %pad_maximum_fusion.1), channel_id=1, source_target_pairs={{0,448},{1,449},{2,450},{3,451},{4,452},{5,453},{6,454},{7,455},{8... | collective-permute-start | bytes 1225736 | tf_op jit(solution)/shard_map/ppermute | solution.py:60
  33.6 71.3 %collective-permute-start.1 = (bf16[57,64,56]{1,2,0:T(8,128)(2,1)}, bf16[57,64,56]{1,2,0:T(8,128)(2,1)}, u32[]{:S(2)}, u32[]{:S(2)}) collective-permute-start(bf16[57,64,56]{1,2,0:T(8,128)(2,1)} %pad_maximum_fusion.1), channel_id=1, source_target_pairs={{64,448},{65,449},{66,450},{67,451},{68,452},{69,453},{70,454},{71... | collective-permute-start | bytes 1225736 | tf_op jit(solution)/shard_map/ppermute | solution.py:60
  35.2 80.9 %collective-permute-start.2 = (bf16[57,64,56]{1,2,0:T(8,128)(2,1)}, bf16[57,64,56]{1,2,0:T(8,128)(2,1)}, u32[]{:S(2)}, u32[]{:S(2)}) collective-permute-start(bf16[57,64,56]{1,2,0:T(8,128)(2,1)} %pad_maximum_fusion.1), channel_id=1, source_target_pairs={{128,448},{129,449},{130,450},{131,451},{132,452},{133,453},{134,4... | collective-permute-start | bytes 1225736 | tf_op jit(solution)/shard_map/ppermute | solution.py:60
  36.8 79.3 %collective-permute-start.3 = (bf16[57,64,56]{1,2,0:T(8,128)(2,1)}, bf16[57,64,56]{1,2,0:T(8,128)(2,1)}, u32[]{:S(2)}, u32[]{:S(2)}) collective-permute-start(bf16[57,64,56]{1,2,0:T(8,128)(2,1)} %pad_maximum_fusion.1), channel_id=1, source_target_pairs={{192,448},{193,449},{194,450},{195,451},{196,452},{197,453},{198,4... | collective-permute-start | bytes 1225736 | tf_op jit(solution)/shard_map/ppermute | solution.py:60
  38.3 77.8 %collective-permute-start.4 = (bf16[57,64,56]{1,2,0:T(8,128)(2,1)}, bf16[57,64,56]{1,2,0:T(8,128)(2,1)}, u32[]{:S(2)}, u32[]{:S(2)}) collective-permute-start(bf16[57,64,56]{1,2,0:T(8,128)(2,1)} %pad_maximum_fusion.1), channel_id=1, source_target_pairs={{256,448},{257,449},{258,450},{259,451},{260,452},{261,453},{262,4... | collective-permute-start | bytes 1225736 | tf_op jit(solution)/shard_map/ppermute | solution.py:60
  103.3 12.8 %collective-permute-start.5 = (bf16[57,64,56]{1,2,0:T(8,128)(2,1)}, bf16[57,64,56]{1,2,0:T(8,128)(2,1)}, u32[]{:S(2)}, u32[]{:S(2)}) collective-permute-start(bf16[57,64,56]{1,2,0:T(8,128)(2,1)} %pad_maximum_fusion.1), channel_id=1, source_target_pairs={{320,448},{321,449},{322,450},{323,451},{324,452},{325,453},{326,4... | collective-permute-start | bytes 1225736 | tf_op jit(solution)/shard_map/ppermute | solution.py:60
  104.9 11.2 %collective-permute-start.6 = (bf16[57,64,56]{1,2,0:T(8,128)(2,1)}, bf16[57,64,56]{1,2,0:T(8,128)(2,1)}, u32[]{:S(2)}, u32[]{:S(2)}) collective-permute-start(bf16[57,64,56]{1,2,0:T(8,128)(2,1)} %pad_maximum_fusion.1), channel_id=1, source_target_pairs={{384,448},{385,449},{386,450},{387,451},{388,452},{389,453},{390,4... | collective-permute-start | bytes 1225736 | tf_op jit(solution)/shard_map/ppermute | solution.py:60
  164.3 22.6 %all-to-all-start.3 = ((bf16[64,2,1792]{2,1,0:T(2,128)(2,1)}), bf16[64,2,1792]{2,1,0:T(2,128)(2,1)S(1)}, u32[]{:S(2)}, u32[]{:S(2)}) async-start(bf16[64,2,1792]{2,1,0:T(2,128)(2,1)} %reshape.285), calls=%async_computation.3 | async-start | bytes 917504 | tf_op jit(solution)/shard_map/all_to_all | solution.py:18
  190.0 22.2 %all-to-all-start.4 = ((bf16[64,2,1792]{2,1,0:T(2,128)(2,1)}), bf16[64,2,1792]{2,1,0:T(2,128)(2,1)S(1)}, u32[]{:S(2)}, u32[]{:S(2)}) async-start(bf16[64,2,1792]{2,1,0:T(2,128)(2,1)} %reshape.287), calls=%async_computation.4 | async-start | bytes 917504 | tf_op jit(solution)/shard_map/all_to_all | solution.py:18
  215.4 22.2 %all-to-all-start.5 = ((bf16[64,2,1792]{2,1,0:T(2,128)(2,1)}), bf16[64,2,1792]{2,1,0:T(2,128)(2,1)S(1)}, u32[]{:S(2)}, u32[]{:S(2)}) async-start(bf16[64,2,1792]{2,1,0:T(2,128)(2,1)} %reshape.289), calls=%async_computation.5 | async-start | bytes 917504 | tf_op jit(solution)/shard_map/all_to_all | solution.py:18
  240.8 22.4 %all-to-all-start.6 = ((bf16[64,2,1792]{2,1,0:T(2,128)(2,1)}), bf16[64,2,1792]{2,1,0:T(2,128)(2,1)S(1)}, u32[]{:S(2)}, u32[]{:S(2)}) async-start(bf16[64,2,1792]{2,1,0:T(2,128)(2,1)} %reshape.291), calls=%async_computation.6 | async-start | bytes 917504 | tf_op jit(solution)/shard_map/all_to_all | solution.py:18
  266.9 22.2 %all-to-all-start.7 = ((bf16[64,2,1792]{2,1,0:T(2,128)(2,1)}), bf16[64,2,1792]{2,1,0:T(2,128)(2,1)S(1)}, u32[]{:S(2)}, u32[]{:S(2)}) async-start(bf16[64,2,1792]{2,1,0:T(2,128)(2,1)} %reshape.293), calls=%async_computation.7 | async-start | bytes 917504 | tf_op jit(solution)/shard_map/all_to_all | solution.py:18
  292.9 22.2 %all-to-all-start.8 = ((bf16[64,2,1792]{2,1,0:T(2,128)(2,1)}), bf16[64,2,1792]{2,1,0:T(2,128)(2,1)S(1)}, u32[]{:S(2)}, u32[]{:S(2)}) async-start(bf16[64,2,1792]{2,1,0:T(2,128)(2,1)} %reshape.295), calls=%async_computation.8 | async-start | bytes 917504 | tf_op jit(solution)/shard_map/all_to_all | solution.py:18
  318.8 22.5 %all-to-all-start.9 = ((bf16[64,2,1792]{2,1,0:T(2,128)(2,1)}), bf16[64,2,1792]{2,1,0:T(2,128)(2,1)}, u32[]{:S(2)}, u32[]{:S(2)}) async-start(bf16[64,2,1792]{2,1,0:T(2,128)(2,1)} %reshape.297), calls=%async_computation.9 | async-start | bytes 917504 | tf_op jit(solution)/shard_map/all_to_all | solution.py:18
  331.1 14.9 %collective-permute-start.13 = (f32[2,64,56]{1,2,0:T(8,128)}, f32[2,64,56]{1,2,0:T(8,128)}, u32[]{:S(2)}, u32[]{:S(2)}) collective-permute-start(f32[2,64,56]{1,2,0:T(8,128)} %pad_maximum_fusion.8), channel_id=1, source_target_pairs={{448,384},{449,385},{450,386},{451,387},{452,388},{453,389},{454,3... | collective-permute-start | bytes 86024 | tf_op jit(solution)/shard_map/ppermute | solution.py:131
  333.0 13.7 %collective-permute-start.12 = (f32[2,64,56]{1,2,0:T(8,128)}, f32[2,64,56]{1,2,0:T(8,128)}, u32[]{:S(2)}, u32[]{:S(2)}) collective-permute-start(f32[2,64,56]{1,2,0:T(8,128)} %pad_maximum_fusion.7), channel_id=1, source_target_pairs={{448,320},{449,321},{450,322},{451,323},{452,324},{453,325},{454,3... | collective-permute-start | bytes 86024 | tf_op jit(solution)/shard_map/ppermute | solution.py:131
  334.3 20.7 %collective-permute-start.11 = (f32[2,64,56]{1,2,0:T(8,128)S(1)}, f32[2,64,56]{1,2,0:T(8,128)}, u32[]{:S(2)}, u32[]{:S(2)}) collective-permute-start(f32[2,64,56]{1,2,0:T(8,128)S(1)} %pad_maximum_fusion.6), channel_id=1, source_target_pairs={{448,256},{449,257},{450,258},{451,259},{452,260},{453,261},{454,2... | collective-permute-start | bytes 86024 | tf_op jit(solution)/shard_map/ppermute | solution.py:131
  335.6 19.5 %collective-permute-start.10 = (f32[2,64,56]{1,2,0:T(8,128)S(1)}, f32[2,64,56]{1,2,0:T(8,128)}, u32[]{:S(2)}, u32[]{:S(2)}) collective-permute-start(f32[2,64,56]{1,2,0:T(8,128)S(1)} %pad_maximum_fusion.5), channel_id=1, source_target_pairs={{448,192},{449,193},{450,194},{451,195},{452,196},{453,197},{454,1... | collective-permute-start | bytes 86024 | tf_op jit(solution)/shard_map/ppermute | solution.py:131
  336.9 18.2 %collective-permute-start.9 = (f32[2,64,56]{1,2,0:T(8,128)S(1)}, f32[2,64,56]{1,2,0:T(8,128)}, u32[]{:S(2)}, u32[]{:S(2)}) collective-permute-start(f32[2,64,56]{1,2,0:T(8,128)S(1)} %pad_maximum_fusion.4), channel_id=1, source_target_pairs={{448,128},{449,129},{450,130},{451,131},{452,132},{453,133},{454,1... | collective-permute-start | bytes 86024 | tf_op jit(solution)/shard_map/ppermute | solution.py:131
  346.7 35.5 %collective-permute-start.7 = (f32[2,64,56]{1,2,0:T(8,128)S(1)}, f32[2,64,56]{1,2,0:T(8,128)}, u32[]{:S(2)}, u32[]{:S(2)}) collective-permute-start(f32[2,64,56]{1,2,0:T(8,128)S(1)} %pad_maximum_fusion.2), channel_id=1, source_target_pairs={{448,0},{449,1},{450,2},{451,3},{452,4},{453,5},{454,6},{455,7},{4... | collective-permute-start | bytes 86024 | tf_op jit(solution)/shard_map/ppermute | solution.py:131
  382.2 91.6 %all-to-all-start.10 = ((bf16[512,2,3,449]{3,1,2,0:T(2,128)(2,1)}), bf16[512,2,3,449]{3,1,2,0:T(2,128)(2,1)S(1)}, u32[]{:S(2)}, u32[]{:S(2)}) async-start(bf16[512,2,3,449]{3,1,2,0:T(2,128)(2,1)} %pad_maximum_fusion), calls=%async_computation.10 | async-start | bytes 6291456 | tf_op jit(solution)/shard_map/all_to_all | solution.py:139
  473.9 24.5 %all-to-all-start.12 = ((bf16[64,2,1792]{2,1,0:T(2,128)(2,1)}), bf16[64,2,1792]{2,1,0:T(2,128)(2,1)}, u32[]{:S(2)}, u32[]{:S(2)}) async-start(bf16[64,2,1792]{2,1,0:T(2,128)(2,1)} %reshape.299), calls=%async_computation.12 | async-start | bytes 917504 | tf_op jit(solution)/shard_map/all_to_all | solution.py:18
  499.4 30.7 %all-to-all-start.11 = ((bf16[8,128,448]{1,2,0:T(8,128)(2,1)}), bf16[8,128,448]{1,2,0:T(8,128)(2,1)S(1)}, u32[]{:S(2)}, u32[]{:S(2)}) async-start(bf16[8,128,448]{1,2,0:T(8,128)(2,1)} %broadcast_in_dim.146), calls=%async_computation.11 | async-start | bytes 1835008 | tf_op jit(solution)/shard_map/all_to_all | solution.py:24
  (17 other events, 298.4 us)

commit v5 on v0

--- a/solution.py
+++ b/solution.py
@@ -73,13 +73,6 @@
         )
         * INVERSE_TEMP
     )
-    passage_sums = (
-        jnp.einsum(
-            "fnyw,fnj->wfyj", weight_matrices, query_row_items, preferred_element_type=jnp.float32
-        )
-        * INVERSE_TEMP
-    )
-    block_terms = passage_sums.reshape(row_block_count, requests, width).astype(jnp.bfloat16)
     micro_count = section_inputs.shape[1] // dp_count
     col_width = width // dp_count
     micro_cols = jnp.transpose(
@@ -87,8 +80,15 @@
     )
     section_count = lax.axis_size("section")
     chunk = width // section_count
-    term_pieces = passage_sums.reshape(dp_count, stripe, requests, section_count, chunk)
-    term_pieces = jnp.transpose(term_pieces, (3, 0, 1, 2, 4)).astype(jnp.bfloat16)
+    term_pieces = (
+        jnp.einsum(
+            "fnydr,fnsc->sdryc",
+            weight_matrices.reshape(blocks_here, row_block_count, slot_count, dp_count, stripe),
+            query_row_items.reshape(blocks_here, row_block_count, section_count, chunk),
+            preferred_element_type=jnp.float32,
+        )
+        * INVERSE_TEMP
+    ).astype(jnp.bfloat16)
     term_pieces = term_pieces.reshape(section_count * dp_count, stripe, requests, chunk)
     own_slots = lax.dynamic_slice_in_dim(all_slots, dp_index * requests, requests)
     slot_tags = jnp.broadcast_to(
@@ -111,8 +111,6 @@
         preferred_element_type=jnp.float32,
     )
     dense = dense.reshape(stripe, block_total, chunk).astype(jnp.bfloat16)
-    passage_out = gathered_columns(dense.reshape(stripe * block_total, chunk), "section")
-    passage_out = passage_out.reshape(stripe, block_total, width)
     entry = lax.all_to_all(carry_start, "dp", split_axis=0, concat_axis=1, tiled=True)
     weight_rows = section_weights[0]
     split_rows = weight_rows.reshape(col_width, dp_count, col_width)
@@ -142,6 +140,9 @@
         grad_weight = jnp.where(is_active, layer_weight, grad_weight)
         if section_turn + 1 < section_count:
             carry = passed_along(updated, "section", -1)
+    dense, grad_cols = lax.optimization_barrier((dense, grad_cols))
+    passage_out = gathered_columns(dense.reshape(stripe * block_total, chunk), "section")
+    passage_out = passage_out.reshape(stripe, block_total, width)
     return (
         query_sums.reshape(blocks_here * row_block_count, width).astype(jnp.bfloat16),
         passage_out,

time: 514 us -> 515 us (level)
  the two profiles are of different devices: /device:TPU:31 before, /device:TPU:6 now
where the time goes in v5:
time: 515 us; the launch traced here: 506 us
  waiting for transfers between devices  192 us (37%)
  blocking collectives  149 us (29%)
  starting transfers between devices  66.8 us (13%)
  local copies, waits for them, and re-layouts  60.4 us (12%)
  matrix products  28.3 us (5%)
  other arithmetic  8.27 us (2%)
    all_to_all x6, blocking collectives, gathered_pieces(): return lax.all_to_all(copies, axis, 0, 0, tiled=True)  133 us
    all_to_all x1, waiting for transfers between devices, body(): lax.all_to_all(term_pieces, ('section', 'dp'), split_axis=0, concat_axis=...  71.4 us
    all_to_all x1, waiting for transfers between devices, body(): lax.all_to_all(outgoing, 'dp', split_axis=1, concat_axis=0, tiled=True)  58.7 us
    ppermute x7, waiting for transfers between devices, passed_along(): lax.ppermute(value, axis, [(source, source + steps) for source in range(i...  26.6 us
    unnamed x74, local copies, waits for them, and re-layouts  22.5 us
    all_to_all x2, waiting for transfers between devices, gathered_pieces(): return lax.all_to_all(copies, axis, 0, 0, tiled=True)  21.6 us
    all_to_all x1, starting transfers between devices, body(): lax.all_to_all(term_pieces, ('section', 'dp'), split_axis=0, concat_axis=...  16.9 us
    all_to_all x1, blocking collectives, body(): lax.all_to_all(carry_start, 'dp', split_axis=0, concat_axis=1, tiled=True)  16.3 us
  transfers between devices with their start and end apart: 12, of which 11 were waited for; matrix products, arithmetic and copies ran while one was open for 7% of the time, Pallas kernels for 0%

profile of v5, /device:TPU:6, one launch (start us, length us, event | category | flops | bytes accessed | tf_op | source)
XLA Modules:
  0.0 506.2 jit_solution(14100216818781475970)
XLA Ops:
  7.1 14.2 %all-to-all-start = ((bf16[2,192,3584]{2,0,1:T(2,128)(2,1)}), bf16[2,192,3584]{2,0,1:T(2,128)(2,1)S(1)}, u32[]{:S(2)}, u32[]{:S(2)}) async-start(bf16[2,192,3584]{2,0,1:T(2,128)(2,1)} %copy.150), calls=%async_computation | async-start | bytes 5505024 | tf_op jit(solution)/shard_map/all_to_all | solution.py:50
  25.3 58.7 %all-to-all-done = bf16[2,192,3584]{2,0,1:T(2,128)(2,1)S(1)} async-done(((bf16[2,192,3584]{2,0,1:T(2,128)(2,1)}), bf16[2,192,3584]{2,0,1:T(2,128)(2,1)S(1)}, u32[]{:S(2)}, u32[]{:S(2)}) %all-to-all-start) | async-done | bytes 2752544 | tf_op jit(solution)/shard_map/all_to_all | solution.py:50
  87.5 5.8 %reshape.330 = bf16[128,3,3584]{2,0,1:T(8,128)(2,1)S(1)} reshape(bf16[64,2,3,3584]{3,1,0,2:T(2,128)(2,1)} %copy.151) | data formatting | bytes 5505024 | tf_op jit(solution)/shard_map/reshape.5
  100.5 5.9 %pad_maximum_fusion = bf16[512,2,3,449]{3,1,2,0:T(2,128)(2,1)} fusion(bf16[512,2,3,1]{3,1,2,0:T(2,128)(2,1)S(1)} %broadcast_in_dim.133, bf16[512,2,3,448]{3,1,2,0:T(2,128)(2,1)S(1)} %copy.156), kind=kLoop, calls=%fused_computation.5 | loop fusion | flops 5517312 | bytes 5517312 | tf_op jit(solution)/shard_map/concatenate | solution.py:98
  106.4 16.9 %all-to-all-start.1 = ((bf16[512,2,3,449]{3,1,2,0:T(2,128)(2,1)}), bf16[512,2,3,449]{3,1,2,0:T(2,128)(2,1)}, u32[]{:S(2)}, u32[]{:S(2)}) async-start(bf16[512,2,3,449]{3,1,2,0:T(2,128)(2,1)} %pad_maximum_fusion), calls=%async_computation.1 | async-start | bytes 6291456 | tf_op jit(solution)/shard_map/all_to_all | solution.py:99
  125.1 71.4 %all-to-all-done.1 = bf16[512,2,3,449]{3,1,2,0:T(2,128)(2,1)} async-done(((bf16[512,2,3,449]{3,1,2,0:T(2,128)(2,1)}), bf16[512,2,3,449]{3,1,2,0:T(2,128)(2,1)}, u32[]{:S(2)}, u32[]{:S(2)}) %all-to-all-start.1) | async-done | bytes 2758688 | tf_op jit(solution)/shard_map/all_to_all | solution.py:99
  196.5 16.3 %all_to_all.74 = f32[64,1,56]{2,1,0:T(1,128)S(1)} all-to-all(f32[64,1,56]{2,1,0:T(1,128)S(1)} %bitcast.240), channel_id=1, replica_groups=mesh['section'=8,'dp'=64] {'dp'}, dimensions={0} | all-to-all | bytes 28672 | tf_op jit(solution)/shard_map/all_to_all | solution.py:114
  214.4 6.6 %all-to-all-start.3 = ((bf16[64,2,1792]{2,1,0:T(2,128)(2,1)}), bf16[64,2,1792]{2,1,0:T(2,128)(2,1)S(1)}, u32[]{:S(2)}, u32[]{:S(2)}) async-start(bf16[64,2,1792]{2,1,0:T(2,128)(2,1)} %reshape.373), calls=%async_computation.3 | async-start | bytes 917504 | tf_op jit(solution)/shard_map/all_to_all | solution.py:18
  222.8 13.5 %all-to-all-done.3 = bf16[64,2,1792]{2,1,0:T(2,128)(2,1)S(1)} async-done(((bf16[64,2,1792]{2,1,0:T(2,128)(2,1)}), bf16[64,2,1792]{2,1,0:T(2,128)(2,1)S(1)}, u32[]{:S(2)}, u32[]{:S(2)}) %all-to-all-start.3) | async-done | bytes 458784 | tf_op jit(solution)/shard_map/all_to_all | solution.py:18
  239.1 4.5 collective-permute-done
  244.3 22.0 %all_to_all.75 = bf16[64,2,1792]{2,1,0:T(2,128)(2,1)S(1)} all-to-all(bf16[64,2,1792]{2,1,0:T(2,128)(2,1)S(1)} %reshape.375), channel_id=1, replica_groups=mesh['section'=8,'dp'=64] {'dp'}, dimensions={0} | all-to-all | bytes 917504 | tf_op jit(solution)/shard_map/all_to_all | solution.py:18
  274.2 22.1 %all_to_all.76 = bf16[64,2,1792]{2,1,0:T(2,128)(2,1)} all-to-all(bf16[64,2,1792]{2,1,0:T(2,128)(2,1)S(1)} %reshape.377), channel_id=1, replica_groups=mesh['section'=8,'dp'=64] {'dp'}, dimensions={0} | all-to-all | bytes 917504 | tf_op jit(solution)/shard_map/all_to_all | solution.py:18
  300.6 4.5 collective-permute-done.2
  305.8 22.1 %all_to_all.77 = bf16[64,2,1792]{2,1,0:T(2,128)(2,1)} all-to-all(bf16[64,2,1792]{2,1,0:T(2,128)(2,1)S(1)} %reshape.379), channel_id=1, replica_groups=mesh['section'=8,'dp'=64] {'dp'}, dimensions={0} | all-to-all | bytes 917504 | tf_op jit(solution)/shard_map/all_to_all | solution.py:18
  332.2 4.5 collective-permute-done.3
  337.4 22.1 %all_to_all.78 = bf16[64,2,1792]{2,1,0:T(2,128)(2,1)} all-to-all(bf16[64,2,1792]{2,1,0:T(2,128)(2,1)S(1)} %reshape.381), channel_id=1, replica_groups=mesh['section'=8,'dp'=64] {'dp'}, dimensions={0} | all-to-all | bytes 917504 | tf_op jit(solution)/shard_map/all_to_all | solution.py:18
  363.8 4.5 collective-permute-done.4
  369.0 22.3 %all_to_all.79 = bf16[64,2,1792]{2,1,0:T(2,128)(2,1)} all-to-all(bf16[64,2,1792]{2,1,0:T(2,128)(2,1)S(1)} %reshape.383), channel_id=1, replica_groups=mesh['section'=8,'dp'=64] {'dp'}, dimensions={0} | all-to-all | bytes 917504 | tf_op jit(solution)/shard_map/all_to_all | solution.py:18
  400.8 22.1 %all_to_all.80 = bf16[64,2,1792]{2,1,0:T(2,128)(2,1)} all-to-all(bf16[64,2,1792]{2,1,0:T(2,128)(2,1)S(1)} %reshape.385), channel_id=1, replica_groups=mesh['section'=8,'dp'=64] {'dp'}, dimensions={0} | all-to-all | bytes 917504 | tf_op jit(solution)/shard_map/all_to_all | solution.py:18
  427.3 8.7 %copy.157 = bf16[512,2,3,449]{0,3,2,1:T(8,128)(2,1)} copy(bf16[512,2,3,449]{3,1,2,0:T(2,128)(2,1)} %all-to-all-done.1) | data formatting | bytes 5517312 | tf_op jit(solution)/shard_map/optimization_barrier | solution.py:102
  437.5 6.8 %all-to-all-start.10 = ((bf16[64,2,1792]{2,1,0:T(2,128)(2,1)}), bf16[64,2,1792]{2,1,0:T(2,128)(2,1)S(1)}, u32[]{:S(2)}, u32[]{:S(2)}) async-start(bf16[64,2,1792]{2,1,0:T(2,128)(2,1)} %reshape.387), calls=%async_computation.10 | async-start | bytes 917504 | tf_op jit(solution)/shard_map/all_to_all | solution.py:18
  451.7 8.0 %all-to-all-done.10 = bf16[64,2,1792]{2,1,0:T(2,128)(2,1)S(1)} async-done(((bf16[64,2,1792]{2,1,0:T(2,128)(2,1)}), bf16[64,2,1792]{2,1,0:T(2,128)(2,1)S(1)}, u32[]{:S(2)}, u32[]{:S(2)}) %all-to-all-start.10) | async-done | bytes 458784 | tf_op jit(solution)/shard_map/all_to_all | solution.py:18
  463.0 13.1 %all-to-all-start.11 = ((bf16[8,128,448]{1,2,0:T(8,128)(2,1)}), bf16[8,128,448]{1,2,0:T(8,128)(2,1)S(1)}, u32[]{:S(2)}, u32[]{:S(2)}) async-start(bf16[8,128,448]{1,2,0:T(8,128)(2,1)} %broadcast_in_dim.145), calls=%async_computation.11 | async-start | bytes 1835008 | tf_op jit(solution)/shard_map/all_to_all | solution.py:24
  489.4 13.3 %all-to-all-done.11 = bf16[8,128,448]{1,2,0:T(8,128)(2,1)S(1)} async-done(((bf16[8,128,448]{1,2,0:T(8,128)(2,1)}), bf16[8,128,448]{1,2,0:T(8,128)(2,1)S(1)}, u32[]{:S(2)}, u32[]{:S(2)}) %all-to-all-start.11) | async-done | bytes 917536 | tf_op jit(solution)/shard_map/all_to_all | solution.py:24
  (137 shorter events, 94.6 us)
Async XLA Ops:
  7.1 14.2 %copy-start.19 = (f32[128,384]{1,0:T(8,128)S(1)}, f32[128,384]{1,0:T(8,128)}, u32[]{:S(2)}) copy-start(f32[128,384]{1,0:T(8,128)} %param.12) | copy-start | bytes 589828
  7.1 16.5 %copy-start.22 = (s32[64]{0:T(128)S(1)}, s32[64]{0:T(128)}, u32[]{:S(2)}) copy-start(s32[64]{0:T(128)} %param.11) | copy-start | bytes 772
  7.1 76.9 %all-to-all-start = ((bf16[2,192,3584]{2,0,1:T(2,128)(2,1)}), bf16[2,192,3584]{2,0,1:T(2,128)(2,1)S(1)}, u32[]{:S(2)}, u32[]{:S(2)}) async-start(bf16[2,192,3584]{2,0,1:T(2,128)(2,1)} %copy.150), calls=%async_computation | async-start | bytes 5505024 | tf_op jit(solution)/shard_map/all_to_all | solution.py:50
  106.4 90.1 %all-to-all-start.1 = ((bf16[512,2,3,449]{3,1,2,0:T(2,128)(2,1)}), bf16[512,2,3,449]{3,1,2,0:T(2,128)(2,1)}, u32[]{:S(2)}, u32[]{:S(2)}) async-start(bf16[512,2,3,449]{3,1,2,0:T(2,128)(2,1)} %pad_maximum_fusion), calls=%async_computation.1 | async-start | bytes 6291456 | tf_op jit(solution)/shard_map/all_to_all | solution.py:99
  123.4 89.5 %copy-start.12 = (bf16[1,64,56]{1,2,0:T(8,128)(2,1)S(1)}, bf16[1,64,56]{1,2,0:T(8,128)(2,1)}, u32[]{:S(2)}) copy-start(bf16[1,64,56]{1,2,0:T(8,128)(2,1)} %param.15) | copy-start | bytes 21508
  125.0 95.9 %copy-start.18 = (bf16[1,56,3584]{2,1,0:T(8,128)(2,1)S(1)}, bf16[1,56,3584]{2,1,0:T(8,128)(2,1)}, u32[]{:S(2)}) copy-start(bf16[1,56,3584]{2,1,0:T(8,128)(2,1)} %param.13) | copy-start | bytes 1204228
  214.4 22.0 %all-to-all-start.3 = ((bf16[64,2,1792]{2,1,0:T(2,128)(2,1)}), bf16[64,2,1792]{2,1,0:T(2,128)(2,1)S(1)}, u32[]{:S(2)}, u32[]{:S(2)}) async-start(bf16[64,2,1792]{2,1,0:T(2,128)(2,1)} %reshape.373), calls=%async_computation.3 | async-start | bytes 917504 | tf_op jit(solution)/shard_map/all_to_all | solution.py:18
  236.9 6.7 %copy-start.13 = (bf16[64,56,64]{2,1,0:T(8,128)(2,1)}, bf16[64,56,64]{2,1,0:T(8,128)(2,1)S(1)}, u32[]{:S(2)}) copy-start(bf16[64,56,64]{2,1,0:T(8,128)(2,1)S(1)} %reshape.374) | copy-start | bytes 1376260
  237.8 5.8 %collective-permute-start = (f32[64,56]{0,1:T(8,128)S(1)}, f32[64,56]{0,1:T(8,128)S(1)}, u32[]{:S(2)}, u32[]{:S(2)}) collective-permute-start(f32[64,56]{0,1:T(8,128)S(1)} %fusion.14), channel_id=1, source_target_pairs={{64,0},{128,64},{192,128},{256,192},{320,256},{384,320},{448,384},... | collective-permute-start | bytes 43016 | tf_op jit(solution)/shard_map/ppermute | solution.py:12
  267.7 5.8 %collective-permute-start.1 = (f32[64,56]{0,1:T(8,128)S(1)}, f32[64,56]{0,1:T(8,128)S(1)}, u32[]{:S(2)}, u32[]{:S(2)}) collective-permute-start(f32[64,56]{0,1:T(8,128)S(1)} %fusion.15), channel_id=1, source_target_pairs={{64,0},{128,64},{192,128},{256,192},{320,256},{384,320},{448,384},... | collective-permute-start | bytes 43016 | tf_op jit(solution)/shard_map/ppermute | solution.py:12
  299.3 5.8 %collective-permute-start.2 = (f32[64,56]{0,1:T(8,128)S(1)}, f32[64,56]{0,1:T(8,128)S(1)}, u32[]{:S(2)}, u32[]{:S(2)}) collective-permute-start(f32[64,56]{0,1:T(8,128)S(1)} %fusion.16), channel_id=1, source_target_pairs={{64,0},{128,64},{192,128},{256,192},{320,256},{384,320},{448,384},... | collective-permute-start | bytes 43016 | tf_op jit(solution)/shard_map/ppermute | solution.py:12
  330.9 5.8 %collective-permute-start.3 = (f32[64,56]{0,1:T(8,128)S(1)}, f32[64,56]{0,1:T(8,128)S(1)}, u32[]{:S(2)}, u32[]{:S(2)}) collective-permute-start(f32[64,56]{0,1:T(8,128)S(1)} %fusion.17), channel_id=1, source_target_pairs={{64,0},{128,64},{192,128},{256,192},{320,256},{384,320},{448,384},... | collective-permute-start | bytes 43016 | tf_op jit(solution)/shard_map/ppermute | solution.py:12
  362.5 5.8 %collective-permute-start.4 = (f32[64,56]{0,1:T(8,128)S(1)}, f32[64,56]{0,1:T(8,128)S(1)}, u32[]{:S(2)}, u32[]{:S(2)}) collective-permute-start(f32[64,56]{0,1:T(8,128)S(1)} %fusion.18), channel_id=1, source_target_pairs={{64,0},{128,64},{192,128},{256,192},{320,256},{384,320},{448,384},... | collective-permute-start | bytes 43016 | tf_op jit(solution)/shard_map/ppermute | solution.py:12
  393.4 6.7 %copy-start.7 = (bf16[64,56,64]{2,1,0:T(8,128)(2,1)}, bf16[64,56,64]{2,1,0:T(8,128)(2,1)S(1)}, u32[]{:S(2)}) copy-start(bf16[64,56,64]{2,1,0:T(8,128)(2,1)S(1)} %reshape.384) | copy-start | bytes 1376260
  394.3 31.6 %copy-start.20 = (f32[64,56]{0,1:T(8,128)}, f32[64,56]{0,1:T(8,128)S(1)}, u32[]{:S(2)}) copy-start(f32[64,56]{0,1:T(8,128)S(1)} %fusion.19) | copy-start | bytes 43012
  394.3 5.8 %collective-permute-start.5 = (f32[64,56]{0,1:T(8,128)S(1)}, f32[64,56]{0,1:T(8,128)S(1)}, u32[]{:S(2)}, u32[]{:S(2)}) collective-permute-start(f32[64,56]{0,1:T(8,128)S(1)} %fusion.19), channel_id=1, source_target_pairs={{64,0},{128,64},{192,128},{256,192},{320,256},{384,320},{448,384},... | collective-permute-start | bytes 43016 | tf_op jit(solution)/shard_map/ppermute | solution.py:12
  425.0 10.9 %copy-start.9 = (bf16[64,56,64]{2,1,0:T(8,128)(2,1)}, bf16[64,56,64]{2,1,0:T(8,128)(2,1)S(1)}, u32[]{:S(2)}) copy-start(bf16[64,56,64]{2,1,0:T(8,128)(2,1)S(1)} %reshape.386) | copy-start | bytes 1376260
  425.9 10.0 %copy-start.21 = (f32[64,56]{0,1:T(8,128)}, f32[64,56]{0,1:T(8,128)S(1)}, u32[]{:S(2)}) copy-start(f32[64,56]{0,1:T(8,128)S(1)} %fusion.20) | copy-start | bytes 43012
  426.0 10.0 %collective-permute-start.6 = (f32[64,56]{0,1:T(8,128)S(1)}, f32[64,56]{0,1:T(8,128)S(1)}, u32[]{:S(2)}, u32[]{:S(2)}) collective-permute-start(f32[64,56]{0,1:T(8,128)S(1)} %fusion.20), channel_id=1, source_target_pairs={{64,0},{128,64},{192,128},{256,192},{320,256},{384,320},{448,384},... | collective-permute-start | bytes 43016 | tf_op jit(solution)/shard_map/ppermute | solution.py:12
  436.1 11.7 %copy-start.17 = (bf16[1,64,56]{1,2,0:T(8,128)(2,1)S(1)}, bf16[1,64,56]{1,2,0:T(8,128)(2,1)}, u32[]{:S(2)}) copy-start(bf16[1,64,56]{1,2,0:T(8,128)(2,1)} %param.14) | copy-start | bytes 21508
  437.5 22.2 %all-to-all-start.10 = ((bf16[64,2,1792]{2,1,0:T(2,128)(2,1)}), bf16[64,2,1792]{2,1,0:T(2,128)(2,1)S(1)}, u32[]{:S(2)}, u32[]{:S(2)}) async-start(bf16[64,2,1792]{2,1,0:T(2,128)(2,1)} %reshape.387), calls=%async_computation.10 | async-start | bytes 917504 | tf_op jit(solution)/shard_map/all_to_all | solution.py:18
  461.8 14.3 %copy-start.3 = (bf16[64,56,64]{2,1,0:T(8,128)(2,1)S(1)}, bf16[64,56,64]{2,1,0:T(8,128)(2,1)}, u32[]{:S(2)}) copy-start(bf16[64,56,64]{2,1,0:T(8,128)(2,1)} %copy-done.2) | copy-start | bytes 1376260
  463.0 39.7 %all-to-all-start.11 = ((bf16[8,128,448]{1,2,0:T(8,128)(2,1)}), bf16[8,128,448]{1,2,0:T(8,128)(2,1)S(1)}, u32[]{:S(2)}, u32[]{:S(2)}) async-start(bf16[8,128,448]{1,2,0:T(8,128)(2,1)} %broadcast_in_dim.145), calls=%async_computation.11 | async-start | bytes 1835008 | tf_op jit(solution)/shard_map/all_to_all | solution.py:24
  484.6 21.2 %copy-start.1 = (bf16[2,64,3584]{2,1,0:T(8,128)(2,1)S(1)}, bf16[2,64,3584]{2,1,0:T(8,128)(2,1)}, u32[]{:S(2)}) copy-start(bf16[2,64,3584]{2,1,0:T(8,128)(2,1)} %param.9) | copy-start | bytes 2752516
  (11 other events, 45.7 us)

commit v6 on v5

--- a/solution.py
+++ b/solution.py
@@ -111,6 +111,8 @@
         preferred_element_type=jnp.float32,
     )
     dense = dense.reshape(stripe, block_total, chunk).astype(jnp.bfloat16)
+    passage_out = gathered_columns(dense.reshape(stripe * block_total, chunk), "section")
+    passage_out = passage_out.reshape(stripe, block_total, width)
     entry = lax.all_to_all(carry_start, "dp", split_axis=0, concat_axis=1, tiled=True)
     weight_rows = section_weights[0]
     split_rows = weight_rows.reshape(col_width, dp_count, col_width)
@@ -140,9 +142,6 @@
         grad_weight = jnp.where(is_active, layer_weight, grad_weight)
         if section_turn + 1 < section_count:
             carry = passed_along(updated, "section", -1)
-    dense, grad_cols = lax.optimization_barrier((dense, grad_cols))
-    passage_out = gathered_columns(dense.reshape(stripe * block_total, chunk), "section")
-    passage_out = passage_out.reshape(stripe, block_total, width)
     return (
         query_sums.reshape(blocks_here * row_block_count, width).astype(jnp.bfloat16),
         passage_out,

time: 515 us -> 499 us (0.969)
  blocking collectives: 149 us -> 104 us
  waiting for transfers between devices: 192 us -> 210 us
  starting transfers between devices: 66.8 us -> 76.2 us
    all_to_all x6 -> x4, blocking collectives: 133 us -> 88 us  [gathered_pieces(): return lax.all_to_all(copies, axis, 0, 0, tiled=True)]
    ppermute x7, waiting for transfers between devices: 26.6 us -> 45.2 us  [passed_along(): lax.ppermute(value, axis, [(source, source + steps) for source in range(i...]
    all_to_all x2 -> x4, starting transfers between devices: 13.4 us -> 27.5 us  [gathered_pieces(): return lax.all_to_all(copies, axis, 0, 0, tiled=True)]
    all_to_all x1, waiting for transfers between devices: 13.3 us -> 1.79 us  [gathered_columns(): pieces = lax.all_to_all(copies, axis, 0, 0, tiled=True)]
    all_to_all x2 -> x4, waiting for transfers between devices: 21.6 us -> 32.5 us  [gathered_pieces(): return lax.all_to_all(copies, axis, 0, 0, tiled=True)]
    unnamed x74 -> x86, local copies, waits for them, and re-layouts: 22.5 us -> 17.3 us
  transfers between devices with their start and end apart: 12 -> 14, of which waited for: 11 -> 14; matrix products, arithmetic and copies ran while one was open for 7% -> 8% of each run, Pallas kernels for 0% -> 0%
where the time goes in v6:
time: 499 us; the launch traced here: 490 us
  waiting for transfers between devices  210 us (42%)
  blocking collectives  104 us (21%)
  starting transfers between devices  76.2 us (15%)
  local copies, waits for them, and re-layouts  56.2 us (11%)
  matrix products  33.1 us (7%)
  other arithmetic  8.21 us (2%)
    all_to_all x4, blocking collectives, gathered_pieces(): return lax.all_to_all(copies, axis, 0, 0, tiled=True)  88 us
    all_to_all x1, waiting for transfers between devices, body(): lax.all_to_all(term_pieces, ('section', 'dp'), split_axis=0, concat_axis=...  71.4 us
    all_to_all x1, waiting for transfers between devices, body(): lax.all_to_all(outgoing, 'dp', split_axis=1, concat_axis=0, tiled=True)  58.7 us
    ppermute x7, waiting for transfers between devices, passed_along(): lax.ppermute(value, axis, [(source, source + steps) for source in range(i...  45.2 us
    all_to_all x4, waiting for transfers between devices, gathered_pieces(): return lax.all_to_all(copies, axis, 0, 0, tiled=True)  32.5 us
    all_to_all x4, starting transfers between devices, gathered_pieces(): return lax.all_to_all(copies, axis, 0, 0, tiled=True)  27.5 us
    unnamed x86, local copies, waits for them, and re-layouts  17.3 us
    all_to_all x1, starting transfers between devices, body(): lax.all_to_all(term_pieces, ('section', 'dp'), split_axis=0, concat_axis=...  16.9 us
  transfers between devices with their start and end apart: 14, of which 14 were waited for; matrix products, arithmetic and copies ran while one was open for 8% of the time, Pallas kernels for 0%

profile of v6, /device:TPU:6, one launch (start us, length us, event | category | flops | bytes accessed | tf_op | source)
XLA Modules:
  0.0 489.5 jit_solution(9938988017851202764)
XLA Ops:
  7.1 14.1 %all-to-all-start = ((bf16[2,192,3584]{2,0,1:T(2,128)(2,1)}), bf16[2,192,3584]{2,0,1:T(2,128)(2,1)S(1)}, u32[]{:S(2)}, u32[]{:S(2)}) async-start(bf16[2,192,3584]{2,0,1:T(2,128)(2,1)} %copy.150), calls=%async_computation | async-start | bytes 5505024 | tf_op jit(solution)/shard_map/all_to_all | solution.py:50
  25.3 58.7 %all-to-all-done = bf16[2,192,3584]{2,0,1:T(2,128)(2,1)S(1)} async-done(((bf16[2,192,3584]{2,0,1:T(2,128)(2,1)}), bf16[2,192,3584]{2,0,1:T(2,128)(2,1)S(1)}, u32[]{:S(2)}, u32[]{:S(2)}) %all-to-all-start) | async-done | bytes 2752544 | tf_op jit(solution)/shard_map/all_to_all | solution.py:50
  87.5 5.8 %reshape.330 = bf16[128,3,3584]{2,0,1:T(8,128)(2,1)S(1)} reshape(bf16[64,2,3,3584]{3,1,0,2:T(2,128)(2,1)} %copy.151) | data formatting | bytes 5505024 | tf_op jit(solution)/shard_map/reshape.5
  100.5 5.9 %pad_maximum_fusion = bf16[512,2,3,449]{3,1,2,0:T(2,128)(2,1)} fusion(bf16[512,2,3,1]{3,1,2,0:T(2,128)(2,1)S(1)} %broadcast_in_dim.133, bf16[512,2,3,448]{3,1,2,0:T(2,128)(2,1)S(1)} %copy.156), kind=kLoop, calls=%fused_computation.5 | loop fusion | flops 5517312 | bytes 5517312 | tf_op jit(solution)/shard_map/concatenate | solution.py:98
  106.4 16.9 %all-to-all-start.1 = ((bf16[512,2,3,449]{3,1,2,0:T(2,128)(2,1)}), bf16[512,2,3,449]{3,1,2,0:T(2,128)(2,1)}, u32[]{:S(2)}, u32[]{:S(2)}) async-start(bf16[512,2,3,449]{3,1,2,0:T(2,128)(2,1)} %pad_maximum_fusion), calls=%async_computation.1 | async-start | bytes 6291456 | tf_op jit(solution)/shard_map/all_to_all | solution.py:99
  125.1 71.4 %all-to-all-done.1 = bf16[512,2,3,449]{3,1,2,0:T(2,128)(2,1)} async-done(((bf16[512,2,3,449]{3,1,2,0:T(2,128)(2,1)}), bf16[512,2,3,449]{3,1,2,0:T(2,128)(2,1)}, u32[]{:S(2)}, u32[]{:S(2)}) %all-to-all-start.1) | async-done | bytes 2758688 | tf_op jit(solution)/shard_map/all_to_all | solution.py:99
  196.5 16.3 %all_to_all.74 = f32[64,1,56]{2,1,0:T(1,128)S(1)} all-to-all(f32[64,1,56]{2,1,0:T(1,128)S(1)} %bitcast.241), channel_id=1, replica_groups=mesh['section'=8,'dp'=64] {'dp'}, dimensions={0} | all-to-all | bytes 28672 | tf_op jit(solution)/shard_map/all_to_all | solution.py:116
  214.3 6.6 %all-to-all-start.4 = ((bf16[64,2,1792]{2,1,0:T(2,128)(2,1)}), bf16[64,2,1792]{2,1,0:T(2,128)(2,1)S(1)}, u32[]{:S(2)}, u32[]{:S(2)}) async-start(bf16[64,2,1792]{2,1,0:T(2,128)(2,1)} %reshape.373), calls=%async_computation.4 | async-start | bytes 917504 | tf_op jit(solution)/shard_map/all_to_all | solution.py:18
  222.8 13.5 %all-to-all-done.4 = bf16[64,2,1792]{2,1,0:T(2,128)(2,1)S(1)} async-done(((bf16[64,2,1792]{2,1,0:T(2,128)(2,1)}), bf16[64,2,1792]{2,1,0:T(2,128)(2,1)S(1)}, u32[]{:S(2)}, u32[]{:S(2)}) %all-to-all-start.4) | async-done | bytes 458784 | tf_op jit(solution)/shard_map/all_to_all | solution.py:18
  239.1 4.5 collective-permute-done
  244.3 22.0 %all_to_all.75 = bf16[64,2,1792]{2,1,0:T(2,128)(2,1)S(1)} all-to-all(bf16[64,2,1792]{2,1,0:T(2,128)(2,1)S(1)} %reshape.375), channel_id=1, replica_groups=mesh['section'=8,'dp'=64] {'dp'}, dimensions={0} | all-to-all | bytes 917504 | tf_op jit(solution)/shard_map/all_to_all | solution.py:18
  274.2 22.0 %all_to_all.76 = bf16[64,2,1792]{2,1,0:T(2,128)(2,1)S(1)} all-to-all(bf16[64,2,1792]{2,1,0:T(2,128)(2,1)S(1)} %reshape.377), channel_id=1, replica_groups=mesh['section'=8,'dp'=64] {'dp'}, dimensions={0} | all-to-all | bytes 917504 | tf_op jit(solution)/shard_map/all_to_all | solution.py:18
  299.0 4.5 collective-permute-done.2
  304.2 22.0 %all_to_all.77 = bf16[64,2,1792]{2,1,0:T(2,128)(2,1)S(1)} all-to-all(bf16[64,2,1792]{2,1,0:T(2,128)(2,1)S(1)} %reshape.379), channel_id=1, replica_groups=mesh['section'=8,'dp'=64] {'dp'}, dimensions={0} | all-to-all | bytes 917504 | tf_op jit(solution)/shard_map/all_to_all | solution.py:18
  329.0 4.5 collective-permute-done.3
  334.1 22.0 %all_to_all.78 = bf16[64,2,1792]{2,1,0:T(2,128)(2,1)S(1)} all-to-all(bf16[64,2,1792]{2,1,0:T(2,128)(2,1)S(1)} %reshape.381), channel_id=1, replica_groups=mesh['section'=8,'dp'=64] {'dp'}, dimensions={0} | all-to-all | bytes 917504 | tf_op jit(solution)/shard_map/all_to_all | solution.py:18
  364.9 6.8 %all-to-all-start.9 = ((bf16[64,2,1792]{2,1,0:T(2,128)(2,1)}), bf16[64,2,1792]{2,1,0:T(2,128)(2,1)S(1)}, u32[]{:S(2)}, u32[]{:S(2)}) async-start(bf16[64,2,1792]{2,1,0:T(2,128)(2,1)} %reshape.383), calls=%async_computation.9 | async-start | bytes 917504 | tf_op jit(solution)/shard_map/all_to_all | solution.py:18
  371.7 8.7 %copy.157 = bf16[512,2,3,449]{0,3,2,1:T(8,128)(2,1)} copy(bf16[512,2,3,449]{3,1,2,0:T(2,128)(2,1)} %all-to-all-done.1) | data formatting | bytes 5517312 | tf_op jit(solution)/shard_map/optimization_barrier | solution.py:102
  388.1 8.3 %all-to-all-start.2 = ((bf16[8,128,448]{1,2,0:T(8,128)(2,1)}), bf16[8,128,448]{1,2,0:T(8,128)(2,1)S(1)}, u32[]{:S(2)}, u32[]{:S(2)}) async-start(bf16[8,128,448]{1,2,0:T(8,128)(2,1)} %broadcast_in_dim.135), calls=%async_computation.2 | async-start | bytes 1835008 | tf_op jit(solution)/shard_map/all_to_all | solution.py:24
  399.2 20.5 %collective-permute-done.5 = f32[64,56]{0,1:T(8,128)S(1)} collective-permute-done((f32[64,56]{0,1:T(8,128)S(1)}, f32[64,56]{0,1:T(8,128)S(1)}, u32[]{:S(2)}, u32[]{:S(2)}) %collective-permute-start.5) | collective-permute-done | bytes 14368 | tf_op jit(solution)/shard_map/ppermute | solution.py:12
  423.0 6.8 %all-to-all-start.10 = ((bf16[64,2,1792]{2,1,0:T(2,128)(2,1)}), bf16[64,2,1792]{2,1,0:T(2,128)(2,1)S(1)}, u32[]{:S(2)}, u32[]{:S(2)}) async-start(bf16[64,2,1792]{2,1,0:T(2,128)(2,1)} %reshape.385), calls=%async_computation.10 | async-start | bytes 917504 | tf_op jit(solution)/shard_map/all_to_all | solution.py:18
  437.0 8.3 %all-to-all-done.10 = bf16[64,2,1792]{2,1,0:T(2,128)(2,1)S(1)} async-done(((bf16[64,2,1792]{2,1,0:T(2,128)(2,1)}), bf16[64,2,1792]{2,1,0:T(2,128)(2,1)S(1)}, u32[]{:S(2)}, u32[]{:S(2)}) %all-to-all-start.10) | async-done | bytes 458784 | tf_op jit(solution)/shard_map/all_to_all | solution.py:18
  455.1 7.3 %all-to-all-start.11 = ((bf16[64,2,1792]{2,1,0:T(2,128)(2,1)}), bf16[64,2,1792]{2,1,0:T(2,128)(2,1)S(1)}, u32[]{:S(2)}, u32[]{:S(2)}) async-start(bf16[64,2,1792]{2,1,0:T(2,128)(2,1)} %reshape.387), calls=%async_computation.11 | async-start | bytes 917504 | tf_op jit(solution)/shard_map/all_to_all | solution.py:18
  470.0 7.6 %all-to-all-done.11 = bf16[64,2,1792]{2,1,0:T(2,128)(2,1)S(1)} async-done(((bf16[64,2,1792]{2,1,0:T(2,128)(2,1)}), bf16[64,2,1792]{2,1,0:T(2,128)(2,1)S(1)}, u32[]{:S(2)}, u32[]{:S(2)}) %all-to-all-start.11) | async-done | bytes 458784 | tf_op jit(solution)/shard_map/all_to_all | solution.py:18
  (151 shorter events, 102.7 us)
Async XLA Ops:
  7.1 14.2 %copy-start.19 = (f32[128,384]{1,0:T(8,128)S(1)}, f32[128,384]{1,0:T(8,128)}, u32[]{:S(2)}) copy-start(f32[128,384]{1,0:T(8,128)} %param.12) | copy-start | bytes 589828
  7.1 16.5 %copy-start.28 = (s32[64]{0:T(128)S(1)}, s32[64]{0:T(128)}, u32[]{:S(2)}) copy-start(s32[64]{0:T(128)} %param.11) | copy-start | bytes 772
  7.1 76.9 %all-to-all-start = ((bf16[2,192,3584]{2,0,1:T(2,128)(2,1)}), bf16[2,192,3584]{2,0,1:T(2,128)(2,1)S(1)}, u32[]{:S(2)}, u32[]{:S(2)}) async-start(bf16[2,192,3584]{2,0,1:T(2,128)(2,1)} %copy.150), calls=%async_computation | async-start | bytes 5505024 | tf_op jit(solution)/shard_map/all_to_all | solution.py:50
  106.4 90.1 %all-to-all-start.1 = ((bf16[512,2,3,449]{3,1,2,0:T(2,128)(2,1)}), bf16[512,2,3,449]{3,1,2,0:T(2,128)(2,1)}, u32[]{:S(2)}, u32[]{:S(2)}) async-start(bf16[512,2,3,449]{3,1,2,0:T(2,128)(2,1)} %pad_maximum_fusion), calls=%async_computation.1 | async-start | bytes 6291456 | tf_op jit(solution)/shard_map/all_to_all | solution.py:99
  123.4 89.5 %copy-start.15 = (bf16[1,64,56]{1,2,0:T(8,128)(2,1)S(1)}, bf16[1,64,56]{1,2,0:T(8,128)(2,1)}, u32[]{:S(2)}) copy-start(bf16[1,64,56]{1,2,0:T(8,128)(2,1)} %param.15) | copy-start | bytes 21508
  125.0 95.9 %copy-start.18 = (bf16[1,56,3584]{2,1,0:T(8,128)(2,1)S(1)}, bf16[1,56,3584]{2,1,0:T(8,128)(2,1)}, u32[]{:S(2)}) copy-start(bf16[1,56,3584]{2,1,0:T(8,128)(2,1)} %param.13) | copy-start | bytes 1204228
  214.3 22.0 %all-to-all-start.4 = ((bf16[64,2,1792]{2,1,0:T(2,128)(2,1)}), bf16[64,2,1792]{2,1,0:T(2,128)(2,1)S(1)}, u32[]{:S(2)}, u32[]{:S(2)}) async-start(bf16[64,2,1792]{2,1,0:T(2,128)(2,1)} %reshape.373), calls=%async_computation.4 | async-start | bytes 917504 | tf_op jit(solution)/shard_map/all_to_all | solution.py:18
  237.8 30.0 %copy-start.21 = (f32[64,56]{0,1:T(8,128)}, f32[64,56]{0,1:T(8,128)S(1)}, u32[]{:S(2)}) copy-start(f32[64,56]{0,1:T(8,128)S(1)} %fusion.11) | copy-start | bytes 43012
  237.8 5.8 %collective-permute-start = (f32[64,56]{0,1:T(8,128)S(1)}, f32[64,56]{0,1:T(8,128)S(1)}, u32[]{:S(2)}, u32[]{:S(2)}) collective-permute-start(f32[64,56]{0,1:T(8,128)S(1)} %fusion.11), channel_id=1, source_target_pairs={{64,0},{128,64},{192,128},{256,192},{320,256},{384,320},{448,384},... | collective-permute-start | bytes 43016 | tf_op jit(solution)/shard_map/ppermute | solution.py:12
  267.7 5.8 %collective-permute-start.1 = (f32[64,56]{0,1:T(8,128)S(1)}, f32[64,56]{0,1:T(8,128)S(1)}, u32[]{:S(2)}, u32[]{:S(2)}) collective-permute-start(f32[64,56]{0,1:T(8,128)S(1)} %fusion.12), channel_id=1, source_target_pairs={{64,0},{128,64},{192,128},{256,192},{320,256},{384,320},{448,384},... | collective-permute-start | bytes 43016 | tf_op jit(solution)/shard_map/ppermute | solution.py:12
  297.7 5.8 %collective-permute-start.2 = (f32[64,56]{0,1:T(8,128)S(1)}, f32[64,56]{0,1:T(8,128)S(1)}, u32[]{:S(2)}, u32[]{:S(2)}) collective-permute-start(f32[64,56]{0,1:T(8,128)S(1)} %fusion.13), channel_id=1, source_target_pairs={{64,0},{128,64},{192,128},{256,192},{320,256},{384,320},{448,384},... | collective-permute-start | bytes 43016 | tf_op jit(solution)/shard_map/ppermute | solution.py:12
  327.6 5.8 %collective-permute-start.3 = (f32[64,56]{0,1:T(8,128)S(1)}, f32[64,56]{0,1:T(8,128)S(1)}, u32[]{:S(2)}, u32[]{:S(2)}) collective-permute-start(f32[64,56]{0,1:T(8,128)S(1)} %fusion.14), channel_id=1, source_target_pairs={{64,0},{128,64},{192,128},{256,192},{320,256},{384,320},{448,384},... | collective-permute-start | bytes 43016 | tf_op jit(solution)/shard_map/ppermute | solution.py:12
  357.6 5.8 %collective-permute-start.4 = (f32[64,56]{0,1:T(8,128)S(1)}, f32[64,56]{0,1:T(8,128)S(1)}, u32[]{:S(2)}, u32[]{:S(2)}) collective-permute-start(f32[64,56]{0,1:T(8,128)S(1)} %fusion.15), channel_id=1, source_target_pairs={{64,0},{128,64},{192,128},{256,192},{320,256},{384,320},{448,384},... | collective-permute-start | bytes 43016 | tf_op jit(solution)/shard_map/ppermute | solution.py:12
  364.9 22.2 %all-to-all-start.9 = ((bf16[64,2,1792]{2,1,0:T(2,128)(2,1)}), bf16[64,2,1792]{2,1,0:T(2,128)(2,1)S(1)}, u32[]{:S(2)}, u32[]{:S(2)}) async-start(bf16[64,2,1792]{2,1,0:T(2,128)(2,1)} %reshape.383), calls=%async_computation.9 | async-start | bytes 917504 | tf_op jit(solution)/shard_map/all_to_all | solution.py:18
  388.1 34.9 %all-to-all-start.2 = ((bf16[8,128,448]{1,2,0:T(8,128)(2,1)}), bf16[8,128,448]{1,2,0:T(8,128)(2,1)S(1)}, u32[]{:S(2)}, u32[]{:S(2)}) async-start(bf16[8,128,448]{1,2,0:T(8,128)(2,1)} %broadcast_in_dim.135), calls=%async_computation.2 | async-start | bytes 1835008 | tf_op jit(solution)/shard_map/all_to_all | solution.py:24
  397.0 22.8 %copy-start.10 = (bf16[64,56,64]{2,1,0:T(8,128)(2,1)}, bf16[64,56,64]{2,1,0:T(8,128)(2,1)S(1)}, u32[]{:S(2)}) copy-start(bf16[64,56,64]{2,1,0:T(8,128)(2,1)S(1)} %reshape.384) | copy-start | bytes 1376260
  397.9 21.8 %collective-permute-start.5 = (f32[64,56]{0,1:T(8,128)S(1)}, f32[64,56]{0,1:T(8,128)S(1)}, u32[]{:S(2)}, u32[]{:S(2)}) collective-permute-start(f32[64,56]{0,1:T(8,128)S(1)} %fusion.16), channel_id=1, source_target_pairs={{64,0},{128,64},{192,128},{256,192},{320,256},{384,320},{448,384},... | collective-permute-start | bytes 43016 | tf_op jit(solution)/shard_map/ppermute | solution.py:12
  421.2 12.6 %copy-start.17 = (bf16[1,64,56]{1,2,0:T(8,128)(2,1)S(1)}, bf16[1,64,56]{1,2,0:T(8,128)(2,1)}, u32[]{:S(2)}) copy-start(bf16[1,64,56]{1,2,0:T(8,128)(2,1)} %param.14) | copy-start | bytes 21508
  423.0 22.2 %all-to-all-start.10 = ((bf16[64,2,1792]{2,1,0:T(2,128)(2,1)}), bf16[64,2,1792]{2,1,0:T(2,128)(2,1)S(1)}, u32[]{:S(2)}, u32[]{:S(2)}) async-start(bf16[64,2,1792]{2,1,0:T(2,128)(2,1)} %reshape.385), calls=%async_computation.10 | async-start | bytes 917504 | tf_op jit(solution)/shard_map/all_to_all | solution.py:18
  433.9 15.2 %copy-start.5 = (bf16[64,56,64]{2,1,0:T(8,128)(2,1)S(1)}, bf16[64,56,64]{2,1,0:T(8,128)(2,1)}, u32[]{:S(2)}) copy-start(bf16[64,56,64]{2,1,0:T(8,128)(2,1)} %copy-done.4) | copy-start | bytes 1376260
  447.7 14.8 %copy-start.7 = (bf16[64,56,64]{2,1,0:T(8,128)(2,1)S(1)}, bf16[64,56,64]{2,1,0:T(8,128)(2,1)}, u32[]{:S(2)}) copy-start(bf16[64,56,64]{2,1,0:T(8,128)(2,1)} %copy-done.6) | copy-start | bytes 1376260
  447.7 5.9 %collective-permute-start.6 = (f32[64,56]{0,1:T(8,128)S(1)}, f32[64,56]{0,1:T(8,128)S(1)}, u32[]{:S(2)}, u32[]{:S(2)}) collective-permute-start(f32[64,56]{0,1:T(8,128)S(1)} %fusion.17), channel_id=1, source_target_pairs={{64,0},{128,64},{192,128},{256,192},{320,256},{384,320},{448,384},... | collective-permute-start | bytes 43016 | tf_op jit(solution)/shard_map/ppermute | solution.py:12
  455.1 22.6 %all-to-all-start.11 = ((bf16[64,2,1792]{2,1,0:T(2,128)(2,1)}), bf16[64,2,1792]{2,1,0:T(2,128)(2,1)S(1)}, u32[]{:S(2)}, u32[]{:S(2)}) async-start(bf16[64,2,1792]{2,1,0:T(2,128)(2,1)} %reshape.387), calls=%async_computation.11 | async-start | bytes 917504 | tf_op jit(solution)/shard_map/all_to_all | solution.py:18
  479.2 9.9 %copy-start.1 = (bf16[2,64,3584]{2,1,0:T(8,128)(2,1)S(1)}, bf16[2,64,3584]{2,1,0:T(8,128)(2,1)}, u32[]{:S(2)}) copy-start(bf16[2,64,3584]{2,1,0:T(8,128)(2,1)} %param.9) | copy-start | bytes 2752516
  (19 other events, 75.4 us)

commit v7 on v6

--- a/solution.py
+++ b/solution.py
@@ -16,13 +16,6 @@
     count = lax.axis_size(axis)
     copies = jnp.broadcast_to(value[None], (count,) + value.shape)
     return lax.all_to_all(copies, axis, 0, 0, tiled=True)
-
-
-def gathered_columns(value, axis):
-    count = lax.axis_size(axis)
-    copies = jnp.broadcast_to(value[None], (count,) + value.shape)
-    pieces = lax.all_to_all(copies, axis, 0, 0, tiled=True)
-    return jnp.transpose(pieces, (1, 0, 2)).reshape(value.shape[0], count * value.shape[1])
 
 
 def soft_weights(logits, valid):
@@ -111,8 +104,7 @@
         preferred_element_type=jnp.float32,
     )
     dense = dense.reshape(stripe, block_total, chunk).astype(jnp.bfloat16)
-    passage_out = gathered_columns(dense.reshape(stripe * block_total, chunk), "section")
-    passage_out = passage_out.reshape(stripe, block_total, width)
+    passage_out = lax.all_gather(dense, "section", axis=2, tiled=True)
     entry = lax.all_to_all(carry_start, "dp", split_axis=0, concat_axis=1, tiled=True)
     weight_rows = section_weights[0]
     split_rows = weight_rows.reshape(col_width, dp_count, col_width)

time: 499 us -> 503 us (level)
  the two profiles are of different devices: /device:TPU:6 before, /device:TPU:31 now
where the time goes in v7:
time: 503 us; the launch traced here: 495 us
  waiting for transfers between devices  183 us (36%)
  blocking collectives  132 us (26%)
  starting transfers between devices  82.3 us (16%)
  local copies, waits for them, and re-layouts  54.5 us (11%)
  matrix products  33.3 us (7%)
  other arithmetic  8.21 us (2%)
    all_to_all x4, blocking collectives, gathered_pieces(): return lax.all_to_all(copies, axis, 0, 0, tiled=True)  92.6 us
    all_to_all x1, waiting for transfers between devices, body(): lax.all_to_all(term_pieces, ('section', 'dp'), split_axis=0, concat_axis=...  70.4 us
    all_to_all x1, waiting for transfers between devices, body(): lax.all_to_all(outgoing, 'dp', split_axis=1, concat_axis=0, tiled=True)  60.9 us
    all_to_all x4, starting transfers between devices, gathered_pieces(): return lax.all_to_all(copies, axis, 0, 0, tiled=True)  38.4 us
    all_to_all x4, waiting for transfers between devices, gathered_pieces(): return lax.all_to_all(copies, axis, 0, 0, tiled=True)  28.8 us
    all_gather x1, blocking collectives, body(): passage_out = lax.all_gather(dense, 'section', axis=2, tiled=True)  24.5 us
    ppermute x7, waiting for transfers between devices, passed_along(): lax.ppermute(value, axis, [(source, source + steps) for source in range(i...  23.3 us
    unnamed x85, local copies, waits for them, and re-layouts  20.6 us
  transfers between devices with their start and end apart: 13, of which 12 were waited for; matrix products, arithmetic and copies ran while one was open for 7% of the time, Pallas kernels for 0%

profile of v7, /device:TPU:31, one launch (start us, length us, event | category | flops | bytes accessed | tf_op | source)
XLA Modules:
  0.0 495.0 jit_solution(15338837324130636634)
XLA Ops:
  2.7 4.3 copy.150
  7.1 14.5 %all-to-all-start = ((bf16[2,192,3584]{2,0,1:T(2,128)(2,1)}), bf16[2,192,3584]{2,0,1:T(2,128)(2,1)S(1)}, u32[]{:S(2)}, u32[]{:S(2)}) async-start(bf16[2,192,3584]{2,0,1:T(2,128)(2,1)} %copy.150), calls=%async_computation | async-start | bytes 5505024 | tf_op jit(solution)/shard_map/all_to_all | solution.py:43
  25.6 60.9 %all-to-all-done = bf16[2,192,3584]{2,0,1:T(2,128)(2,1)S(1)} async-done(((bf16[2,192,3584]{2,0,1:T(2,128)(2,1)}), bf16[2,192,3584]{2,0,1:T(2,128)(2,1)S(1)}, u32[]{:S(2)}, u32[]{:S(2)}) %all-to-all-start) | async-done | bytes 2752544 | tf_op jit(solution)/shard_map/all_to_all | solution.py:43
  89.9 5.8 %reshape.329 = bf16[128,3,3584]{2,0,1:T(8,128)(2,1)S(1)} reshape(bf16[64,2,3,3584]{3,1,0,2:T(2,128)(2,1)} %copy.151) | data formatting | bytes 5505024 | tf_op jit(solution)/shard_map/reshape.5
  102.9 5.9 %pad_maximum_fusion = bf16[512,2,3,449]{3,1,2,0:T(2,128)(2,1)} fusion(bf16[512,2,3,1]{3,1,2,0:T(2,128)(2,1)S(1)} %broadcast_in_dim.126, bf16[512,2,3,448]{3,1,2,0:T(2,128)(2,1)S(1)} %copy.156), kind=kLoop, calls=%fused_computation.5 | loop fusion | flops 5517312 | bytes 5517312 | tf_op jit(solution)/shard_map/concatenate | solution.py:91
  108.8 14.6 %all-to-all-start.1 = ((bf16[512,2,3,449]{3,1,2,0:T(2,128)(2,1)}), bf16[512,2,3,449]{3,1,2,0:T(2,128)(2,1)}, u32[]{:S(2)}, u32[]{:S(2)}) async-start(bf16[512,2,3,449]{3,1,2,0:T(2,128)(2,1)} %pad_maximum_fusion), calls=%async_computation.1 | async-start | bytes 6291456 | tf_op jit(solution)/shard_map/all_to_all | solution.py:92
  125.1 70.4 %all-to-all-done.1 = bf16[512,2,3,449]{3,1,2,0:T(2,128)(2,1)} async-done(((bf16[512,2,3,449]{3,1,2,0:T(2,128)(2,1)}), bf16[512,2,3,449]{3,1,2,0:T(2,128)(2,1)}, u32[]{:S(2)}, u32[]{:S(2)}) %all-to-all-start.1) | async-done | bytes 2758688 | tf_op jit(solution)/shard_map/all_to_all | solution.py:92
  195.5 14.6 %all_to_all.69 = f32[64,1,56]{2,1,0:T(1,128)S(1)} all-to-all(f32[64,1,56]{2,1,0:T(1,128)S(1)} %bitcast.240), channel_id=1, replica_groups=mesh['section'=8,'dp'=64] {'dp'}, dimensions={0} | all-to-all | bytes 28672 | tf_op jit(solution)/shard_map/all_to_all | solution.py:108
  211.7 6.9 %all-to-all-start.3 = ((bf16[64,2,1792]{2,1,0:T(2,128)(2,1)}), bf16[64,2,1792]{2,1,0:T(2,128)(2,1)S(1)}, u32[]{:S(2)}, u32[]{:S(2)}) async-start(bf16[64,2,1792]{2,1,0:T(2,128)(2,1)} %reshape.372), calls=%async_computation.3 | async-start | bytes 917504 | tf_op jit(solution)/shard_map/all_to_all | solution.py:18
  220.5 13.9 %all-to-all-done.3 = bf16[64,2,1792]{2,1,0:T(2,128)(2,1)S(1)} async-done(((bf16[64,2,1792]{2,1,0:T(2,128)(2,1)}), bf16[64,2,1792]{2,1,0:T(2,128)(2,1)S(1)}, u32[]{:S(2)}, u32[]{:S(2)}) %all-to-all-start.3) | async-done | bytes 458784 | tf_op jit(solution)/shard_map/all_to_all | solution.py:18
  242.3 23.2 %all_to_all.70 = bf16[64,2,1792]{2,1,0:T(2,128)(2,1)S(1)} all-to-all(bf16[64,2,1792]{2,1,0:T(2,128)(2,1)S(1)} %reshape.374), channel_id=1, replica_groups=mesh['section'=8,'dp'=64] {'dp'}, dimensions={0} | all-to-all | bytes 917504 | tf_op jit(solution)/shard_map/all_to_all | solution.py:18
  273.5 23.2 %all_to_all.71 = bf16[64,2,1792]{2,1,0:T(2,128)(2,1)S(1)} all-to-all(bf16[64,2,1792]{2,1,0:T(2,128)(2,1)S(1)} %reshape.376), channel_id=1, replica_groups=mesh['section'=8,'dp'=64] {'dp'}, dimensions={0} | all-to-all | bytes 917504 | tf_op jit(solution)/shard_map/all_to_all | solution.py:18
  300.1 3.9 collective-permute-done.2
  304.7 23.2 %all_to_all.72 = bf16[64,2,1792]{2,1,0:T(2,128)(2,1)S(1)} all-to-all(bf16[64,2,1792]{2,1,0:T(2,128)(2,1)S(1)} %reshape.378), channel_id=1, replica_groups=mesh['section'=8,'dp'=64] {'dp'}, dimensions={0} | all-to-all | bytes 917504 | tf_op jit(solution)/shard_map/all_to_all | solution.py:18
  331.2 3.9 collective-permute-done.3
  335.8 23.2 %all_to_all.73 = bf16[64,2,1792]{2,1,0:T(2,128)(2,1)S(1)} all-to-all(bf16[64,2,1792]{2,1,0:T(2,128)(2,1)S(1)} %reshape.380), channel_id=1, replica_groups=mesh['section'=8,'dp'=64] {'dp'}, dimensions={0} | all-to-all | bytes 917504 | tf_op jit(solution)/shard_map/all_to_all | solution.py:18
  362.4 3.9 collective-permute-done.4
  367.8 7.9 %all-to-all-start.8 = ((bf16[64,2,1792]{2,1,0:T(2,128)(2,1)}), bf16[64,2,1792]{2,1,0:T(2,128)(2,1)S(1)}, u32[]{:S(2)}, u32[]{:S(2)}) async-start(bf16[64,2,1792]{2,1,0:T(2,128)(2,1)} %reshape.382), calls=%async_computation.8 | async-start | bytes 917504 | tf_op jit(solution)/shard_map/all_to_all | solution.py:18
  375.7 8.7 %copy.157 = bf16[512,2,3,449]{0,3,2,1:T(8,128)(2,1)} copy(bf16[512,2,3,449]{3,1,2,0:T(2,128)(2,1)} %all-to-all-done.1) | data formatting | bytes 5517312 | tf_op jit(solution)/shard_map/optimization_barrier | solution.py:95
  384.4 6.9 %all-to-all-done.8 = bf16[64,2,1792]{2,1,0:T(2,128)(2,1)S(1)} async-done(((bf16[64,2,1792]{2,1,0:T(2,128)(2,1)}), bf16[64,2,1792]{2,1,0:T(2,128)(2,1)S(1)}, u32[]{:S(2)}, u32[]{:S(2)}) %all-to-all-start.8) | async-done | bytes 458784 | tf_op jit(solution)/shard_map/all_to_all | solution.py:18
  400.1 7.6 %all-to-all-start.9 = ((bf16[64,2,1792]{2,1,0:T(2,128)(2,1)}), bf16[64,2,1792]{2,1,0:T(2,128)(2,1)S(1)}, u32[]{:S(2)}, u32[]{:S(2)}) async-start(bf16[64,2,1792]{2,1,0:T(2,128)(2,1)} %reshape.384), calls=%async_computation.9 | async-start | bytes 917504 | tf_op jit(solution)/shard_map/all_to_all | solution.py:18
  410.5 24.5 %all_gather.3 = bf16[2,64,3584]{1,0,2:T(2,128)(2,1)S(1)} all-gather(bf16[2,64,448]{1,0,2:T(2,128)(2,1)S(1)} %copy.159), channel_id=1, replica_groups=mesh['section'=8,'dp'=64] {'section'}, dimensions={2}, use_global_device_ids=true | all-gather | bytes 1032192 | tf_op jit(solution)/shard_map/all_gather | solution.py:107
  451.4 16.1 %all-to-all-start.10 = ((bf16[64,2,1792]{2,1,0:T(2,128)(2,1)}), bf16[64,2,1792]{2,1,0:T(2,128)(2,1)S(1)}, u32[]{:S(2)}, u32[]{:S(2)}) async-start(bf16[64,2,1792]{2,1,0:T(2,128)(2,1)} %reshape.386), calls=%async_computation.10 | async-start | bytes 917504 | tf_op jit(solution)/shard_map/all_to_all | solution.py:18
  475.1 8.0 %all-to-all-done.10 = bf16[64,2,1792]{2,1,0:T(2,128)(2,1)S(1)} async-done(((bf16[64,2,1792]{2,1,0:T(2,128)(2,1)}), bf16[64,2,1792]{2,1,0:T(2,128)(2,1)S(1)}, u32[]{:S(2)}, u32[]{:S(2)}) %all-to-all-start.10) | async-done | bytes 458784 | tf_op jit(solution)/shard_map/all_to_all | solution.py:18
  (146 shorter events, 97.8 us)
Async XLA Ops:
  7.1 14.5 %copy-start.18 = (f32[128,384]{1,0:T(8,128)S(1)}, f32[128,384]{1,0:T(8,128)}, u32[]{:S(2)}) copy-start(f32[128,384]{1,0:T(8,128)} %param.12) | copy-start | bytes 589828
  7.1 16.8 %copy-start.27 = (s32[64]{0:T(128)S(1)}, s32[64]{0:T(128)}, u32[]{:S(2)}) copy-start(s32[64]{0:T(128)} %param.11) | copy-start | bytes 772
  7.1 79.4 %all-to-all-start = ((bf16[2,192,3584]{2,0,1:T(2,128)(2,1)}), bf16[2,192,3584]{2,0,1:T(2,128)(2,1)S(1)}, u32[]{:S(2)}, u32[]{:S(2)}) async-start(bf16[2,192,3584]{2,0,1:T(2,128)(2,1)} %copy.150), calls=%async_computation | async-start | bytes 5505024 | tf_op jit(solution)/shard_map/all_to_all | solution.py:43
  108.8 86.7 %all-to-all-start.1 = ((bf16[512,2,3,449]{3,1,2,0:T(2,128)(2,1)}), bf16[512,2,3,449]{3,1,2,0:T(2,128)(2,1)}, u32[]{:S(2)}, u32[]{:S(2)}) async-start(bf16[512,2,3,449]{3,1,2,0:T(2,128)(2,1)} %pad_maximum_fusion), calls=%async_computation.1 | async-start | bytes 6291456 | tf_op jit(solution)/shard_map/all_to_all | solution.py:92
  123.4 86.8 %copy-start.14 = (bf16[1,64,56]{1,2,0:T(8,128)(2,1)S(1)}, bf16[1,64,56]{1,2,0:T(8,128)(2,1)}, u32[]{:S(2)}) copy-start(bf16[1,64,56]{1,2,0:T(8,128)(2,1)} %param.15) | copy-start | bytes 21508
  125.0 93.6 %copy-start.17 = (bf16[1,56,3584]{2,1,0:T(8,128)(2,1)S(1)}, bf16[1,56,3584]{2,1,0:T(8,128)(2,1)}, u32[]{:S(2)}) copy-start(bf16[1,56,3584]{2,1,0:T(8,128)(2,1)} %param.13) | copy-start | bytes 1204228
  211.7 22.6 %all-to-all-start.3 = ((bf16[64,2,1792]{2,1,0:T(2,128)(2,1)}), bf16[64,2,1792]{2,1,0:T(2,128)(2,1)S(1)}, u32[]{:S(2)}, u32[]{:S(2)}) async-start(bf16[64,2,1792]{2,1,0:T(2,128)(2,1)} %reshape.372), calls=%async_computation.3 | async-start | bytes 917504 | tf_op jit(solution)/shard_map/all_to_all | solution.py:18
  235.8 31.2 %copy-start.20 = (f32[64,56]{0,1:T(8,128)}, f32[64,56]{0,1:T(8,128)S(1)}, u32[]{:S(2)}) copy-start(f32[64,56]{0,1:T(8,128)S(1)} %fusion.14) | copy-start | bytes 43012
  235.8 5.8 %collective-permute-start = (f32[64,56]{0,1:T(8,128)S(1)}, f32[64,56]{0,1:T(8,128)S(1)}, u32[]{:S(2)}, u32[]{:S(2)}) collective-permute-start(f32[64,56]{0,1:T(8,128)S(1)} %fusion.14), channel_id=1, source_target_pairs={{64,0},{128,64},{192,128},{256,192},{320,256},{384,320},{448,384},... | collective-permute-start | bytes 43016 | tf_op jit(solution)/shard_map/ppermute | solution.py:12
  267.0 5.8 %collective-permute-start.1 = (f32[64,56]{0,1:T(8,128)S(1)}, f32[64,56]{0,1:T(8,128)S(1)}, u32[]{:S(2)}, u32[]{:S(2)}) collective-permute-start(f32[64,56]{0,1:T(8,128)S(1)} %fusion.15), channel_id=1, source_target_pairs={{64,0},{128,64},{192,128},{256,192},{320,256},{384,320},{448,384},... | collective-permute-start | bytes 43016 | tf_op jit(solution)/shard_map/ppermute | solution.py:12
  298.1 5.8 %collective-permute-start.2 = (f32[64,56]{0,1:T(8,128)S(1)}, f32[64,56]{0,1:T(8,128)S(1)}, u32[]{:S(2)}, u32[]{:S(2)}) collective-permute-start(f32[64,56]{0,1:T(8,128)S(1)} %fusion.16), channel_id=1, source_target_pairs={{64,0},{128,64},{192,128},{256,192},{320,256},{384,320},{448,384},... | collective-permute-start | bytes 43016 | tf_op jit(solution)/shard_map/ppermute | solution.py:12
  329.3 5.8 %collective-permute-start.3 = (f32[64,56]{0,1:T(8,128)S(1)}, f32[64,56]{0,1:T(8,128)S(1)}, u32[]{:S(2)}, u32[]{:S(2)}) collective-permute-start(f32[64,56]{0,1:T(8,128)S(1)} %fusion.17), channel_id=1, source_target_pairs={{64,0},{128,64},{192,128},{256,192},{320,256},{384,320},{448,384},... | collective-permute-start | bytes 43016 | tf_op jit(solution)/shard_map/ppermute | solution.py:12
  360.5 5.8 %collective-permute-start.4 = (f32[64,56]{0,1:T(8,128)S(1)}, f32[64,56]{0,1:T(8,128)S(1)}, u32[]{:S(2)}, u32[]{:S(2)}) collective-permute-start(f32[64,56]{0,1:T(8,128)S(1)} %fusion.18), channel_id=1, source_target_pairs={{64,0},{128,64},{192,128},{256,192},{320,256},{384,320},{448,384},... | collective-permute-start | bytes 43016 | tf_op jit(solution)/shard_map/ppermute | solution.py:12
  367.8 23.5 %all-to-all-start.8 = ((bf16[64,2,1792]{2,1,0:T(2,128)(2,1)}), bf16[64,2,1792]{2,1,0:T(2,128)(2,1)S(1)}, u32[]{:S(2)}, u32[]{:S(2)}) async-start(bf16[64,2,1792]{2,1,0:T(2,128)(2,1)} %reshape.382), calls=%async_computation.8 | async-start | bytes 917504 | tf_op jit(solution)/shard_map/all_to_all | solution.py:18
  392.8 5.8 %collective-permute-start.5 = (f32[64,56]{0,1:T(8,128)S(1)}, f32[64,56]{0,1:T(8,128)S(1)}, u32[]{:S(2)}, u32[]{:S(2)}) collective-permute-start(f32[64,56]{0,1:T(8,128)S(1)} %fusion.19), channel_id=1, source_target_pairs={{64,0},{128,64},{192,128},{256,192},{320,256},{384,320},{448,384},... | collective-permute-start | bytes 43016 | tf_op jit(solution)/shard_map/ppermute | solution.py:12
  400.1 41.4 %all-to-all-start.9 = ((bf16[64,2,1792]{2,1,0:T(2,128)(2,1)}), bf16[64,2,1792]{2,1,0:T(2,128)(2,1)S(1)}, u32[]{:S(2)}, u32[]{:S(2)}) async-start(bf16[64,2,1792]{2,1,0:T(2,128)(2,1)} %reshape.384), calls=%async_computation.9 | async-start | bytes 917504 | tf_op jit(solution)/shard_map/all_to_all | solution.py:18
  410.3 28.0 %copy-start.16 = (bf16[1,64,56]{1,2,0:T(8,128)(2,1)S(1)}, bf16[1,64,56]{1,2,0:T(8,128)(2,1)}, u32[]{:S(2)}) copy-start(bf16[1,64,56]{1,2,0:T(8,128)(2,1)} %param.14) | copy-start | bytes 21508
  438.3 7.6 %copy-start.4 = (bf16[64,56,64]{2,1,0:T(8,128)(2,1)S(1)}, bf16[64,56,64]{2,1,0:T(8,128)(2,1)}, u32[]{:S(2)}) copy-start(bf16[64,56,64]{2,1,0:T(8,128)(2,1)} %copy-done.3) | copy-start | bytes 1376260
  443.9 23.6 %copy-start.6 = (bf16[64,56,64]{2,1,0:T(8,128)(2,1)S(1)}, bf16[64,56,64]{2,1,0:T(8,128)(2,1)}, u32[]{:S(2)}) copy-start(bf16[64,56,64]{2,1,0:T(8,128)(2,1)} %copy-done.5) | copy-start | bytes 1376260
  443.9 6.0 %collective-permute-start.6 = (f32[64,56]{0,1:T(8,128)S(1)}, f32[64,56]{0,1:T(8,128)S(1)}, u32[]{:S(2)}, u32[]{:S(2)}) collective-permute-start(f32[64,56]{0,1:T(8,128)S(1)} %fusion.20), channel_id=1, source_target_pairs={{64,0},{128,64},{192,128},{256,192},{320,256},{384,320},{448,384},... | collective-permute-start | bytes 43016 | tf_op jit(solution)/shard_map/ppermute | solution.py:12
  449.8 21.4 %copy-start.19 = (f32[64,56]{0,1:T(8,128)}, f32[64,56]{0,1:T(8,128)S(1)}, u32[]{:S(2)}) copy-start(f32[64,56]{0,1:T(8,128)S(1)} %collective-permute-done.6) | copy-start | bytes 43012
  451.4 18.0 %copy-start.8 = (bf16[64,56,64]{2,1,0:T(8,128)(2,1)S(1)}, bf16[64,56,64]{2,1,0:T(8,128)(2,1)}, u32[]{:S(2)}) copy-start(bf16[64,56,64]{2,1,0:T(8,128)(2,1)} %copy-done.7) | copy-start | bytes 1376260
  451.4 31.7 %all-to-all-start.10 = ((bf16[64,2,1792]{2,1,0:T(2,128)(2,1)}), bf16[64,2,1792]{2,1,0:T(2,128)(2,1)S(1)}, u32[]{:S(2)}, u32[]{:S(2)}) async-start(bf16[64,2,1792]{2,1,0:T(2,128)(2,1)} %reshape.386), calls=%async_computation.10 | async-start | bytes 917504 | tf_op jit(solution)/shard_map/all_to_all | solution.py:18
  484.6 10.2 %copy-start.1 = (bf16[2,64,3584]{2,1,0:T(8,128)(2,1)S(1)}, bf16[2,64,3584]{2,1,0:T(8,128)(2,1)}, u32[]{:S(2)}) copy-start(bf16[2,64,3584]{2,1,0:T(8,128)(2,1)} %param.9) | copy-start | bytes 2752516
  (17 other events, 69.5 us)

commit v8 on v6

--- a/solution.py
+++ b/solution.py
@@ -48,6 +48,8 @@
         "rpj,sp->rsj", passages, chooser, preferred_element_type=jnp.float32
     ).astype(passages.dtype)
     pulled_rows = lax.all_to_all(outgoing, "dp", split_axis=1, concat_axis=0, tiled=True)
+    every_slot = lax.all_gather(candidates, "section", axis=0, tiled=True)
+    pulled_rows, every_slot = lax.optimization_barrier((pulled_rows, every_slot))
     pulled_rows = pulled_rows.reshape(row_block_count, blocks_here, slot_count, width)
     own_counts = lax.dynamic_slice_in_dim(counts, dp_index * blocks_here, blocks_here)
     slot_valid = jnp.arange(slot_count, dtype=jnp.int32)[None, :] < own_counts[:, None]
@@ -90,23 +92,16 @@
         * INVERSE_TEMP
     ).astype(jnp.bfloat16)
     term_pieces = term_pieces.reshape(section_count * dp_count, stripe, requests, chunk)
-    own_slots = lax.dynamic_slice_in_dim(all_slots, dp_index * requests, requests)
-    slot_tags = jnp.broadcast_to(
-        own_slots.astype(jnp.bfloat16)[None, None, :, None],
-        (section_count * dp_count, stripe, requests, 1),
-    )
-    term_pieces = jnp.concatenate([term_pieces, slot_tags], axis=3)
     incoming_terms = lax.all_to_all(
         term_pieces, ("section", "dp"), split_axis=0, concat_axis=0, tiled=True
     )
     incoming_terms, carry_start = lax.optimization_barrier((incoming_terms, micro_cols))
-    every_slot = incoming_terms[:, 0, :, chunk].astype(jnp.int32)
     onehot = (every_slot[:, :, None] == jnp.arange(block_total, dtype=jnp.int32)).astype(
         jnp.bfloat16
     )
     dense = jnp.einsum(
         "qsfc,qfn->snc",
-        incoming_terms[:, :, :, :chunk],
+        incoming_terms,
         onehot,
         preferred_element_type=jnp.float32,
     )

time: 499 us -> 508 us (1.018)
  blocking collectives: 104 us -> 129 us
  waiting for transfers between devices: 210 us -> 189 us
  matrix products: 33.1 us -> 40.1 us
  other arithmetic: 8.21 us -> 1.44 us
  local copies, waits for them, and re-layouts: 56.2 us -> 61.4 us
    all_gather x0 -> x1, blocking collectives: none -> 24.2 us  [body(): every_slot = lax.all_gather(candidates, 'section', axis=0, tiled=True)]
    all_to_all x1, waiting for transfers between devices: 58.7 us -> 36 us  [body(): lax.all_to_all(outgoing, 'dp', split_axis=1, concat_axis=0, tiled=True)]
    unnamed x86 -> x65, local copies, waits for them, and re-layouts: 17.3 us -> 26.2 us
    all_to_all x1 -> x2, local copies, waits for them, and re-layouts: 3.4 us -> 12 us  [body(): lax.all_to_all(outgoing, 'dp', split_axis=1, concat_axis=0, tiled=True)]
    optimization_barrier x1, local copies, waits for them, and re-layouts: 8.7 us -> 0.08 us  [body(): lax.optimization_barrier((pulled_rows, every_slot))]
    all_to_all x4, waiting for transfers between devices: 32.5 us -> 40.8 us  [gathered_pieces(): return lax.all_to_all(copies, axis, 0, 0, tiled=True)]
    concatenate x1 -> x0, other arithmetic: 5.94 us -> none  [body(): term_pieces = jnp.concatenate([term_pieces, slot_tags], axis=3)]
    another operation x1 -> x0, local copies, waits for them, and re-layouts: 5.79 us -> none
  transfers between devices with their start and end apart: 14 -> 14, of which waited for: 14 -> 13; matrix products, arithmetic and copies ran while one was open for 8% -> 7% of each run, Pallas kernels for 0% -> 0%
where the time goes in v8:
time: 508 us; the launch traced here: 499 us
  waiting for transfers between devices  189 us (37%)
  blocking collectives  129 us (25%)
  starting transfers between devices  76 us (15%)
  local copies, waits for them, and re-layouts  61.4 us (12%)
  matrix products  40.1 us (8%)
    all_to_all x4, blocking collectives, gathered_pieces(): return lax.all_to_all(copies, axis, 0, 0, tiled=True)  88.8 us
    all_to_all x1, waiting for transfers between devices, body(): lax.all_to_all(term_pieces, ('section', 'dp'), split_axis=0, concat_axis=...  69.4 us
    ppermute x7, waiting for transfers between devices, passed_along(): lax.ppermute(value, axis, [(source, source + steps) for source in range(i...  43.2 us
    all_to_all x4, waiting for transfers between devices, gathered_pieces(): return lax.all_to_all(copies, axis, 0, 0, tiled=True)  40.8 us
    all_to_all x1, waiting for transfers between devices, body(): lax.all_to_all(outgoing, 'dp', split_axis=1, concat_axis=0, tiled=True)  36 us
    all_to_all x4, starting transfers between devices, gathered_pieces(): return lax.all_to_all(copies, axis, 0, 0, tiled=True)  26.8 us
    unnamed x65, local copies, waits for them, and re-layouts  26.2 us
    all_gather x1, blocking collectives, body(): every_slot = lax.all_gather(candidates, 'section', axis=0, tiled=True)  24.2 us
  transfers between devices with their start and end apart: 14, of which 13 were waited for; matrix products, arithmetic and copies ran while one was open for 7% of the time, Pallas kernels for 0%

profile of v8, /device:TPU:6, one launch (start us, length us, event | category | flops | bytes accessed | tf_op | source)
XLA Modules:
  0.0 499.2 jit_solution(16363897981642886788)
XLA Ops:
  7.1 14.3 %all-to-all-start = ((bf16[2,192,3584]{2,0,1:T(2,128)(2,1)}), bf16[2,192,3584]{2,0,1:T(2,128)(2,1)}, u32[]{:S(2)}, u32[]{:S(2)}) async-start(bf16[2,192,3584]{2,0,1:T(2,128)(2,1)} %copy.105), calls=%async_computation | async-start | bytes 5505024 | tf_op jit(solution)/shard_map/all_to_all | solution.py:50
  21.5 24.2 %all-gather = s32[8,64,3]{1,2,0:T(4,128)S(1)} all-gather(s32[1,64,3]{1,2,0:T(4,128)S(1)} %bitcast.242), channel_id=1, replica_groups=mesh['section'=8,'dp'=64] {'section'}, dimensions={0}, use_global_device_ids=true | all-gather | bytes 6912 | tf_op jit(solution)/shard_map/all_gather | solution.py:51
  48.2 36.0 %all-to-all-done = bf16[2,192,3584]{2,0,1:T(2,128)(2,1)} async-done(((bf16[2,192,3584]{2,0,1:T(2,128)(2,1)}), bf16[2,192,3584]{2,0,1:T(2,128)(2,1)}, u32[]{:S(2)}, u32[]{:S(2)}) %all-to-all-start) | async-done | bytes 2752544 | tf_op jit(solution)/shard_map/all_to_all | solution.py:50
  84.2 5.2 %copy.106 = bf16[64,2,3,3584]{3,1,0,2:T(2,128)(2,1)} copy(bf16[64,2,3,3584]{3,1,2,0:T(2,128)(2,1)} %bitcast.5) | data formatting | bytes 5505024 | tf_op jit(solution)/shard_map/all_to_all | solution.py:50
  89.4 6.8 %all_to_all.53 = bf16[128,3,3584]{2,0,1:T(8,128)(2,1)} reshape(bf16[64,2,3,3584]{3,1,0,2:T(2,128)(2,1)} %copy.106) | data formatting | bytes 5505024 | tf_op jit(solution)/shard_map/all_to_all | solution.py:50
  100.2 4.9 copy.112
  105.1 17.3 %all-to-all-start.1 = ((bf16[512,2,3,448]{3,1,2,0:T(2,128)(2,1)}), bf16[512,2,3,448]{3,1,2,0:T(2,128)(2,1)}, u32[]{:S(2)}, u32[]{:S(2)}) async-start(bf16[512,2,3,448]{3,1,2,0:T(2,128)(2,1)} %copy.112), calls=%async_computation.1 | async-start | bytes 6291456 | tf_op jit(solution)/shard_map/all_to_all | solution.py:95
  126.0 69.4 %all-to-all-done.1 = bf16[512,2,3,448]{3,1,2,0:T(2,128)(2,1)} async-done(((bf16[512,2,3,448]{3,1,2,0:T(2,128)(2,1)}), bf16[512,2,3,448]{3,1,2,0:T(2,128)(2,1)}, u32[]{:S(2)}, u32[]{:S(2)}) %all-to-all-start.1) | async-done | bytes 2752544 | tf_op jit(solution)/shard_map/all_to_all | solution.py:95
  195.4 16.3 %all_to_all.77 = f32[64,1,56]{2,1,0:T(1,128)S(1)} all-to-all(f32[64,1,56]{2,1,0:T(1,128)S(1)} %bitcast.240), channel_id=1, replica_groups=mesh['section'=8,'dp'=64] {'dp'}, dimensions={0} | all-to-all | bytes 28672 | tf_op jit(solution)/shard_map/all_to_all | solution.py:111
  213.3 6.6 %all-to-all-start.4 = ((bf16[64,2,1792]{2,1,0:T(2,128)(2,1)}), bf16[64,2,1792]{2,1,0:T(2,128)(2,1)S(1)}, u32[]{:S(2)}, u32[]{:S(2)}) async-start(bf16[64,2,1792]{2,1,0:T(2,128)(2,1)} %reshape.360), calls=%async_computation.4 | async-start | bytes 917504 | tf_op jit(solution)/shard_map/all_to_all | solution.py:18
  221.7 13.5 %all-to-all-done.4 = bf16[64,2,1792]{2,1,0:T(2,128)(2,1)S(1)} async-done(((bf16[64,2,1792]{2,1,0:T(2,128)(2,1)}), bf16[64,2,1792]{2,1,0:T(2,128)(2,1)S(1)}, u32[]{:S(2)}, u32[]{:S(2)}) %all-to-all-start.4) | async-done | bytes 458784 | tf_op jit(solution)/shard_map/all_to_all | solution.py:18
  240.1 4.5 collective-permute-done
  245.3 22.1 %all_to_all.78 = bf16[64,2,1792]{2,1,0:T(2,128)(2,1)} all-to-all(bf16[64,2,1792]{2,1,0:T(2,128)(2,1)S(1)} %reshape.362), channel_id=1, replica_groups=mesh['section'=8,'dp'=64] {'dp'}, dimensions={0} | all-to-all | bytes 917504 | tf_op jit(solution)/shard_map/all_to_all | solution.py:18
  276.9 22.5 %all_to_all.79 = bf16[64,2,1792]{2,1,0:T(2,128)(2,1)} all-to-all(bf16[64,2,1792]{2,1,0:T(2,128)(2,1)S(1)} %reshape.364), channel_id=1, replica_groups=mesh['section'=8,'dp'=64] {'dp'}, dimensions={0} | all-to-all | bytes 917504 | tf_op jit(solution)/shard_map/all_to_all | solution.py:18
  308.9 22.1 %all_to_all.80 = bf16[64,2,1792]{2,1,0:T(2,128)(2,1)} all-to-all(bf16[64,2,1792]{2,1,0:T(2,128)(2,1)S(1)} %reshape.366), channel_id=1, replica_groups=mesh['section'=8,'dp'=64] {'dp'}, dimensions={0} | all-to-all | bytes 917504 | tf_op jit(solution)/shard_map/all_to_all | solution.py:18
  340.5 22.1 %all_to_all.81 = bf16[64,2,1792]{2,1,0:T(2,128)(2,1)} all-to-all(bf16[64,2,1792]{2,1,0:T(2,128)(2,1)S(1)} %reshape.368), channel_id=1, replica_groups=mesh['section'=8,'dp'=64] {'dp'}, dimensions={0} | all-to-all | bytes 917504 | tf_op jit(solution)/shard_map/all_to_all | solution.py:18
  372.8 6.8 %all-to-all-start.9 = ((bf16[64,2,1792]{2,1,0:T(2,128)(2,1)}), bf16[64,2,1792]{2,1,0:T(2,128)(2,1)S(1)}, u32[]{:S(2)}, u32[]{:S(2)}) async-start(bf16[64,2,1792]{2,1,0:T(2,128)(2,1)} %reshape.370), calls=%async_computation.9 | async-start | bytes 917504 | tf_op jit(solution)/shard_map/all_to_all | solution.py:18
  382.3 12.7 %all-to-all-done.9 = bf16[64,2,1792]{2,1,0:T(2,128)(2,1)S(1)} async-done(((bf16[64,2,1792]{2,1,0:T(2,128)(2,1)}), bf16[64,2,1792]{2,1,0:T(2,128)(2,1)S(1)}, u32[]{:S(2)}, u32[]{:S(2)}) %all-to-all-start.9) | async-done | bytes 458784 | tf_op jit(solution)/shard_map/all_to_all | solution.py:18
  396.1 8.5 %all-to-all-start.2 = ((bf16[8,128,448]{1,2,0:T(8,128)(2,1)}), bf16[8,128,448]{1,2,0:T(8,128)(2,1)S(1)}, u32[]{:S(2)}, u32[]{:S(2)}) async-start(bf16[8,128,448]{1,2,0:T(8,128)(2,1)} %broadcast_in_dim.128), calls=%async_computation.2 | async-start | bytes 1835008 | tf_op jit(solution)/shard_map/all_to_all | solution.py:24
  409.5 18.4 %collective-permute-done.5 = f32[64,56]{0,1:T(8,128)S(1)} collective-permute-done((f32[64,56]{0,1:T(8,128)S(1)}, f32[64,56]{0,1:T(8,128)S(1)}, u32[]{:S(2)}, u32[]{:S(2)}) %collective-permute-start.5) | collective-permute-done | bytes 14368 | tf_op jit(solution)/shard_map/ppermute | solution.py:12
  431.8 6.1 %all-to-all-start.10 = ((bf16[64,2,1792]{2,1,0:T(2,128)(2,1)}), bf16[64,2,1792]{2,1,0:T(2,128)(2,1)S(1)}, u32[]{:S(2)}, u32[]{:S(2)}) async-start(bf16[64,2,1792]{2,1,0:T(2,128)(2,1)} %reshape.372), calls=%async_computation.10 | async-start | bytes 917504 | tf_op jit(solution)/shard_map/all_to_all | solution.py:18
  445.2 8.2 %all-to-all-done.10 = bf16[64,2,1792]{2,1,0:T(2,128)(2,1)S(1)} async-done(((bf16[64,2,1792]{2,1,0:T(2,128)(2,1)}), bf16[64,2,1792]{2,1,0:T(2,128)(2,1)S(1)}, u32[]{:S(2)}, u32[]{:S(2)}) %all-to-all-start.10) | async-done | bytes 458784 | tf_op jit(solution)/shard_map/all_to_all | solution.py:18
  464.2 7.3 %all-to-all-start.11 = ((bf16[64,2,1792]{2,1,0:T(2,128)(2,1)}), bf16[64,2,1792]{2,1,0:T(2,128)(2,1)S(1)}, u32[]{:S(2)}, u32[]{:S(2)}) async-start(bf16[64,2,1792]{2,1,0:T(2,128)(2,1)} %reshape.374), calls=%async_computation.11 | async-start | bytes 917504 | tf_op jit(solution)/shard_map/all_to_all | solution.py:18
  480.4 6.4 %all-to-all-done.11 = bf16[64,2,1792]{2,1,0:T(2,128)(2,1)S(1)} async-done(((bf16[64,2,1792]{2,1,0:T(2,128)(2,1)}), bf16[64,2,1792]{2,1,0:T(2,128)(2,1)S(1)}, u32[]{:S(2)}, u32[]{:S(2)}) %all-to-all-start.11) | async-done | bytes 458784 | tf_op jit(solution)/shard_map/all_to_all | solution.py:18
  (128 shorter events, 115.4 us)
Async XLA Ops:
  7.1 14.4 %copy-start.17 = (s32[64,3]{0,1:T(4,128)S(1)}, s32[64,3]{0,1:T(4,128)}, u32[]{:S(2)}) copy-start(s32[64,3]{0,1:T(4,128)} %param.10) | copy-start | bytes 2308
  7.1 38.7 %copy-start.14 = (f32[128,384]{1,0:T(8,128)S(1)}, f32[128,384]{1,0:T(8,128)}, u32[]{:S(2)}) copy-start(f32[128,384]{1,0:T(8,128)} %param.12) | copy-start | bytes 589828
  7.1 38.8 %copy-start.1 = (bf16[128,3584]{1,0:T(8,128)(2,1)S(1)}, bf16[128,3584]{1,0:T(8,128)(2,1)}, u32[]{:S(2)}) copy-start(bf16[128,3584]{1,0:T(8,128)(2,1)} %param.8) | copy-start | bytes 2752516
  7.1 39.4 %copy-start.18 = (s32[64]{0:T(128)S(1)}, s32[64]{0:T(128)}, u32[]{:S(2)}) copy-start(s32[64]{0:T(128)} %param.11) | copy-start | bytes 772
  7.1 77.1 %all-to-all-start = ((bf16[2,192,3584]{2,0,1:T(2,128)(2,1)}), bf16[2,192,3584]{2,0,1:T(2,128)(2,1)}, u32[]{:S(2)}, u32[]{:S(2)}) async-start(bf16[2,192,3584]{2,0,1:T(2,128)(2,1)} %copy.105), calls=%async_computation | async-start | bytes 5505024 | tf_op jit(solution)/shard_map/all_to_all | solution.py:50
  105.1 90.3 %all-to-all-start.1 = ((bf16[512,2,3,448]{3,1,2,0:T(2,128)(2,1)}), bf16[512,2,3,448]{3,1,2,0:T(2,128)(2,1)}, u32[]{:S(2)}, u32[]{:S(2)}) async-start(bf16[512,2,3,448]{3,1,2,0:T(2,128)(2,1)} %copy.112), calls=%async_computation.1 | async-start | bytes 6291456 | tf_op jit(solution)/shard_map/all_to_all | solution.py:95
  122.5 89.3 %copy-start.11 = (bf16[1,64,56]{1,2,0:T(8,128)(2,1)S(1)}, bf16[1,64,56]{1,2,0:T(8,128)(2,1)}, u32[]{:S(2)}) copy-start(bf16[1,64,56]{1,2,0:T(8,128)(2,1)} %param.15) | copy-start | bytes 21508
  125.8 94.0 %copy-start.13 = (bf16[1,56,3584]{2,1,0:T(8,128)(2,1)S(1)}, bf16[1,56,3584]{2,1,0:T(8,128)(2,1)}, u32[]{:S(2)}) copy-start(bf16[1,56,3584]{2,1,0:T(8,128)(2,1)} %param.13) | copy-start | bytes 1204228
  213.3 22.0 %all-to-all-start.4 = ((bf16[64,2,1792]{2,1,0:T(2,128)(2,1)}), bf16[64,2,1792]{2,1,0:T(2,128)(2,1)S(1)}, u32[]{:S(2)}, u32[]{:S(2)}) async-start(bf16[64,2,1792]{2,1,0:T(2,128)(2,1)} %reshape.360), calls=%async_computation.4 | async-start | bytes 917504 | tf_op jit(solution)/shard_map/all_to_all | solution.py:18
  238.8 5.8 %collective-permute-start = (f32[64,56]{0,1:T(8,128)S(1)}, f32[64,56]{0,1:T(8,128)S(1)}, u32[]{:S(2)}, u32[]{:S(2)}) collective-permute-start(f32[64,56]{0,1:T(8,128)S(1)} %fusion.11), channel_id=1, source_target_pairs={{64,0},{128,64},{192,128},{256,192},{320,256},{384,320},{448,384},... | collective-permute-start | bytes 43016 | tf_op jit(solution)/shard_map/ppermute | solution.py:12
  270.4 5.8 %collective-permute-start.1 = (f32[64,56]{0,1:T(8,128)S(1)}, f32[64,56]{0,1:T(8,128)S(1)}, u32[]{:S(2)}, u32[]{:S(2)}) collective-permute-start(f32[64,56]{0,1:T(8,128)S(1)} %fusion.12), channel_id=1, source_target_pairs={{64,0},{128,64},{192,128},{256,192},{320,256},{384,320},{448,384},... | collective-permute-start | bytes 43016 | tf_op jit(solution)/shard_map/ppermute | solution.py:12
  302.4 5.8 %collective-permute-start.2 = (f32[64,56]{0,1:T(8,128)S(1)}, f32[64,56]{0,1:T(8,128)S(1)}, u32[]{:S(2)}, u32[]{:S(2)}) collective-permute-start(f32[64,56]{0,1:T(8,128)S(1)} %fusion.13), channel_id=1, source_target_pairs={{64,0},{128,64},{192,128},{256,192},{320,256},{384,320},{448,384},... | collective-permute-start | bytes 43016 | tf_op jit(solution)/shard_map/ppermute | solution.py:12
  334.0 5.8 %collective-permute-start.3 = (f32[64,56]{0,1:T(8,128)S(1)}, f32[64,56]{0,1:T(8,128)S(1)}, u32[]{:S(2)}, u32[]{:S(2)}) collective-permute-start(f32[64,56]{0,1:T(8,128)S(1)} %fusion.14), channel_id=1, source_target_pairs={{64,0},{128,64},{192,128},{256,192},{320,256},{384,320},{448,384},... | collective-permute-start | bytes 43016 | tf_op jit(solution)/shard_map/ppermute | solution.py:12
  365.6 5.8 %collective-permute-start.4 = (f32[64,56]{0,1:T(8,128)S(1)}, f32[64,56]{0,1:T(8,128)S(1)}, u32[]{:S(2)}, u32[]{:S(2)}) collective-permute-start(f32[64,56]{0,1:T(8,128)S(1)} %fusion.15), channel_id=1, source_target_pairs={{64,0},{128,64},{192,128},{256,192},{320,256},{384,320},{448,384},... | collective-permute-start | bytes 43016 | tf_op jit(solution)/shard_map/ppermute | solution.py:12
  372.8 22.2 %all-to-all-start.9 = ((bf16[64,2,1792]{2,1,0:T(2,128)(2,1)}), bf16[64,2,1792]{2,1,0:T(2,128)(2,1)S(1)}, u32[]{:S(2)}, u32[]{:S(2)}) async-start(bf16[64,2,1792]{2,1,0:T(2,128)(2,1)} %reshape.370), calls=%async_computation.9 | async-start | bytes 917504 | tf_op jit(solution)/shard_map/all_to_all | solution.py:18
  396.1 35.7 %all-to-all-start.2 = ((bf16[8,128,448]{1,2,0:T(8,128)(2,1)}), bf16[8,128,448]{1,2,0:T(8,128)(2,1)S(1)}, u32[]{:S(2)}, u32[]{:S(2)}) async-start(bf16[8,128,448]{1,2,0:T(8,128)(2,1)} %broadcast_in_dim.128), calls=%async_computation.2 | async-start | bytes 1835008 | tf_op jit(solution)/shard_map/all_to_all | solution.py:24
  408.2 19.7 %collective-permute-start.5 = (f32[64,56]{0,1:T(8,128)S(1)}, f32[64,56]{0,1:T(8,128)S(1)}, u32[]{:S(2)}, u32[]{:S(2)}) collective-permute-start(f32[64,56]{0,1:T(8,128)S(1)} %fusion.16), channel_id=1, source_target_pairs={{64,0},{128,64},{192,128},{256,192},{320,256},{384,320},{448,384},... | collective-permute-start | bytes 43016 | tf_op jit(solution)/shard_map/ppermute | solution.py:12
  431.8 10.2 %copy-start.12 = (bf16[1,64,56]{1,2,0:T(8,128)(2,1)S(1)}, bf16[1,64,56]{1,2,0:T(8,128)(2,1)}, u32[]{:S(2)}) copy-start(bf16[1,64,56]{1,2,0:T(8,128)(2,1)} %param.14) | copy-start | bytes 21508
  431.8 21.6 %all-to-all-start.10 = ((bf16[64,2,1792]{2,1,0:T(2,128)(2,1)}), bf16[64,2,1792]{2,1,0:T(2,128)(2,1)S(1)}, u32[]{:S(2)}, u32[]{:S(2)}) async-start(bf16[64,2,1792]{2,1,0:T(2,128)(2,1)} %reshape.372), calls=%async_computation.10 | async-start | bytes 917504 | tf_op jit(solution)/shard_map/all_to_all | solution.py:18
  442.0 12.9 %copy-start.16 = (f32[64,56]{0,1:T(8,128)S(1)}, f32[64,56]{0,1:T(8,128)}, u32[]{:S(2)}) copy-start(f32[64,56]{0,1:T(8,128)} %copy-done.15) | copy-start | bytes 43012
  442.0 16.3 %copy-start.5 = (bf16[64,56,64]{2,1,0:T(8,128)(2,1)S(1)}, bf16[64,56,64]{2,1,0:T(8,128)(2,1)}, u32[]{:S(2)}) copy-start(bf16[64,56,64]{2,1,0:T(8,128)(2,1)} %copy-done.4) | copy-start | bytes 1376260
  456.9 5.8 %collective-permute-start.6 = (f32[64,56]{0,1:T(8,128)S(1)}, f32[64,56]{0,1:T(8,128)S(1)}, u32[]{:S(2)}, u32[]{:S(2)}) collective-permute-start(f32[64,56]{0,1:T(8,128)S(1)} %fusion.17), channel_id=1, source_target_pairs={{64,0},{128,64},{192,128},{256,192},{320,256},{384,320},{448,384},... | collective-permute-start | bytes 43016 | tf_op jit(solution)/shard_map/ppermute | solution.py:12
  464.2 10.5 %copy-start.8 = (bf16[64,56,64]{2,1,0:T(8,128)(2,1)S(1)}, bf16[64,56,64]{2,1,0:T(8,128)(2,1)}, u32[]{:S(2)}) copy-start(bf16[64,56,64]{2,1,0:T(8,128)(2,1)} %copy-done.7) | copy-start | bytes 1376260
  464.2 22.5 %all-to-all-start.11 = ((bf16[64,2,1792]{2,1,0:T(2,128)(2,1)}), bf16[64,2,1792]{2,1,0:T(2,128)(2,1)S(1)}, u32[]{:S(2)}, u32[]{:S(2)}) async-start(bf16[64,2,1792]{2,1,0:T(2,128)(2,1)} %reshape.374), calls=%async_computation.11 | async-start | bytes 917504 | tf_op jit(solution)/shard_map/all_to_all | solution.py:18
  (9 other events, 56.3 us)
